TPU v7x, 512 devices: a whole 4x4x16 slice. The times are simulated.
512 devices in a mesh: ctx: 64 (over y, z), kvh: 8 (over x, core).
Axes of the slice: x: 4, y: 4, z: 16, core: 2. Of those that a mesh axis runs over, the one named last changes fastest.
Arguments:
- queries: bfloat16 [16384, 8192], P('ctx', 'kvh'), may hold values from -256 to 256
- keys: bfloat16 [16384, 1024], P('ctx', 'kvh'), may hold values from -4 to 4
- values: bfloat16 [16384, 1024], P('ctx', 'kvh'), may hold values from -6 to 6
- selection: int32 [8, 256, 16], P('kvh', 'ctx'), may hold values from -1 to 250, as said below
Outputs:
- attention_out: bfloat16 [16384, 8192], P(('ctx', 'kvh'))
Inputs may be any that keep to these rules, and one draw needn't show every extreme that they name: `selection`: entries -1 stand after the named tiles; the tiles of one list are distinct and each is at most b - 256 / 64 - 1 for block b. The query blocks held by one index of ctx (blocks c * 4 to (c + 1) * 4 - 1) name, together, at most 2 distinct tiles of any one other such group of blocks, and only tiles of earlier groups; some group reaches 2 in every draw.
All inputs are finite; a program needn't handle non-finite values.
Results may differ from a plain program's by a relative error of at most 0.008.
Values may be sent and summed in bfloat16 or wider, within the bound.
No kernel may reach another device: no remote copies, remote signals or barrier semaphores. Data moves between devices by JAX's collectives and lax.ppermute only.
A program may use at most 64 MiB of HBM per device.

v0:
```python
import jax
import jax.numpy as jnp
from jax import lax
from jax.sharding import PartitionSpec as P

TILE = 64
SEL = 16
WINDOW = 256


masked_score = -1e30


def passed_along(value, axis, steps):
    count = lax.axis_size(axis)
    first, last = (max(0, -steps), min(count, count - steps))
    return lax.ppermute(value, axis, [(source, source + steps) for source in range(first, last)])


def block_attention_step(
    query_rows, window_keys, window_values, window_ok, chosen_keys, chosen_values, chosen_ok, scale
):
    win_scores = (
        jnp.einsum("rhd,jd->hrj", query_rows, window_keys, preferred_element_type=jnp.float32)
        * scale
    )
    sel_scores = (
        jnp.einsum("rhd,jd->hrj", query_rows, chosen_keys, preferred_element_type=jnp.float32)
        * scale
    )
    win_scores = jnp.where(window_ok[None, :, :], win_scores, masked_score)
    sel_scores = jnp.where(chosen_ok[None, None, :], sel_scores, masked_score)
    peak = jnp.maximum(jnp.max(win_scores, axis=-1), jnp.max(sel_scores, axis=-1))
    win_weights = jnp.exp(win_scores - peak[:, :, None])
    sel_weights = jnp.exp(sel_scores - peak[:, :, None])
    total = jnp.sum(win_weights, axis=-1) + jnp.sum(sel_weights, axis=-1)
    numerator = jnp.einsum(
        "hrj,jd->rhd",
        win_weights.astype(jnp.bfloat16),
        window_values,
        preferred_element_type=jnp.float32,
    )
    numerator = numerator + jnp.einsum(
        "hrj,jd->rhd",
        sel_weights.astype(jnp.bfloat16),
        chosen_values,
        preferred_element_type=jnp.float32,
    )
    result = numerator / jnp.transpose(total)[:, :, None]
    return result.astype(jnp.bfloat16).reshape(query_rows.shape[0], -1)


def per_device(queries, keys, values, selection):
    tok_rows = queries.shape[0]
    head_size = keys.shape[1]
    per_dev = tok_rows // TILE
    here = lax.axis_index("ctx")
    scale = 1.0 / head_size**0.5
    tile_width = TILE * head_size
    flat_list = selection[0].reshape(-1)
    listed = flat_list >= 0
    safe_list = jnp.maximum(flat_list, 0)
    earlier_keys, earlier_values = passed_along((keys, values), "ctx", 1)
    window_keys = jnp.concatenate([earlier_keys, keys], axis=0)
    window_values = jnp.concatenate([earlier_values, values], axis=0)
    piece_keys = lax.all_gather(keys, "ctx", axis=0, tiled=True)
    piece_values = lax.all_gather(values, "ctx", axis=0, tiled=True)
    count = piece_keys.shape[0] // TILE
    piece_tiles = jnp.concatenate(
        [piece_keys.reshape(count, tile_width), piece_values.reshape(count, tile_width)], axis=1
    )
    picker = (safe_list[:, None] == jnp.arange(count, dtype=jnp.int32)[None, :]).astype(
        jnp.bfloat16
    )
    chosen = jnp.dot(picker, piece_tiles, preferred_element_type=jnp.float32).astype(jnp.bfloat16)
    chosen_keys = chosen[:, :tile_width].reshape(per_dev, SEL * TILE, head_size)
    chosen_values = chosen[:, tile_width:].reshape(per_dev, SEL * TILE, head_size)
    chosen_ok = jnp.repeat(listed.reshape(per_dev, SEL), TILE, axis=1)
    key_pos = here * tok_rows - tok_rows + jnp.arange(2 * tok_rows, dtype=jnp.int32)
    block_queries = queries.reshape(per_dev, TILE, -1, head_size)

    def one_block(inner):
        block_index, block_rows, block_keys, block_values, block_ok = inner
        query_pos = here * tok_rows + block_index * TILE + jnp.arange(TILE, dtype=jnp.int32)
        window_ok = (
            (key_pos[None, :] <= query_pos[:, None])
            & (key_pos[None, :] > query_pos[:, None] - WINDOW)
            & (key_pos[None, :] >= 0)
        )
        return block_attention_step(
            block_rows,
            window_keys,
            window_values,
            window_ok,
            block_keys,
            block_values,
            block_ok,
            scale,
        )

    attended = lax.map(
        one_block,
        (
            jnp.arange(per_dev, dtype=jnp.int32),
            block_queries,
            chosen_keys,
            chosen_values,
            chosen_ok,
        ),
    )
    attended = attended.reshape(tok_rows, -1)
    return lax.all_to_all(attended, "kvh", split_axis=0, concat_axis=1, tiled=True)


def solution(mesh):
    return jax.shard_map(
        per_device,
        mesh=mesh,
        in_specs=(P("ctx", "kvh"), P("ctx", "kvh"), P("ctx", "kvh"), P("kvh", "ctx", None)),
        out_specs=P(("ctx", "kvh"), None),
        check_vma=False,
    )
```

profile of v0, /device:TPU:1, one launch (start us, length us, event | category | flops | bytes accessed | tf_op | source)
XLA Modules:
  0.0 379.2 jit_solution(10833743811720009542)
XLA Ops:
  6.5 0.7 all-gather.3.cloned.1.call-update
  7.3 0.7 all-gather.5.cloned.1.call-update
  8.0 4.4 %collective-permute-start = (bf16[256,128]{1,0:T(8,128)(2,1)}, bf16[256,128]{1,0:T(8,128)(2,1)S(1)}, u32[]{:S(2)}, u32[]{:S(2)}) collective-permute-start(bf16[256,128]{1,0:T(8,128)(2,1)} %param.7), channel_id=1, source_target_pairs={{0,8},{8,16},{16,24},{24,32},{32,40},{40,48},{48,56},{56,64},{64,7... | collective-permute-start | bytes 196616 | tf_op jit(solution)/shard_map/ppermute | solution.py:17
  12.4 3.5 collective-permute-start.1
  15.9 0.7 broadcast_maximum_fusion
  16.6 0.7 compare_bitcast_fusion
  17.4 2.0 copy.42
  19.6 0.9 pad_maximum_fusion
  20.4 0.9 pad_maximum_fusion.1
  21.3 132.8 %all-gather.3.cloned.1.call-done = bf16[16384,128]{1,0:T(8,128)(2,1)} async-done(((bf16[256,128]{1,0:T(8,128)(2,1)}), bf16[16384,128]{1,0:T(8,128)(2,1)}) %all-gather.3.cloned.1.call-update) | async-done | bytes 4194320 | tf_op jit(solution)/shard_map/all_gather | solution.py:66
  154.1 7.3 %reshape.136 = bf16[256,8192]{1,0:T(8,128)(2,1)} reshape(bf16[16384,128]{1,0:T(8,128)(2,1)} %all-gather.3.cloned.1.call-done) | data formatting | bytes 8388608 | tf_op jit(solution)/shard_map/reshape | solution.py:70
  161.5 136.8 %all-gather.5.cloned.1.call-done = bf16[16384,128]{1,0:T(8,128)(2,1)} async-done(((bf16[256,128]{1,0:T(8,128)(2,1)}), bf16[16384,128]{1,0:T(8,128)(2,1)}) %all-gather.5.cloned.1.call-update) | async-done | bytes 4194320 | tf_op jit(solution)/shard_map/all_gather | solution.py:67
  298.3 7.3 %reshape.137 = bf16[256,8192]{1,0:T(8,128)(2,1)} reshape(bf16[16384,128]{1,0:T(8,128)(2,1)} %all-gather.5.cloned.1.call-done) | data formatting | bytes 8388608 | tf_op jit(solution)/shard_map/reshape | solution.py:70
  305.6 5.1 %convolution_convert_fusion = bf16[64,16384]{1,0:T(8,128)(2,1)S(1)} fusion(bf16[256,8192]{1,0:T(8,128)(2,1)} %reshape.137, bf16[256,8192]{1,0:T(8,128)(2,1)} %reshape.136, s32[64]{0:T(128)S(1)} %max.21), kind=kOutput, calls=%fused_computation.43 | convolution fusion | flops 554713088 | bytes 10486016 | tf_op jit(solution)/shard_map/dot_general | solution.py:75
  310.9 1.3 reshape.138
  312.2 1.3 reshape.139
  313.5 35.6 %while.13 = (s32[]{:T(128)}, bf16[4,64,1024]{2,1,0:T(8,128)(2,1)}, s32[4]{0:T(128)S(1)}, s32[]{:T(128)}, bf16[4,64,8,128]{3,2,1,0:T(8,128)(2,1)}, /*index=5*/bf1...) while((s32[]{:T(128)}, bf16[4,64,1024]{2,1,0:T(8,128)(2,1)}, ...), condition=%wide.region_5.6_spmd.clone, body=%wide.region_0.5_spmd.clone.sunk | while | flops 410321536 | bytes 14410449 | solution.py:101
  313.5 0.6 dynamic_slice.60
  314.9 0.9 dynamic-slice_bitcast_fusion.2
  316.3 1.5 bitcast_reduce_fusion.2
  317.8 0.5 fusion.53
  318.6 1.0 fusion.52
  319.6 1.6 convolution_bitcast_fusion.3
  321.7 0.7 constant_dynamic-update-slice_fusion.2
  322.4 0.6 dynamic_slice.60
  323.8 0.9 dynamic-slice_bitcast_fusion.2
  325.2 1.5 bitcast_reduce_fusion.2
  326.7 0.5 fusion.53
  327.5 1.0 fusion.52
  328.6 1.6 convolution_bitcast_fusion.3
  330.6 0.7 constant_dynamic-update-slice_fusion.2
  331.3 0.6 dynamic_slice.60
  332.7 0.9 dynamic-slice_bitcast_fusion.2
  334.2 1.5 bitcast_reduce_fusion.2
  335.6 0.5 fusion.53
  336.4 1.0 fusion.52
  337.5 1.6 convolution_bitcast_fusion.3
  339.6 0.7 constant_dynamic-update-slice_fusion.2
  340.2 0.6 dynamic_slice.60
  341.6 0.9 dynamic-slice_bitcast_fusion.2
  342.5 0.4 fusion.51
  343.1 1.5 bitcast_reduce_fusion.2
  344.6 0.5 fusion.53
  345.3 1.0 fusion.52
  346.4 1.6 convolution_bitcast_fusion.3
  348.5 0.7 constant_dynamic-update-slice_fusion.2
  349.1 22.4 %all_to_all.19 = bf16[8,32,1024]{2,1,0:T(8,128)(2,1)S(1)} all-to-all(bf16[8,32,1024]{2,1,0:T(8,128)(2,1)} %bitcast.83), channel_id=1, replica_groups=mesh['ctx'=64,'kvh'=8] {'kvh'}, dimensions={0} | all-to-all | bytes 1048576 | tf_op jit(solution)/shard_map/all_to_all | solution.py:112
  371.5 0.8 copy.41
  (77 shorter events, 5.5 us)
Async XLA Ops:
  6.5 147.6 %all-gather.3.cloned.1.call-start = ((), (), s32[]{:S(2)}) async-start(), calls=%async_computation.1 | async-start | bytes 4259840 | tf_op jit(solution)/shard_map/all_gather | solution.py:66
  7.3 291.0 %all-gather.5.cloned.1.call-start = ((), (), s32[]{:S(2)}) async-start(), calls=%async_computation.2 | async-start | bytes 4259840 | tf_op jit(solution)/shard_map/all_gather | solution.py:67
  8.0 11.5 %collective-permute-start = (bf16[256,128]{1,0:T(8,128)(2,1)}, bf16[256,128]{1,0:T(8,128)(2,1)S(1)}, u32[]{:S(2)}, u32[]{:S(2)}) collective-permute-start(bf16[256,128]{1,0:T(8,128)(2,1)} %param.7), channel_id=1, source_target_pairs={{0,8},{8,16},{16,24},{24,32},{32,40},{40,48},{48,56},{56,64},{64,7... | collective-permute-start | bytes 196616 | tf_op jit(solution)/shard_map/ppermute | solution.py:17
  12.4 8.0 %collective-permute-start.1 = (bf16[256,128]{1,0:T(8,128)(2,1)}, bf16[256,128]{1,0:T(8,128)(2,1)S(1)}, u32[]{:S(2)}, u32[]{:S(2)}) collective-permute-start(bf16[256,128]{1,0:T(8,128)(2,1)} %param.8), channel_id=1, source_target_pairs={{0,8},{8,16},{16,24},{24,32},{32,40},{40,48},{48,56},{56,64},{64,7... | collective-permute-start | bytes 196616 | tf_op jit(solution)/shard_map/ppermute | solution.py:17
  319.6 1.7 copy-start
  328.5 1.7 copy-start
  337.4 1.7 copy-start
  346.3 1.7 copy-start
Sparse Core Ops, SparseCore 0:
  10.3 143.7 all-gather.2
  157.1 141.1 all-gather.4
where the time goes:
time: 380 us; the launch traced here: 379 us
  waiting for transfers between devices  271 us (71%)
  local copies, waits for them, and re-layouts  31.2 us (8%)
  blocking collectives  22.4 us (6%)
  matrix products  20.4 us (5%)
  between operations  13.5 us (4%)
  other arithmetic  9.84 us (3%)
  starting transfers between devices  7.96 us (2%)
    all_gather x1, waiting for transfers between devices, per_device(): piece_values = lax.all_gather(values, 'ctx', axis=0, tiled=True)  137 us
    all_gather x1, waiting for transfers between devices, per_device(): piece_keys = lax.all_gather(keys, 'ctx', axis=0, tiled=True)  133 us
    all_to_all x1, blocking collectives, per_device(): lax.all_to_all(attended, 'kvh', split_axis=0, concat_axis=1, tiled=True)  22.4 us
    ppermute x2, starting transfers between devices, passed_along(): lax.ppermute(value, axis, [(source, source + steps) for source in range(f...  7.92 us
  transfers between devices with their start and end apart: 4, of which 2 were waited for; matrix products, arithmetic and copies ran while one was open for 3% of the time, Pallas kernels for 0%

commit v1 on v0

v1 whole, which is shorter than its diff:
```python
import jax
import jax.numpy as jnp
from jax import lax
from jax.sharding import Mesh
from jax.sharding import PartitionSpec as P

TILE = 64
SEL = 16
WINDOW = 256

masked_score = -1e30


def per_device(queries, keys, values, selection):
    tok_rows, head_size = keys.shape
    per_dev = tok_rows // TILE
    n_y = lax.axis_size("cy")
    n_z = lax.axis_size("cz")
    here = lax.axis_index("cy") * n_z + lax.axis_index("cz")
    scale = 1.0 / head_size**0.5
    heads = queries.shape[1] // head_size

    both = jnp.concatenate([keys, values], axis=0)
    gathered = lax.all_gather(both, "cy", axis=0, tiled=False)
    gathered = lax.all_gather(gathered, "cz", axis=0, tiled=False)
    tiles = gathered.reshape(n_z * n_y * 2 * per_dev, TILE, head_size)

    def tile_row(tile_id, kv):
        owner = tile_id // per_dev
        return (((owner % n_z) * n_y + owner // n_z) * 2 + kv) * per_dev + tile_id % per_dev

    flat_list = selection[0].reshape(-1)
    listed = flat_list >= 0
    safe_list = jnp.maximum(flat_list, 0)
    chosen_keys = jnp.take(tiles, tile_row(safe_list, 0), axis=0).reshape(per_dev, SEL * TILE, head_size)
    chosen_values = jnp.take(tiles, tile_row(safe_list, 1), axis=0).reshape(per_dev, SEL * TILE, head_size)

    prev = jnp.maximum(here - 1, 0)
    prev_rows = lax.dynamic_slice_in_dim(
        tiles, tile_row(prev * per_dev, 0), per_dev, axis=0
    ).reshape(tok_rows, head_size)
    prev_vals = lax.dynamic_slice_in_dim(
        tiles, tile_row(prev * per_dev, 1), per_dev, axis=0
    ).reshape(tok_rows, head_size)
    win_keys_all = jnp.concatenate([prev_rows, keys], axis=0)
    win_vals_all = jnp.concatenate([prev_vals, values], axis=0)
    span = WINDOW + TILE
    win_keys = jnp.stack(
        [win_keys_all[tok_rows - WINDOW + b * TILE : tok_rows - WINDOW + b * TILE + span] for b in range(per_dev)]
    )
    win_vals = jnp.stack(
        [win_vals_all[tok_rows - WINDOW + b * TILE : tok_rows - WINDOW + b * TILE + span] for b in range(per_dev)]
    )

    all_keys = jnp.concatenate([win_keys, chosen_keys], axis=1)
    all_vals = jnp.concatenate([win_vals, chosen_values], axis=1)

    block_index = jnp.arange(per_dev, dtype=jnp.int32)
    query_pos = here * tok_rows + block_index[:, None] * TILE + jnp.arange(TILE, dtype=jnp.int32)[None, :]
    key_pos = here * tok_rows + block_index[:, None] * TILE - WINDOW + jnp.arange(span, dtype=jnp.int32)[None, :]
    window_ok = (
        (key_pos[:, None, :] <= query_pos[:, :, None])
        & (key_pos[:, None, :] > query_pos[:, :, None] - WINDOW)
        & (key_pos[:, None, :] >= 0)
    )
    chosen_ok = jnp.repeat(listed.reshape(per_dev, SEL), TILE, axis=1)
    ok = jnp.concatenate(
        [window_ok, jnp.broadcast_to(chosen_ok[:, None, :], (per_dev, TILE, SEL * TILE))], axis=2
    )

    block_queries = queries.reshape(per_dev, TILE, heads, head_size)
    scores = (
        jnp.einsum("brhd,bjd->bhrj", block_queries, all_keys, preferred_element_type=jnp.float32) * scale
    )
    scores = jnp.where(ok[:, None, :, :], scores, masked_score)
    peak = jnp.max(scores, axis=-1, keepdims=True)
    weights = jnp.exp(scores - peak)
    total = jnp.sum(weights, axis=-1)
    numerator = jnp.einsum(
        "bhrj,bjd->brhd", weights.astype(jnp.bfloat16), all_vals, preferred_element_type=jnp.float32
    )
    result = numerator / jnp.transpose(total, (0, 2, 1))[:, :, :, None]
    attended = result.astype(jnp.bfloat16).reshape(tok_rows, heads * head_size)
    return lax.all_to_all(attended, "kvh", split_axis=0, concat_axis=1, tiled=True)


def solution(mesh):
    devices = mesh.devices
    ctx = devices.shape[0]
    z = len({tuple(d.coords)[2] for d in devices[:, 0]})
    z = z if ctx % z == 0 else ctx
    grid = Mesh(devices.reshape(ctx // z, z, devices.shape[1]), ("cy", "cz", "kvh"))
    row = P(("cy", "cz"), "kvh")
    return jax.shard_map(
        per_device,
        mesh=grid,
        in_specs=(row, row, row, P("kvh", ("cy", "cz"), None)),
        out_specs=P(("cy", "cz", "kvh"), None),
        check_vma=False,
    )
```

time: 380 us -> 178 us (0.47)
  waiting for transfers between devices: 271 us -> 107 us
  local copies, waits for them, and re-layouts: 31.2 us -> 12.3 us
  matrix products: 20.4 us -> 7.21 us
  starting transfers between devices: 7.96 us -> 0.01 us
  blocking collectives: 22.4 us -> 26.6 us
    all_gather x2 -> x1, waiting for transfers between devices: 270 us -> 107 us  [per_device(): gathered = lax.all_gather(gathered, 'cz', axis=0, tiled=False)]
    reshape x5 -> x0, local copies, waits for them, and re-layouts: 17.4 us -> none  [the longest x1 7.33 us: per_device(): piece_keys.reshape(count, tile_width)]
    dot_general x17 -> x2, matrix products: 20.4 us -> 7.21 us  [the longest x1 4.88 us: per_device(): jnp.einsum('bhrj,bjd->brhd', weights.astype(jnp.bfloat16), all_vals, pref...]
    all_gather x0 -> x1, blocking collectives: none -> 12.5 us  [per_device(): gathered = lax.all_gather(both, 'cy', axis=0, tiled=False)]
    gather x0 -> x2, local copies, waits for them, and re-layouts: none -> 8.38 us  [the longest x1 4.25 us: per_device(): jnp.take(tiles, tile_row(safe_list, 1), axis=0)]
    all_to_all x1, blocking collectives: 22.4 us -> 14.1 us  [per_device(): lax.all_to_all(attended, 'kvh', split_axis=0, concat_axis=1, tiled=True)]
    ppermute x2 -> x0, starting transfers between devices: 7.92 us -> none  [passed_along(): lax.ppermute(value, axis, [(source, source + steps) for source in range(f...]
  transfers between devices with their start and end apart: 4 -> 1, of which waited for: 2 -> 1; matrix products, arithmetic and copies ran while one was open for 3% -> 3% of each run, Pallas kernels for 0% -> 0%
where the time goes in v1:
time: 178 us; the launch traced here: 177 us
  waiting for transfers between devices  107 us (60%)
  blocking collectives  26.6 us (15%)
  between operations  13.6 us (8%)
  local copies, waits for them, and re-layouts  12.3 us (7%)
  other arithmetic  10.3 us (6%)
  matrix products  7.21 us (4%)
    all_gather x1, waiting for transfers between devices, per_device(): gathered = lax.all_gather(gathered, 'cz', axis=0, tiled=False)  107 us
    all_to_all x1, blocking collectives, per_device(): lax.all_to_all(attended, 'kvh', split_axis=0, concat_axis=1, tiled=True)  14.1 us
    all_gather x1, blocking collectives, per_device(): gathered = lax.all_gather(both, 'cy', axis=0, tiled=False)  12.5 us
    dot_general x1, matrix products, per_device(): jnp.einsum('bhrj,bjd->brhd', weights.astype(jnp.bfloat16), all_vals, pref...  4.88 us
    gather x1, local copies, waits for them, and re-layouts, per_device(): jnp.take(tiles, tile_row(safe_list, 1), axis=0)  4.25 us
    gather x1, local copies, waits for them, and re-layouts, per_device(): jnp.take(tiles, tile_row(safe_list, 0), axis=0)  4.13 us
  transfers between devices with their start and end apart: 1, of which 1 were waited for; matrix products, arithmetic and copies ran while one was open for 3% of the time, Pallas kernels for 0%

profile of v1, /device:TPU:1, one launch (start us, length us, event | category | flops | bytes accessed | tf_op | source)
XLA Modules:
  0.0 177.3 jit_solution(10611880718977461163)
XLA Ops:
  6.5 0.0 copy-start.1
  6.5 0.0 copy-start
  6.5 0.0 all-gather.4.cloned.1.call-start
  6.5 0.9 pad_maximum_fusion
  7.5 12.5 %all-gather = bf16[2048,128]{1,0:T(8,128)(2,1)} all-gather(bf16[512,128]{1,0:T(8,128)(2,1)S(1)} %pad_maximum_fusion), channel_id=2, replica_groups=mesh['cy'=4,'cz'=16,'kvh'=8] {'cy'}, dimensions={0}, use_global_device_ids=true | all-gather | bytes 655360 | tf_op jit(solution)/shard_map/all_gather | solution.py:24
  20.0 0.0 all-gather.4.cloned.1.call-update
  20.1 0.7 compare_bitcast_fusion
  20.8 0.1 ne.84
  20.9 0.7 maximum_shift-right-logical_fusion
  21.6 0.1 div.57
  21.7 0.1 rem.92
  21.7 0.1 broadcast_in_dim.23
  21.8 0.1 broadcast_in_dim.28
  21.9 1.1 copy.17
  23.1 0.6 compare_and_fusion.1
  23.7 0.6 compare_and_fusion
  24.2 0.6 pad_clamp_fusion.1
  24.8 0.1 broadcast_compare_fusion
  24.9 0.1 iota_add_fusion.1
  25.0 0.1 iota_add_fusion
  25.0 0.2 and_and_fusion
  25.2 0.1 broadcast_in_dim.29
  25.3 0.4 pad_add_fusion
  25.7 107.2 %all-gather.4.cloned.1.call-done = bf16[64,512,128]{2,1,0:T(8,128)(2,1)} async-done(((bf16[4,512,128]{2,1,0:T(8,128)(2,1)}), bf16[64,512,128]{2,1,0:T(8,128)(2,1)}) %all-gather.4.cloned.1.call-update) | async-done | bytes 8388624 | tf_op jit(solution)/shard_map/all_gather | solution.py:25
  132.9 0.9 constant_dynamic-slice_fusion.1
  133.8 0.0 copy-done
  133.8 0.7 fusion.32
  134.5 0.0 copy-done.1
  134.5 4.1 %gather_fusion.1 = bf16[64,64,128]{2,1,0:T(8,128)(2,1)S(1)} fusion(bf16[512,64,128]{2,1,0:T(8,128)(2,1)} %bitcast.71, s32[1024]{0:T(1024)S(1)} %pad_clamp_fusion), kind=kCustom, calls=%fused_computation.1.clone | custom fusion | bytes 2097408 | tf_op jit(solution)/shard_map/jit(_take)/gather | solution.py:35
  138.7 4.3 %gather_fusion = bf16[64,64,128]{2,1,0:T(8,128)(2,1)S(1)} fusion(bf16[512,64,128]{2,1,0:T(8,128)(2,1)} %bitcast.72, s32[1024]{0:T(1024)} %pad_clamp_fusion.1), kind=kCustom, calls=%fused_computation.clone | custom fusion | bytes 2097408 | tf_op jit(solution)/shard_map/jit(_take)/gather | solution.py:36
  142.9 0.0 copy-start.2
  142.9 0.9 broadcast_select_fusion.1
  143.8 0.8 broadcast_select_fusion
  144.6 0.0 copy-done.2
  144.6 2.3 %fusion.2 = (f32[4,8,64]{2,1,0:T(8,128)S(1)}, f32[4,1344,64,8]{1,2,3,0:T(8,128)S(1)}) fusion(pred[4,64,1344]{2,1,0:T(8,128)(4,1)S(1)} %pad_add_fusion, bf16[4,64,8,128]{3,2,1,0:T(8,128)(2,1)S(1)} %bitcast.74, bf16[4,1024,128]{2,1,0:T(8,128)(2,1)S(1)} %bitcast.69, bf16[1,320,128]{2,1,0:T(8,128)(2,1)S(1)} %get-tuple-element.19, ...), kind=kOutput, calls=%fused_computation.6 | convolution fusion | flops 719779840 | bytes 13262848 | tf_op jit(solution)/shard_map/brhd,bjd->bhrj/dot_general | solution.py:73
  147.0 3.1 %fusion = f32[4,8,64]{2,1,0:T(8,128)S(1)} fusion(f32[4,1344,64,8]{1,2,3,0:T(8,128)S(1)} %get-tuple-element.28, f32[4,8,64]{2,1,0:T(8,128)S(1)} %get-tuple-element.27, pred[4,64,1344]{2,1,0:T(8,128)(4,1)S(1)} %pad_add_fusion), kind=kLoop, calls=%fused_computation.4 | loop fusion | flops 11008000 | bytes 11370496 | tf_op jit(solution)/shard_map/reduce_sum | solution.py:78
  150.0 4.9 %divide_convert_fusion = bf16[4,64,8,128]{3,1,2,0:T(8,128)(2,1)S(1)} fusion(f32[4,1344,64,8]{1,2,3,0:T(8,128)S(1)} %get-tuple-element.28, f32[4,8,64]{2,1,0:T(8,128)S(1)} %get-tuple-element.27, pred[4,64,1344]{2,1,0:T(8,128)(4,1)S(1)} %pad_add_fusion, bf16[4,1024,128]{2,1,0:T(8,128)(2,1)S(1)} %bitcast.68, bf16[1,320,128]{2,1,0:T(8,128)(2,1)S(1)} %get-tuple-element.15, ...), kind=kOutput, calls=%fused_computation.30 | convolution fusion | flops 723058688 | bytes 13271040 | tf_op jit(solution)/shard_map/bhrj,bjd->brhd/dot_general | solution.py:79
  154.9 0.3 copy.12
  155.3 0.2 all_to_all.14
  155.5 14.1 %all_to_all.19 = bf16[8,32,1024]{2,1,0:T(8,128)(2,1)S(1)} all-to-all(bf16[8,32,1024]{2,1,0:T(8,128)(2,1)S(1)} %all_to_all.14), channel_id=1, replica_groups=mesh['cy'=4,'cz'=16,'kvh'=8] {'kvh'}, dimensions={0} | all-to-all | bytes 1048576 | tf_op jit(solution)/shard_map/all_to_all | solution.py:84
  169.6 0.8 copy.16
  (3 shorter events, 0.1 us)
Async XLA Ops:
  6.5 127.9 %copy-start.1 = (bf16[256,128]{1,0:T(8,128)(2,1)S(1)}, bf16[256,128]{1,0:T(8,128)(2,1)}, u32[]{:S(2)}) copy-start(bf16[256,128]{1,0:T(8,128)(2,1)} %param.8) | copy-start | bytes 196612
  6.5 127.2 %copy-start = (bf16[256,128]{1,0:T(8,128)(2,1)S(1)}, bf16[256,128]{1,0:T(8,128)(2,1)}, u32[]{:S(2)}) copy-start(bf16[256,128]{1,0:T(8,128)(2,1)} %param.7) | copy-start | bytes 196612
  6.5 126.4 %all-gather.4.cloned.1.call-start = ((), (), s32[]{:S(2)}) async-start(), calls=%async_computation.1 | async-start | bytes 8912896 | tf_op jit(solution)/shard_map/all_gather | solution.py:25
  142.9 1.7 copy-start.2
Sparse Core Ops, SparseCore 0:
  20.2 112.6 all-gather.3

commit v2 on v1

v2 whole, which is shorter than its diff:
```python
import functools

import jax
import jax.numpy as jnp
from jax import lax
from jax.experimental import pallas as pl
from jax.experimental.pallas import tpu as pltpu
from jax.sharding import Mesh
from jax.sharding import PartitionSpec as P

TILE = 64
SEL = 16
WINDOW = 256
WIN_TILES = WINDOW // TILE + 1
SLOTS = WIN_TILES + SEL + 1

masked_score = -1e30


def attention_kernel(rows_ref, q_ref, colmask_ref, tiles_hbm, out_ref, kbuf, vbuf, sems, *, per_dev, scale):
    b = pl.program_id(0)
    head_size = kbuf.shape[1]
    copies = []
    for i in range(SLOTS):
        row = rows_ref[b * SLOTS + i]
        dst = pl.ds(i * TILE, TILE)
        ck = pltpu.make_async_copy(tiles_hbm.at[row], kbuf.at[dst], sems.at[0, i])
        cv = pltpu.make_async_copy(tiles_hbm.at[row + per_dev], vbuf.at[dst], sems.at[1, i])
        ck.start()
        cv.start()
        copies += [ck, cv]
    for c in copies:
        c.wait()
    q = q_ref[...]
    heads = q.shape[1] // head_size
    qs = jnp.concatenate([q[:, h * head_size : (h + 1) * head_size] for h in range(heads)], axis=0)
    s = lax.dot_general(qs, kbuf[...], (((1,), (1,)), ((), ())), preferred_element_type=jnp.float32) * scale
    r = lax.broadcasted_iota(jnp.int32, s.shape, 0) % TILE
    j = lax.broadcasted_iota(jnp.int32, s.shape, 1)
    in_window = (j > r) & (j <= r + WINDOW)
    ok = (colmask_ref[0] > 0) & ((j >= WIN_TILES * TILE) | in_window)
    s = jnp.where(ok, s, masked_score)
    peak = jnp.max(s, axis=1, keepdims=True)
    w = jnp.exp(s - peak)
    total = jnp.sum(w, axis=1, keepdims=True)
    num = jnp.dot(w.astype(jnp.bfloat16), vbuf[...], preferred_element_type=jnp.float32)
    res = (num / total).astype(out_ref.dtype)
    for h in range(heads):
        out_ref[:, h * head_size : (h + 1) * head_size] = res[h * TILE : (h + 1) * TILE]


def block_attention(rows, queries, colmask, tiles, per_dev, scale):
    tok_rows, width = queries.shape
    head_size = tiles.shape[2]
    keys_per_block = SLOTS * TILE
    flops = 4 * tok_rows * width * keys_per_block
    return pl.pallas_call(
        functools.partial(attention_kernel, per_dev=per_dev, scale=scale),
        out_shape=jax.ShapeDtypeStruct((tok_rows, width), queries.dtype),
        grid_spec=pltpu.PrefetchScalarGridSpec(
            num_scalar_prefetch=1,
            grid=(per_dev,),
            in_specs=[
                pl.BlockSpec((TILE, width), lambda b, rows: (b, 0)),
                pl.BlockSpec((1, 1, keys_per_block), lambda b, rows: (b, 0, 0)),
                pl.BlockSpec(memory_space=pl.ANY),
            ],
            out_specs=pl.BlockSpec((TILE, width), lambda b, rows: (b, 0)),
            scratch_shapes=[
                pltpu.VMEM((keys_per_block, head_size), tiles.dtype),
                pltpu.VMEM((keys_per_block, head_size), tiles.dtype),
                pltpu.SemaphoreType.DMA((2, SLOTS)),
            ],
        ),
        cost_estimate=pl.CostEstimate(
            flops=flops,
            transcendentals=tok_rows * (width // head_size) * keys_per_block,
            bytes_accessed=2 * tok_rows * width * 2 + 2 * per_dev * SLOTS * TILE * head_size * 2,
        ),
    )(rows, queries, colmask, tiles)


def per_device(queries, keys, values, selection):
    tok_rows, head_size = keys.shape
    per_dev = tok_rows // TILE
    n_y = lax.axis_size("cy")
    n_z = lax.axis_size("cz")
    here = lax.axis_index("cy") * n_z + lax.axis_index("cz")
    scale = 1.0 / head_size**0.5

    both = jnp.concatenate([keys, values], axis=0)
    gathered = lax.all_gather(both, "cy", axis=0, tiled=False)
    gathered = lax.all_gather(gathered, "cz", axis=0, tiled=False)
    tiles = gathered.reshape(n_z * n_y * 2 * per_dev, TILE, head_size)

    def tile_row(tile_id):
        owner = tile_id // per_dev
        return (((owner % n_z) * n_y + owner // n_z) * 2) * per_dev + tile_id % per_dev

    lists = selection[0]
    listed = lists >= 0
    safe_list = jnp.maximum(lists, 0)
    block_index = jnp.arange(per_dev, dtype=jnp.int32)
    first = here * per_dev + block_index - (WIN_TILES - 1)
    window_tiles = jnp.maximum(first[:, None] + jnp.arange(WIN_TILES, dtype=jnp.int32)[None, :], 0)
    slot_tiles = jnp.concatenate([window_tiles, safe_list, window_tiles[:, :1]], axis=1)
    rows = tile_row(slot_tiles).reshape(-1)

    col = jnp.arange(SLOTS * TILE, dtype=jnp.int32)
    lowest = WINDOW - here * tok_rows - block_index * TILE
    window_cols = (col[None, :] < WIN_TILES * TILE) & (col[None, :] >= lowest[:, None])
    slot_of = jnp.clip(col // TILE - WIN_TILES, 0, SEL - 1)
    sel_cols = (col[None, :] >= WIN_TILES * TILE) & (col[None, :] < (WIN_TILES + SEL) * TILE)
    sel_cols = sel_cols & jnp.take(listed, slot_of, axis=1)
    colmask = (window_cols | sel_cols).astype(jnp.int32).reshape(per_dev, 1, SLOTS * TILE)

    attended = block_attention(rows, queries, colmask, tiles, per_dev, scale)
    return lax.all_to_all(attended, "kvh", split_axis=0, concat_axis=1, tiled=True)


def solution(mesh):
    devices = mesh.devices
    ctx = devices.shape[0]
    z = len({tuple(d.coords)[2] for d in devices[:, 0]})
    z = z if ctx % z == 0 else ctx
    grid = Mesh(devices.reshape(ctx // z, z, devices.shape[1]), ("cy", "cz", "kvh"))
    row = P(("cy", "cz"), "kvh")
    return jax.shard_map(
        per_device,
        mesh=grid,
        in_specs=(row, row, row, P("kvh", ("cy", "cz"), None)),
        out_specs=P(("cy", "cz", "kvh"), None),
        check_vma=False,
    )
```

time: 178 us -> 175 us (0.983)
  Pallas kernels: 0 us -> 19.3 us
  local copies, waits for them, and re-layouts: 12.3 us -> 4.92 us
  matrix products: 7.21 us -> 0 us
  other arithmetic: 10.3 us -> 3.73 us
    pallas_call x0 -> x1, Pallas kernels: none -> 19.3 us  [block_attention(): pl.pallas_call(functools.partial(attention_kernel, per_dev=per_dev, scale...]
    dot_general x2 -> x0, matrix products: 7.21 us -> none  [the longest x1 4.88 us: per_device(): jnp.einsum('bhrj,bjd->brhd', weights.astype(jnp.bfloat16), all_vals, pref...]
    gather x2, local copies, waits for them, and re-layouts: 8.38 us -> 3.91 us  [per_device(): sel_cols = sel_cols & jnp.take(listed, slot_of, axis=1)]
    reduce_sum x1 -> x0, other arithmetic: 3.09 us -> none  [per_device(): total = jnp.sum(weights, axis=-1)]
  transfers between devices with their start and end apart: 1 -> 1, of which waited for: 1 -> 1; matrix products, arithmetic and copies ran while one was open for 3% -> 4% of each run, Pallas kernels for 0% -> 0%
where the time goes in v2:
time: 175 us; the launch traced here: 174 us
  waiting for transfers between devices  106 us (61%)
  blocking collectives  26.8 us (15%)
  Pallas kernels  19.3 us (11%)
  between operations  13.5 us (8%)
  local copies, waits for them, and re-layouts  4.92 us (3%)
  other arithmetic  3.73 us (2%)
    all_gather x1, waiting for transfers between devices, per_device(): gathered = lax.all_gather(gathered, 'cz', axis=0, tiled=False)  106 us
    pallas_call x1, Pallas kernels, block_attention(): pl.pallas_call(functools.partial(attention_kernel, per_dev=per_dev, scale...  19.3 us
    all_to_all x1, blocking collectives, per_device(): lax.all_to_all(attended, 'kvh', split_axis=0, concat_axis=1, tiled=True)  14.3 us
    all_gather x1, blocking collectives, per_device(): gathered = lax.all_gather(both, 'cy', axis=0, tiled=False)  12.5 us
    gather x2, local copies, waits for them, and re-layouts, per_device(): sel_cols = sel_cols & jnp.take(listed, slot_of, axis=1)  3.91 us
  transfers between devices with their start and end apart: 1, of which 1 were waited for; matrix products, arithmetic and copies ran while one was open for 4% of the time, Pallas kernels for 0%

profile of v2, /device:TPU:1, one launch (start us, length us, event | category | flops | bytes accessed | tf_op | source)
XLA Modules:
  0.0 174.1 jit_solution(5530962419550098105)
XLA Ops:
  6.5 0.0 all-gather.4.cloned.1.call-start
  6.5 0.9 pad_maximum_fusion
  7.4 12.5 %all-gather = bf16[2048,128]{1,0:T(8,128)(2,1)} all-gather(bf16[512,128]{1,0:T(8,128)(2,1)S(1)} %pad_maximum_fusion), channel_id=2, replica_groups=mesh['cy'=4,'cz'=16,'kvh'=8] {'cy'}, dimensions={0}, use_global_device_ids=true | all-gather | bytes 655360 | tf_op jit(solution)/shard_map/all_gather | solution.py:92
  20.0 0.0 all-gather.4.cloned.1.call-update
  20.0 0.7 compare_bitcast_fusion
  20.7 0.1 copy.12
  20.8 0.1 add_maximum_fusion
  20.9 0.7 maximum_bitcast_fusion
  21.6 0.1 pad_add_fusion
  21.6 0.1 concatenate.9
  21.8 3.0 %gather_fusion = pred[1408,4]{1,0:T(8,128)(4,1)S(1)} fusion(pred[4,16]{0,1:T(8,128)(4,1)S(1)} %copy.12, s32[2048]{0:T(1024)S(1)} %pad_clamp_fusion), kind=kCustom, calls=%fused_computation | custom fusion | bytes 16896 | tf_op jit(solution)/shard_map/jit(_take)/gather | solution.py:114
  24.8 0.9 copy.14
  25.7 0.6 fusion.9.rows_ref
  26.3 0.7 or_convert_fusion.colmask_ref
  27.0 105.9 %all-gather.4.cloned.1.call-done = bf16[64,512,128]{2,1,0:T(8,128)(2,1)} async-done(((bf16[4,512,128]{2,1,0:T(8,128)(2,1)}), bf16[64,512,128]{2,1,0:T(8,128)(2,1)}) %all-gather.4.cloned.1.call-update) | async-done | bytes 8388624 | tf_op jit(solution)/shard_map/all_gather | solution.py:93
  132.9 19.3 %shard_map.46 = bf16[256,1024]{1,0:T(8,128)(2,1)} custom-call(s32[88]{0:T(128)} %fusion.9.rows_ref, bf16[256,1024]{1,0:T(8,128)(2,1)} %q_ref.1, s32[4,1,1408]{2,1,0:T(1,128)} %or_convert_fusion.colmask_ref, bf16[512,64,128]{2,1,0:T(8,128)(2,1)} %bitcast.14), custom_call_target="tpu_custom_call" | custom-call | flops 1476395008 | bytes 3932160 | tf_op jit(solution)/shard_map/pallas_call | solution.py:57
  152.2 14.3 %all_to_all.19 = bf16[8,32,1024]{2,1,0:T(8,128)(2,1)S(1)} all-to-all(bf16[8,32,1024]{2,1,0:T(8,128)(2,1)} %bitcast.15), channel_id=1, replica_groups=mesh['cy'=4,'cz'=16,'kvh'=8] {'kvh'}, dimensions={0} | all-to-all | bytes 1048576 | tf_op jit(solution)/shard_map/all_to_all | solution.py:118
  166.5 0.8 copy.18
  (6 shorter events, 0.1 us)
Async XLA Ops:
  6.5 126.3 %all-gather.4.cloned.1.call-start = ((), (), s32[]{:S(2)}) async-start(), calls=%async_computation.1 | async-start | bytes 8912896 | tf_op jit(solution)/shard_map/all_gather | solution.py:93
Sparse Core Ops, SparseCore 0:
  20.1 112.7 all-gather.3

commit v3 on v2

--- a/solution.py
+++ b/solution.py
@@ -18,35 +18,48 @@
 
 
 def attention_kernel(rows_ref, q_ref, colmask_ref, tiles_hbm, out_ref, kbuf, vbuf, sems, *, per_dev, scale):
-    b = pl.program_id(0)
-    head_size = kbuf.shape[1]
-    copies = []
-    for i in range(SLOTS):
-        row = rows_ref[b * SLOTS + i]
-        dst = pl.ds(i * TILE, TILE)
-        ck = pltpu.make_async_copy(tiles_hbm.at[row], kbuf.at[dst], sems.at[0, i])
-        cv = pltpu.make_async_copy(tiles_hbm.at[row + per_dev], vbuf.at[dst], sems.at[1, i])
-        ck.start()
-        cv.start()
-        copies += [ck, cv]
-    for c in copies:
-        c.wait()
-    q = q_ref[...]
-    heads = q.shape[1] // head_size
-    qs = jnp.concatenate([q[:, h * head_size : (h + 1) * head_size] for h in range(heads)], axis=0)
-    s = lax.dot_general(qs, kbuf[...], (((1,), (1,)), ((), ())), preferred_element_type=jnp.float32) * scale
-    r = lax.broadcasted_iota(jnp.int32, s.shape, 0) % TILE
-    j = lax.broadcasted_iota(jnp.int32, s.shape, 1)
-    in_window = (j > r) & (j <= r + WINDOW)
-    ok = (colmask_ref[0] > 0) & ((j >= WIN_TILES * TILE) | in_window)
-    s = jnp.where(ok, s, masked_score)
-    peak = jnp.max(s, axis=1, keepdims=True)
-    w = jnp.exp(s - peak)
-    total = jnp.sum(w, axis=1, keepdims=True)
-    num = jnp.dot(w.astype(jnp.bfloat16), vbuf[...], preferred_element_type=jnp.float32)
-    res = (num / total).astype(out_ref.dtype)
-    for h in range(heads):
-        out_ref[:, h * head_size : (h + 1) * head_size] = res[h * TILE : (h + 1) * TILE]
+    head_size = kbuf.shape[2]
+    heads = q_ref.shape[1] // head_size
+    keys_per_block = kbuf.shape[1]
+
+    def fetch(b):
+        slot = b % 2
+        copies = []
+        for i in range(SLOTS):
+            row = rows_ref[b * SLOTS + i]
+            dst = pl.ds(i * TILE, TILE)
+            ck = pltpu.make_async_copy(tiles_hbm.at[row], kbuf.at[slot, dst], sems.at[slot, 0, i])
+            cv = pltpu.make_async_copy(tiles_hbm.at[row + per_dev], vbuf.at[slot, dst], sems.at[slot, 1, i])
+            ck.start()
+            cv.start()
+            copies += [ck, cv]
+        return copies
+
+    r = lax.broadcasted_iota(jnp.int32, (TILE, keys_per_block), 0)
+    j = lax.broadcasted_iota(jnp.int32, (TILE, keys_per_block), 1)
+    row_ok = (j >= WIN_TILES * TILE) | ((j > r) & (j <= r + WINDOW))
+    pending = fetch(0)
+    for b in range(per_dev):
+        for c in pending:
+            c.wait()
+        if b + 1 < per_dev:
+            pending = fetch(b + 1)
+        slot = b % 2
+        q = q_ref[pl.ds(b * TILE, TILE), :]
+        qs = jnp.concatenate([q[:, h * head_size : (h + 1) * head_size] for h in range(heads)], axis=0)
+        s = lax.dot_general(
+            qs, kbuf[slot], (((1,), (1,)), ((), ())), preferred_element_type=jnp.float32
+        )
+        ok = row_ok & (colmask_ref[b] > 0)
+        s = jnp.where(ok[None], (s * scale).reshape(heads, TILE, keys_per_block), masked_score)
+        s = s.reshape(heads * TILE, keys_per_block)
+        peak = jnp.max(s, axis=1, keepdims=True)
+        w = jnp.exp(s - peak)
+        total = jnp.sum(w, axis=1, keepdims=True)
+        num = jnp.dot(w.astype(jnp.bfloat16), vbuf[slot], preferred_element_type=jnp.float32)
+        res = (num / total).astype(out_ref.dtype)
+        for h in range(heads):
+            out_ref[pl.ds(b * TILE, TILE), h * head_size : (h + 1) * head_size] = res[h * TILE : (h + 1) * TILE]
 
 
 def block_attention(rows, queries, colmask, tiles, per_dev, scale):
@@ -54,24 +67,22 @@
     head_size = tiles.shape[2]
     keys_per_block = SLOTS * TILE
     flops = 4 * tok_rows * width * keys_per_block
+    vmem = pltpu.MemorySpace.VMEM
     return pl.pallas_call(
         functools.partial(attention_kernel, per_dev=per_dev, scale=scale),
         out_shape=jax.ShapeDtypeStruct((tok_rows, width), queries.dtype),
-        grid_spec=pltpu.PrefetchScalarGridSpec(
-            num_scalar_prefetch=1,
-            grid=(per_dev,),
-            in_specs=[
-                pl.BlockSpec((TILE, width), lambda b, rows: (b, 0)),
-                pl.BlockSpec((1, 1, keys_per_block), lambda b, rows: (b, 0, 0)),
-                pl.BlockSpec(memory_space=pl.ANY),
-            ],
-            out_specs=pl.BlockSpec((TILE, width), lambda b, rows: (b, 0)),
-            scratch_shapes=[
-                pltpu.VMEM((keys_per_block, head_size), tiles.dtype),
-                pltpu.VMEM((keys_per_block, head_size), tiles.dtype),
-                pltpu.SemaphoreType.DMA((2, SLOTS)),
-            ],
-        ),
+        in_specs=[
+            pl.BlockSpec(memory_space=pltpu.MemorySpace.SMEM),
+            pl.BlockSpec(memory_space=vmem),
+            pl.BlockSpec(memory_space=vmem),
+            pl.BlockSpec(memory_space=pl.ANY),
+        ],
+        out_specs=pl.BlockSpec(memory_space=vmem),
+        scratch_shapes=[
+            pltpu.VMEM((2, keys_per_block, head_size), tiles.dtype),
+            pltpu.VMEM((2, keys_per_block, head_size), tiles.dtype),
+            pltpu.SemaphoreType.DMA((2, 2, SLOTS)),
+        ],
         cost_estimate=pl.CostEstimate(
             flops=flops,
             transcendentals=tok_rows * (width // head_size) * keys_per_block,

time: 175 us -> 169 us (0.966)
  Pallas kernels: 19.3 us -> 13.2 us
    pallas_call x1, Pallas kernels: 19.3 us -> 13.2 us  [block_attention(): pl.pallas_call(functools.partial(attention_kernel, per_dev=per_dev, scale...]
where the time goes in v3:
time: 169 us; the launch traced here: 168 us
  waiting for transfers between devices  106 us (63%)
  blocking collectives  26.8 us (16%)
  between operations  13.5 us (8%)
  Pallas kernels  13.2 us (8%)
  local copies, waits for them, and re-layouts  4.92 us (3%)
  other arithmetic  3.73 us (2%)
    all_gather x1, waiting for transfers between devices, per_device(): gathered = lax.all_gather(gathered, 'cz', axis=0, tiled=False)  106 us
    all_to_all x1, blocking collectives, per_device(): lax.all_to_all(attended, 'kvh', split_axis=0, concat_axis=1, tiled=True)  14.3 us
    pallas_call x1, Pallas kernels, block_attention(): pl.pallas_call(functools.partial(attention_kernel, per_dev=per_dev, scale...  13.2 us
    all_gather x1, blocking collectives, per_device(): gathered = lax.all_gather(both, 'cy', axis=0, tiled=False)  12.5 us
    gather x2, local copies, waits for them, and re-layouts, per_device(): sel_cols = sel_cols & jnp.take(listed, slot_of, axis=1)  3.91 us
  transfers between devices with their start and end apart: 1, of which 1 were waited for; matrix products, arithmetic and copies ran while one was open for 4% of the time, Pallas kernels for 0%

profile of v3, /device:TPU:1, one launch (start us, length us, event | category | flops | bytes accessed | tf_op | source)
XLA Modules:
  0.0 168.1 jit_solution(14857066717250689493)
XLA Ops:
  6.5 0.0 all-gather.4.cloned.1.call-start
  6.5 0.9 pad_maximum_fusion
  7.4 12.5 %all-gather = bf16[2048,128]{1,0:T(8,128)(2,1)} all-gather(bf16[512,128]{1,0:T(8,128)(2,1)S(1)} %pad_maximum_fusion), channel_id=2, replica_groups=mesh['cy'=4,'cz'=16,'kvh'=8] {'cy'}, dimensions={0}, use_global_device_ids=true | all-gather | bytes 655360 | tf_op jit(solution)/shard_map/all_gather | solution.py:103
  20.0 0.0 all-gather.4.cloned.1.call-update
  20.0 0.7 compare_bitcast_fusion
  20.7 0.1 copy.12
  20.8 0.1 add_maximum_fusion
  20.9 0.7 maximum_bitcast_fusion
  21.6 0.1 pad_add_fusion
  21.6 0.1 concatenate.9
  21.8 3.0 %gather_fusion = pred[1408,4]{1,0:T(8,128)(4,1)S(1)} fusion(pred[4,16]{0,1:T(8,128)(4,1)S(1)} %copy.12, s32[2048]{0:T(1024)S(1)} %pad_clamp_fusion), kind=kCustom, calls=%fused_computation | custom fusion | bytes 16896 | tf_op jit(solution)/shard_map/jit(_take)/gather | solution.py:125
  24.8 0.9 copy.14
  25.7 0.6 fusion.9.rows_ref
  26.3 0.7 or_convert_fusion.colmask_ref
  27.0 105.9 %all-gather.4.cloned.1.call-done = bf16[64,512,128]{2,1,0:T(8,128)(2,1)} async-done(((bf16[4,512,128]{2,1,0:T(8,128)(2,1)}), bf16[64,512,128]{2,1,0:T(8,128)(2,1)}) %all-gather.4.cloned.1.call-update) | async-done | bytes 8388624 | tf_op jit(solution)/shard_map/all_gather | solution.py:104
  132.9 13.2 %shard_map.46 = bf16[256,1024]{1,0:T(8,128)(2,1)} custom-call(s32[88]{0:T(128)} %fusion.9.rows_ref, bf16[256,1024]{1,0:T(8,128)(2,1)} %q_ref.1, s32[4,1,1408]{2,1,0:T(1,128)} %or_convert_fusion.colmask_ref, bf16[512,64,128]{2,1,0:T(8,128)(2,1)} %bitcast.14), custom_call_target="tpu_custom_call" | custom-call | flops 1476395008 | bytes 3932160 | tf_op jit(solution)/shard_map/pallas_call | solution.py:71
  146.1 14.3 %all_to_all.19 = bf16[8,32,1024]{2,1,0:T(8,128)(2,1)S(1)} all-to-all(bf16[8,32,1024]{2,1,0:T(8,128)(2,1)} %bitcast.15), channel_id=1, replica_groups=mesh['cy'=4,'cz'=16,'kvh'=8] {'kvh'}, dimensions={0} | all-to-all | bytes 1048576 | tf_op jit(solution)/shard_map/all_to_all | solution.py:129
  160.4 0.8 copy.18
  (6 shorter events, 0.1 us)
Async XLA Ops:
  6.5 126.3 %all-gather.4.cloned.1.call-start = ((), (), s32[]{:S(2)}) async-start(), calls=%async_computation.1 | async-start | bytes 8912896 | tf_op jit(solution)/shard_map/all_gather | solution.py:104
Sparse Core Ops, SparseCore 0:
  20.1 112.7 all-gather.3

commit v4 on v3

v4 whole, which is shorter than its diff:
```python
import functools

import jax
import jax.numpy as jnp
from jax import lax
from jax.experimental import pallas as pl
from jax.experimental.pallas import tpu as pltpu
from jax.sharding import Mesh
from jax.sharding import PartitionSpec as P

TILE = 64
SEL = 16
WINDOW = 256
WIN_COLS = WINDOW + 2 * TILE
SEL_COLS = SEL * TILE

masked_score = -1e30


def attention_kernel(
    rows_ref, prev_ref, q_ref, keys_ref, values_ref, colmask_ref, tiles_hbm, out_ref,
    selbuf, prevbuf, wink, winv, sems, prev_sem, *, per_dev, scale,
):
    head_size = keys_ref.shape[1]
    tok_rows = keys_ref.shape[0]
    heads = q_ref.shape[1] // head_size

    def fetch(b):
        slot = b % 2
        copies = []
        for i in range(SEL):
            cp = pltpu.make_async_copy(tiles_hbm.at[rows_ref[b * SEL + i]], selbuf.at[slot, i], sems.at[slot, i])
            cp.start()
            copies.append(cp)
        return copies

    prev_copy = pltpu.make_async_copy(tiles_hbm.at[pl.ds(prev_ref[0], per_dev)], prevbuf, prev_sem.at[0])
    prev_copy.start()
    pending = fetch(0)
    wink[pl.ds(tok_rows, tok_rows), :] = keys_ref[...]
    winv[pl.ds(tok_rows, tok_rows), :] = values_ref[...]
    pad = wink.shape[0] - 2 * tok_rows
    wink[pl.ds(2 * tok_rows, pad), :] = jnp.zeros((pad, head_size), wink.dtype)
    winv[pl.ds(2 * tok_rows, pad), :] = jnp.zeros((pad, head_size), winv.dtype)
    prev_copy.wait()
    wink[pl.ds(0, tok_rows), :] = prevbuf[:, 0].reshape(tok_rows, head_size)
    winv[pl.ds(0, tok_rows), :] = prevbuf[:, 1].reshape(tok_rows, head_size)

    r = lax.broadcasted_iota(jnp.int32, (TILE, WIN_COLS), 0)
    j = lax.broadcasted_iota(jnp.int32, (TILE, WIN_COLS), 1)
    in_window = (j > r) & (j <= r + WINDOW)
    dims = (((1,), (1,)), ((), ()))
    for b in range(per_dev):
        for c in pending:
            c.wait()
        if b + 1 < per_dev:
            pending = fetch(b + 1)
        slot = b % 2
        q = q_ref[pl.ds(b * TILE, TILE), :]
        qs = jnp.concatenate([q[:, h * head_size : (h + 1) * head_size] for h in range(heads)], axis=0)
        k_win = wink[pl.ds(b * TILE, WIN_COLS), :]
        v_win = winv[pl.ds(b * TILE, WIN_COLS), :]
        k_sel = selbuf[slot, :, 0].reshape(SEL_COLS, head_size)
        v_sel = selbuf[slot, :, 1].reshape(SEL_COLS, head_size)
        mask = colmask_ref[b]
        win_ok = in_window & (mask[:, :WIN_COLS] > 0)
        sel_ok = mask[:, WIN_COLS:] > 0
        s_win = lax.dot_general(qs, k_win, dims, preferred_element_type=jnp.float32) * scale
        s_sel = lax.dot_general(qs, k_sel, dims, preferred_element_type=jnp.float32) * scale
        s_win = jnp.where(win_ok[None], s_win.reshape(heads, TILE, WIN_COLS), masked_score)
        s_win = s_win.reshape(heads * TILE, WIN_COLS)
        s_sel = jnp.where(sel_ok, s_sel, masked_score)
        peak = jnp.maximum(jnp.max(s_win, axis=1, keepdims=True), jnp.max(s_sel, axis=1, keepdims=True))
        w_win = jnp.exp(s_win - peak)
        w_sel = jnp.exp(s_sel - peak)
        total = jnp.sum(w_win, axis=1, keepdims=True) + jnp.sum(w_sel, axis=1, keepdims=True)
        num = jnp.dot(w_win.astype(jnp.bfloat16), v_win, preferred_element_type=jnp.float32)
        num = num + jnp.dot(w_sel.astype(jnp.bfloat16), v_sel, preferred_element_type=jnp.float32)
        res = (num / total).astype(out_ref.dtype)
        for h in range(heads):
            out_ref[pl.ds(b * TILE, TILE), h * head_size : (h + 1) * head_size] = res[h * TILE : (h + 1) * TILE]


def block_attention(rows, prev, queries, keys, values, colmask, tiles, per_dev, scale):
    tok_rows, width = queries.shape
    head_size = keys.shape[1]
    keys_per_block = WIN_COLS + SEL_COLS
    vmem = pltpu.MemorySpace.VMEM
    smem = pltpu.MemorySpace.SMEM
    return pl.pallas_call(
        functools.partial(attention_kernel, per_dev=per_dev, scale=scale),
        out_shape=jax.ShapeDtypeStruct((tok_rows, width), queries.dtype),
        in_specs=[
            pl.BlockSpec(memory_space=smem),
            pl.BlockSpec(memory_space=smem),
            pl.BlockSpec(memory_space=vmem),
            pl.BlockSpec(memory_space=vmem),
            pl.BlockSpec(memory_space=vmem),
            pl.BlockSpec(memory_space=vmem),
            pl.BlockSpec(memory_space=pl.ANY),
        ],
        out_specs=pl.BlockSpec(memory_space=vmem),
        scratch_shapes=[
            pltpu.VMEM((2, SEL, 2, TILE, head_size), tiles.dtype),
            pltpu.VMEM((per_dev, 2, TILE, head_size), tiles.dtype),
            pltpu.VMEM((2 * tok_rows + TILE, head_size), tiles.dtype),
            pltpu.VMEM((2 * tok_rows + TILE, head_size), tiles.dtype),
            pltpu.SemaphoreType.DMA((2, SEL)),
            pltpu.SemaphoreType.DMA((1,)),
        ],
        cost_estimate=pl.CostEstimate(
            flops=4 * tok_rows * width * keys_per_block,
            transcendentals=tok_rows * (width // head_size) * keys_per_block,
            bytes_accessed=2 * tok_rows * width * 2 + 2 * per_dev * SEL_COLS * head_size * 2,
        ),
    )(rows, prev, queries, keys, values, colmask, tiles)


def device_attention(queries, keys, values, lists, tiles, here, n_y, n_z):
    tok_rows, head_size = keys.shape
    per_dev = tok_rows // TILE
    scale = 1.0 / head_size**0.5

    def tile_index(tile_id):
        owner = tile_id // per_dev
        return ((owner % n_z) * n_y + owner // n_z) * per_dev + tile_id % per_dev

    listed = lists >= 0
    rows = tile_index(jnp.maximum(lists, 0)).reshape(-1).astype(jnp.int32)
    prev = tile_index(jnp.maximum(here - 1, 0) * per_dev).reshape(1).astype(jnp.int32)

    block_index = jnp.arange(per_dev, dtype=jnp.int32)
    win_col = jnp.arange(WIN_COLS, dtype=jnp.int32)
    lowest = WINDOW - here * tok_rows - block_index * TILE
    win_flags = (win_col[None, :] < WINDOW + TILE) & (win_col[None, :] >= lowest[:, None])
    sel_flags = jnp.repeat(listed, TILE, axis=1)
    colmask = jnp.concatenate([win_flags, sel_flags], axis=1).astype(jnp.int32)
    colmask = colmask.reshape(per_dev, 1, WIN_COLS + SEL_COLS)
    return block_attention(rows, prev, queries, keys, values, colmask, tiles, per_dev, scale)


def per_device(queries, keys, values, selection):
    tok_rows, head_size = keys.shape
    per_dev = tok_rows // TILE
    n_y = lax.axis_size("cy")
    n_z = lax.axis_size("cz")
    here = lax.axis_index("cy") * n_z + lax.axis_index("cz")

    both = jnp.stack(
        [keys.reshape(per_dev, TILE, head_size), values.reshape(per_dev, TILE, head_size)], axis=1
    )
    gathered = lax.all_gather(both, "cy", axis=0, tiled=False)
    gathered = lax.all_gather(gathered, "cz", axis=0, tiled=False)
    tiles = gathered.reshape(n_z * n_y * per_dev, 2, TILE, head_size)
    attended = device_attention(queries, keys, values, selection[0], tiles, here, n_y, n_z)
    return lax.all_to_all(attended, "kvh", split_axis=0, concat_axis=1, tiled=True)


def solution(mesh):
    devices = mesh.devices
    ctx = devices.shape[0]
    z = len({tuple(d.coords)[2] for d in devices[:, 0]})
    z = z if ctx % z == 0 else ctx
    grid = Mesh(devices.reshape(ctx // z, z, devices.shape[1]), ("cy", "cz", "kvh"))
    row = P(("cy", "cz"), "kvh")
    return jax.shard_map(
        per_device,
        mesh=grid,
        in_specs=(row, row, row, P("kvh", ("cy", "cz"), None)),
        out_specs=P(("cy", "cz", "kvh"), None),
        check_vma=False,
    )
```

time: 169 us -> 167 us (0.988)
  waiting for transfers between devices: 106 us -> 110 us
  local copies, waits for them, and re-layouts: 4.92 us -> 1.89 us
    gather x2 -> x0, local copies, waits for them, and re-layouts: 3.91 us -> none  [per_device(): sel_cols = sel_cols & jnp.take(listed, slot_of, axis=1)]
    all_gather x1, waiting for transfers between devices: 106 us -> 110 us  [per_device(): gathered = lax.all_gather(gathered, 'cz', axis=0, tiled=False)]
  transfers between devices with their start and end apart: 1 -> 1, of which waited for: 1 -> 1; matrix products, arithmetic and copies ran while one was open for 4% -> 2% of each run, Pallas kernels for 0% -> 0%
where the time goes in v4:
time: 167 us; the launch traced here: 166 us
  waiting for transfers between devices  110 us (66%)
  blocking collectives  26.8 us (16%)
  between operations  13.5 us (8%)
  Pallas kernels  11.6 us (7%)
  other arithmetic  2.91 us (2%)
  local copies, waits for them, and re-layouts  1.89 us (1%)
    all_gather x1, waiting for transfers between devices, per_device(): gathered = lax.all_gather(gathered, 'cz', axis=0, tiled=False)  110 us
    all_to_all x1, blocking collectives, per_device(): lax.all_to_all(attended, 'kvh', split_axis=0, concat_axis=1, tiled=True)  14.3 us
    all_gather x1, blocking collectives, per_device(): gathered = lax.all_gather(both, 'cy', axis=0, tiled=False)  12.5 us
    pallas_call x1, Pallas kernels, block_attention(): pl.pallas_call(functools.partial(attention_kernel, per_dev=per_dev, scale...  11.6 us
  transfers between devices with their start and end apart: 1, of which 1 were waited for; matrix products, arithmetic and copies ran while one was open for 2% of the time, Pallas kernels for 0%

profile of v4, /device:TPU:1, one launch (start us, length us, event | category | flops | bytes accessed | tf_op | source)
XLA Modules:
  0.0 166.4 jit_solution(7246827955131143839)
XLA Ops:
  6.5 0.0 all-gather.4.cloned.1.call-start
  6.5 0.9 pad_maximum_fusion
  7.4 12.5 %all-gather = bf16[16,2,64,128]{3,2,1,0:T(8,128)(2,1)} all-gather(bf16[4,2,64,128]{3,2,1,0:T(8,128)(2,1)S(1)} %pad_maximum_fusion), channel_id=2, replica_groups=mesh['cy'=4,'cz'=16,'kvh'=8] {'cy'}, dimensions={0}, use_global_device_ids=true | all-gather | bytes 655360 | tf_op jit(solution)/shard_map/all_gather | solution.py:152
  20.0 0.0 all-gather.4.cloned.1.call-update
  20.0 0.7 compare_bitcast_fusion
  20.7 0.1 ne.66
  20.8 0.7 maximum_shift-right-logical_fusion
  21.5 0.1 div.35
  21.6 0.1 rem.70
  21.7 0.1 broadcast_in_dim.2
  21.8 0.1 concatenate.15
  21.9 0.1 fusion.1
  22.0 0.6 copy.17.colmask_ref
  22.6 0.5 fusion.2.rows_ref
  23.1 109.7 %all-gather.4.cloned.1.call-done = bf16[64,4,2,64,128]{4,3,2,1,0:T(8,128)(2,1)} async-done(((bf16[4,4,2,64,128]{4,3,2,1,0:T(8,128)(2,1)}), bf16[64,4,2,64,128]{4,3,2,1,0:T(8,128)(2,1)}) %all-gather.4.cloned.1.call-update) | async-done | bytes 8388624 | tf_op jit(solution)/shard_map/all_gather | solution.py:153
  132.8 11.6 %shard_map.46 = bf16[256,1024]{1,0:T(8,128)(2,1)} custom-call(s32[64]{0:T(128)} %fusion.2.rows_ref, s32[1]{0:T(128)} %bitcast.prev_ref, bf16[256,1024]{1,0:T(8,128)(2,1)} %q_ref.1, bf16[256,128]{1,0:T(8,128)(2,1)} %keys_ref.1, bf16[256,128]{1,0:T(8,128)(2,1)} %values_ref.1, s32[4,1,1408]{2,1,0:T(1,128)} %copy.17.colmask_ref, bf16[256,2,64,128]{3,2,1,0:T(8,128)(2,1)} %bitcast.13), custom_call_target="tpu_custom_call" | custom-call | flops 1476395008 | bytes 3145728 | tf_op jit(solution)/shard_map/pallas_call | solution.py:90
  144.4 14.3 %all_to_all.19 = bf16[8,32,1024]{2,1,0:T(8,128)(2,1)S(1)} all-to-all(bf16[8,32,1024]{2,1,0:T(8,128)(2,1)} %bitcast.14), channel_id=1, replica_groups=mesh['cy'=4,'cz'=16,'kvh'=8] {'kvh'}, dimensions={0} | all-to-all | bytes 1048576 | tf_op jit(solution)/shard_map/all_to_all | solution.py:156
  158.7 0.8 copy.19
  (3 shorter events, 0.0 us)
Async XLA Ops:
  6.5 126.3 %all-gather.4.cloned.1.call-start = ((), (), s32[]{:S(2)}) async-start(), calls=%async_computation.1 | async-start | bytes 8912896 | tf_op jit(solution)/shard_map/all_gather | solution.py:153
Sparse Core Ops, SparseCore 0:
  20.1 112.6 all-gather.3

commit v5 on v4

v5 whole, which is shorter than its diff:
```python
import functools

import jax
import jax.numpy as jnp
from jax import lax
from jax.experimental import pallas as pl
from jax.experimental.pallas import tpu as pltpu
from jax.sharding import Mesh
from jax.sharding import PartitionSpec as P

TILE = 64
SEL = 16
WINDOW = 256
WIN_COLS = WINDOW + 2 * TILE
SEL_COLS = SEL * TILE

masked_score = -1e30


def window_kernel(q_ref, wink_ref, winv_ref, colmask_ref, acc_ref, peak_ref, total_ref, *, per_dev, scale):
    head_size = wink_ref.shape[1]
    heads = q_ref.shape[1] // head_size
    r = lax.broadcasted_iota(jnp.int32, (TILE, WIN_COLS), 0)
    j = lax.broadcasted_iota(jnp.int32, (TILE, WIN_COLS), 1)
    in_window = (j > r) & (j <= r + WINDOW)
    dims = (((1,), (1,)), ((), ()))
    for b in range(per_dev):
        q = q_ref[pl.ds(b * TILE, TILE), :]
        qs = jnp.concatenate([q[:, h * head_size : (h + 1) * head_size] for h in range(heads)], axis=0)
        k_win = wink_ref[pl.ds(b * TILE, WIN_COLS), :]
        v_win = winv_ref[pl.ds(b * TILE, WIN_COLS), :]
        win_ok = in_window & (colmask_ref[b] > 0)
        s_win = lax.dot_general(qs, k_win, dims, preferred_element_type=jnp.float32) * scale
        s_win = jnp.where(win_ok[None], s_win.reshape(heads, TILE, WIN_COLS), masked_score)
        s_win = s_win.reshape(heads * TILE, WIN_COLS)
        peak = jnp.max(s_win, axis=1, keepdims=True)
        w_win = jnp.exp(s_win - peak)
        total_ref[b] = jnp.sum(w_win, axis=1, keepdims=True)
        peak_ref[b] = peak
        acc_ref[b] = jnp.dot(w_win.astype(jnp.bfloat16), v_win, preferred_element_type=jnp.float32)


def window_attention(queries, wink, winv, colmask, per_dev, scale):
    tok_rows, width = queries.shape
    head_size = wink.shape[1]
    rows = tok_rows * (width // head_size) // per_dev
    vmem = pltpu.MemorySpace.VMEM
    return pl.pallas_call(
        functools.partial(window_kernel, per_dev=per_dev, scale=scale),
        out_shape=(
            jax.ShapeDtypeStruct((per_dev, rows, head_size), jnp.float32),
            jax.ShapeDtypeStruct((per_dev, rows, 1), jnp.float32),
            jax.ShapeDtypeStruct((per_dev, rows, 1), jnp.float32),
        ),
        in_specs=[pl.BlockSpec(memory_space=vmem)] * 4,
        out_specs=tuple([pl.BlockSpec(memory_space=vmem)] * 3),
        cost_estimate=pl.CostEstimate(
            flops=4 * tok_rows * width * WIN_COLS,
            transcendentals=tok_rows * (width // head_size) * WIN_COLS,
            bytes_accessed=tok_rows * width * 2 + per_dev * rows * (head_size + 2) * 4,
        ),
    )(queries, wink, winv, colmask)


def attention_kernel(
    rows_ref, q_ref, colmask_ref, acc_ref, peak_ref, total_ref, tiles_hbm, out_ref, selbuf, sems, *, per_dev, scale,
):
    head_size = tiles_hbm.shape[3]
    heads = q_ref.shape[1] // head_size

    def fetch(b):
        slot = b % 2
        copies = []
        for i in range(SEL):
            cp = pltpu.make_async_copy(tiles_hbm.at[rows_ref[b * SEL + i]], selbuf.at[slot, i], sems.at[slot, i])
            cp.start()
            copies.append(cp)
        return copies

    pending = fetch(0)
    dims = (((1,), (1,)), ((), ()))
    for b in range(per_dev):
        for c in pending:
            c.wait()
        if b + 1 < per_dev:
            pending = fetch(b + 1)
        slot = b % 2
        q = q_ref[pl.ds(b * TILE, TILE), :]
        qs = jnp.concatenate([q[:, h * head_size : (h + 1) * head_size] for h in range(heads)], axis=0)
        k_sel = selbuf[slot, :, 0].reshape(SEL_COLS, head_size)
        v_sel = selbuf[slot, :, 1].reshape(SEL_COLS, head_size)
        sel_ok = colmask_ref[b] > 0
        s_sel = lax.dot_general(qs, k_sel, dims, preferred_element_type=jnp.float32) * scale
        s_sel = jnp.where(sel_ok, s_sel, masked_score)
        win_peak = peak_ref[b]
        peak = jnp.maximum(win_peak, jnp.max(s_sel, axis=1, keepdims=True))
        w_sel = jnp.exp(s_sel - peak)
        rescale = jnp.exp(win_peak - peak)
        total = total_ref[b] * rescale + jnp.sum(w_sel, axis=1, keepdims=True)
        num = acc_ref[b] * rescale
        num = num + jnp.dot(w_sel.astype(jnp.bfloat16), v_sel, preferred_element_type=jnp.float32)
        res = (num / total).astype(out_ref.dtype)
        for h in range(heads):
            out_ref[pl.ds(b * TILE, TILE), h * head_size : (h + 1) * head_size] = res[h * TILE : (h + 1) * TILE]


def block_attention(rows, queries, colmask, acc, peak, total, tiles, per_dev, scale):
    tok_rows, width = queries.shape
    head_size = tiles.shape[3]
    vmem = pltpu.MemorySpace.VMEM
    smem = pltpu.MemorySpace.SMEM
    return pl.pallas_call(
        functools.partial(attention_kernel, per_dev=per_dev, scale=scale),
        out_shape=jax.ShapeDtypeStruct((tok_rows, width), queries.dtype),
        in_specs=[pl.BlockSpec(memory_space=smem)]
        + [pl.BlockSpec(memory_space=vmem)] * 5
        + [pl.BlockSpec(memory_space=pl.ANY)],
        out_specs=pl.BlockSpec(memory_space=vmem),
        scratch_shapes=[
            pltpu.VMEM((2, SEL, 2, TILE, head_size), tiles.dtype),
            pltpu.SemaphoreType.DMA((2, SEL)),
        ],
        cost_estimate=pl.CostEstimate(
            flops=4 * tok_rows * width * SEL_COLS,
            transcendentals=tok_rows * (width // head_size) * SEL_COLS,
            bytes_accessed=2 * tok_rows * width * 2 + 2 * per_dev * SEL_COLS * head_size * 2,
        ),
    )(rows, queries, colmask, acc, peak, total, tiles)


def window_part(queries, keys, values, prev_keys, prev_values, here):
    tok_rows, head_size = keys.shape
    per_dev = tok_rows // TILE
    scale = 1.0 / head_size**0.5
    pad = jnp.zeros((TILE, head_size), keys.dtype)
    wink = jnp.concatenate([prev_keys, keys, pad], axis=0)
    winv = jnp.concatenate([prev_values, values, pad], axis=0)
    block_index = jnp.arange(per_dev, dtype=jnp.int32)
    win_col = jnp.arange(WIN_COLS, dtype=jnp.int32)
    lowest = WINDOW - here * tok_rows - block_index * TILE
    win_flags = (win_col[None, :] < WINDOW + TILE) & (win_col[None, :] >= lowest[:, None])
    win_flags = win_flags.astype(jnp.int32).reshape(per_dev, 1, WIN_COLS)
    return window_attention(queries, wink, winv, win_flags, per_dev, scale)


def selected_part(queries, lists, tiles, window, n_y, n_z):
    tok_rows, width = queries.shape
    head_size = tiles.shape[3]
    per_dev = tok_rows // TILE
    scale = 1.0 / head_size**0.5

    def tile_index(tile_id):
        owner = tile_id // per_dev
        return ((owner % n_z) * n_y + owner // n_z) * per_dev + tile_id % per_dev

    rows = tile_index(jnp.maximum(lists, 0)).reshape(-1).astype(jnp.int32)
    sel_flags = jnp.repeat(lists >= 0, TILE, axis=1).astype(jnp.int32).reshape(per_dev, 1, SEL_COLS)
    acc, peak, total = window
    return block_attention(rows, queries, sel_flags, acc, peak, total, tiles, per_dev, scale)


def per_device(queries, keys, values, selection):
    tok_rows, head_size = keys.shape
    per_dev = tok_rows // TILE
    n_y = lax.axis_size("cy")
    n_z = lax.axis_size("cz")
    here = lax.axis_index("cy") * n_z + lax.axis_index("cz")

    both = jnp.stack(
        [keys.reshape(per_dev, TILE, head_size), values.reshape(per_dev, TILE, head_size)], axis=1
    )
    gathered = lax.all_gather(both, "cy", axis=0, tiled=False)
    gathered = lax.all_gather(gathered, "cz", axis=0, tiled=False)
    tiles = gathered.reshape(n_z * n_y * per_dev, 2, TILE, head_size)
    count = n_y * n_z
    earlier = [(i, i + 1) for i in range(count - 1)]
    prev_keys, prev_values = lax.ppermute((keys, values), ("cy", "cz"), earlier)
    window = window_part(queries, keys, values, prev_keys, prev_values, here)
    attended = selected_part(queries, selection[0], tiles, window, n_y, n_z)
    return lax.all_to_all(attended, "kvh", split_axis=0, concat_axis=1, tiled=True)


def solution(mesh):
    devices = mesh.devices
    ctx = devices.shape[0]
    z = len({tuple(d.coords)[2] for d in devices[:, 0]})
    z = z if ctx % z == 0 else ctx
    grid = Mesh(devices.reshape(ctx // z, z, devices.shape[1]), ("cy", "cz", "kvh"))
    row = P(("cy", "cz"), "kvh")
    return jax.shard_map(
        per_device,
        mesh=grid,
        in_specs=(row, row, row, P("kvh", ("cy", "cz"), None)),
        out_specs=P(("cy", "cz", "kvh"), None),
        check_vma=False,
    )
```

time: 167 us -> 168 us (level)
  waiting for transfers between devices: 110 us -> 95.5 us
  starting transfers between devices: 0.01 us -> 7.54 us
  Pallas kernels: 11.6 us -> 16.5 us
  other arithmetic: 2.91 us -> 5.26 us
    all_gather x1, waiting for transfers between devices: 110 us -> 95.5 us  [per_device(): gathered = lax.all_gather(gathered, 'cz', axis=0, tiled=False)]
    ppermute x0 -> x2, starting transfers between devices: none -> 7.54 us  [per_device(): prev_keys, prev_values = lax.ppermute((keys, values), ('cy', 'cz'), earlier)]
    pallas_call x0 -> x1, Pallas kernels: none -> 4.36 us  [window_attention(): pl.pallas_call(functools.partial(window_kernel, per_dev=per_dev, scale=sc...]
  transfers between devices with their start and end apart: 1 -> 3, of which waited for: 1 -> 1; matrix products, arithmetic and copies ran while one was open for 2% -> 3% of each run, Pallas kernels for 0% -> 3%
where the time goes in v5:
time: 168 us; the launch traced here: 167 us
  waiting for transfers between devices  95.5 us (57%)
  blocking collectives  26.8 us (16%)
  Pallas kernels  16.5 us (10%)
  between operations  13.4 us (8%)
  starting transfers between devices  7.54 us (4%)
  other arithmetic  5.26 us (3%)
  local copies, waits for them, and re-layouts  1.86 us (1%)
    all_gather x1, waiting for transfers between devices, per_device(): gathered = lax.all_gather(gathered, 'cz', axis=0, tiled=False)  95.5 us
    all_to_all x1, blocking collectives, per_device(): lax.all_to_all(attended, 'kvh', split_axis=0, concat_axis=1, tiled=True)  14.3 us
    all_gather x1, blocking collectives, per_device(): gathered = lax.all_gather(both, 'cy', axis=0, tiled=False)  12.5 us
    pallas_call x1, Pallas kernels, block_attention(): pl.pallas_call(functools.partial(attention_kernel, per_dev=per_dev, scale...  12.2 us
    ppermute x2, starting transfers between devices, per_device(): prev_keys, prev_values = lax.ppermute((keys, values), ('cy', 'cz'), earlier)  7.54 us
    pallas_call x1, Pallas kernels, window_attention(): pl.pallas_call(functools.partial(window_kernel, per_dev=per_dev, scale=sc...  4.36 us
  transfers between devices with their start and end apart: 3, of which 1 were waited for; matrix products, arithmetic and copies ran while one was open for 3% of the time, Pallas kernels for 3%

profile of v5, /device:TPU:1, one launch (start us, length us, event | category | flops | bytes accessed | tf_op | source)
XLA Modules:
  0.0 167.0 jit_solution(16336595125423298794)
XLA Ops:
  6.5 0.0 all-gather.4.cloned.1.call-start
  6.5 0.9 pad_maximum_fusion
  7.4 12.5 %all-gather = bf16[16,2,64,128]{3,2,1,0:T(8,128)(2,1)} all-gather(bf16[4,2,64,128]{3,2,1,0:T(8,128)(2,1)S(1)} %pad_maximum_fusion), channel_id=2, replica_groups=mesh['cy'=4,'cz'=16,'kvh'=8] {'cy'}, dimensions={0}, use_global_device_ids=true | all-gather | bytes 655360 | tf_op jit(solution)/shard_map/all_gather | solution.py:172
  20.0 0.0 all-gather.4.cloned.1.call-update
  20.0 4.0 %collective-permute-start = (bf16[256,128]{1,0:T(8,128)(2,1)}, bf16[256,128]{1,0:T(8,128)(2,1)S(1)}, u32[]{:S(2)}, u32[]{:S(2)}) collective-permute-start(bf16[256,128]{1,0:T(8,128)(2,1)} %param.5), channel_id=1, source_target_pairs={{0,8},{8,16},{16,24},{24,32},{32,40},{40,48},{48,56},{56,64},{64,7... | collective-permute-start | bytes 196616 | tf_op jit(solution)/shard_map/ppermute | solution.py:177
  24.0 3.5 %collective-permute-start.1 = (bf16[256,128]{1,0:T(8,128)(2,1)}, bf16[256,128]{1,0:T(8,128)(2,1)S(1)}, u32[]{:S(2)}, u32[]{:S(2)}) collective-permute-start(bf16[256,128]{1,0:T(8,128)(2,1)} %param.6), channel_id=1, source_target_pairs={{0,8},{8,16},{16,24},{24,32},{32,40},{40,48},{48,56},{56,64},{64,7... | collective-permute-start | bytes 196616 | tf_op jit(solution)/shard_map/ppermute | solution.py:177
  27.6 0.7 convert_bitcast_fusion
  28.2 0.1 ne.46
  28.3 0.7 maximum_shift-right-logical_fusion
  29.0 0.1 div.20
  29.1 0.1 rem.40
  29.2 0.7 and_convert_fusion.colmask_ref
  29.9 0.6 fusion.rows_ref
  30.5 0.1 broadcast_in_dim.4
  30.5 0.7 convert_element_type.29.colmask_ref
  31.2 0.0 collective-permute-done
  31.2 0.0 collective-permute-done.1
  31.3 1.7 %maximum_maximum_fusion.1 = (bf16[576,128]{1,0:T(8,128)(2,1)}, bf16[576,128]{1,0:T(8,128)(2,1)}) fusion(bf16[256,128]{1,0:T(8,128)(2,1)} %param.6, bf16[256,128]{1,0:T(8,128)(2,1)S(1)} %collective-permute-done.1, bf16[576]{0:T(1024)(128)(2,1)S(1)} %pad.7.clone, bf16[256,128]{1,0:T(8,128)(2,1)} %param.5, bf16[256,128]{1,0:T(8,128)(2,1)S(1)} %collective-permute-done), kind=kLoop, calls=%fused_computation.1 | loop fusion | flops 811008 | bytes 558208 | tf_op jit(solution)/shard_map/concatenate | solution.py:137
  33.0 4.4 %shard_map.46 = (f32[4,512,128]{2,1,0:T(8,128)}, f32[4,512,1]{2,1,0:T(8,128)}, f32[4,512,1]{2,1,0:T(8,128)}) custom-call(bf16[256,1024]{1,0:T(8,128)(2,1)} %q_ref.3, bf16[576,128]{1,0:T(8,128)(2,1)} %get-tuple-element.12.wink_ref, bf16[576,128]{1,0:T(8,128)(2,1)} %get-tuple-element.11.winv_ref, s32[4,1,384]{2,1,0:T(1,128)} %and_convert_fusion.colmask_ref), custom_call_target="tpu_custom_call" | custom-call | flops 402653184 | bytes 1589248 | tf_op jit(solution)/shard_map/pallas_call | solution.py:48
  37.3 95.5 %all-gather.4.cloned.1.call-done = bf16[64,4,2,64,128]{4,3,2,1,0:T(8,128)(2,1)} async-done(((bf16[4,4,2,64,128]{4,3,2,1,0:T(8,128)(2,1)}), bf16[64,4,2,64,128]{4,3,2,1,0:T(8,128)(2,1)}) %all-gather.4.cloned.1.call-update) | async-done | bytes 8388624 | tf_op jit(solution)/shard_map/all_gather | solution.py:173
  132.8 12.2 %shard_map.47 = bf16[256,1024]{1,0:T(8,128)(2,1)} custom-call(s32[64]{0:T(128)} %fusion.rows_ref, bf16[256,1024]{1,0:T(8,128)(2,1)} %q_ref.3, s32[4,1,1024]{2,1,0:T(1,128)} %convert_element_type.29.colmask_ref, f32[4,512,128]{2,1,0:T(8,128)} %get-tuple-element.8.acc_ref, f32[4,512,1]{2,1,0:T(8,128)} %get-tuple-element.9.peak_ref, ...), custom_call_target="tpu_custom_call" | custom-call | flops 1073741824 | bytes 3145728 | tf_op jit(solution)/shard_map/pallas_call | solution.py:112
  145.0 14.3 %all_to_all.19 = bf16[8,32,1024]{2,1,0:T(8,128)(2,1)S(1)} all-to-all(bf16[8,32,1024]{2,1,0:T(8,128)(2,1)} %bitcast.11), channel_id=1, replica_groups=mesh['cy'=4,'cz'=16,'kvh'=8] {'kvh'}, dimensions={0} | all-to-all | bytes 1048576 | tf_op jit(solution)/shard_map/all_to_all | solution.py:180
  159.3 0.8 copy.11
  (4 shorter events, 0.0 us)
Async XLA Ops:
  6.5 126.3 %all-gather.4.cloned.1.call-start = ((), (), s32[]{:S(2)}) async-start(), calls=%async_computation.1 | async-start | bytes 8912896 | tf_op jit(solution)/shard_map/all_gather | solution.py:173
  20.0 11.3 %collective-permute-start = (bf16[256,128]{1,0:T(8,128)(2,1)}, bf16[256,128]{1,0:T(8,128)(2,1)S(1)}, u32[]{:S(2)}, u32[]{:S(2)}) collective-permute-start(bf16[256,128]{1,0:T(8,128)(2,1)} %param.5), channel_id=1, source_target_pairs={{0,8},{8,16},{16,24},{24,32},{32,40},{40,48},{48,56},{56,64},{64,7... | collective-permute-start | bytes 196616 | tf_op jit(solution)/shard_map/ppermute | solution.py:177
  24.0 7.3 %collective-permute-start.1 = (bf16[256,128]{1,0:T(8,128)(2,1)}, bf16[256,128]{1,0:T(8,128)(2,1)S(1)}, u32[]{:S(2)}, u32[]{:S(2)}) collective-permute-start(bf16[256,128]{1,0:T(8,128)(2,1)} %param.6), channel_id=1, source_target_pairs={{0,8},{8,16},{16,24},{24,32},{32,40},{40,48},{48,56},{56,64},{64,7... | collective-permute-start | bytes 196616 | tf_op jit(solution)/shard_map/ppermute | solution.py:177
Sparse Core Ops, SparseCore 0:
  20.1 112.6 all-gather.3

commit v6 on v4

--- a/solution.py
+++ b/solution.py
@@ -149,7 +149,8 @@
     both = jnp.stack(
         [keys.reshape(per_dev, TILE, head_size), values.reshape(per_dev, TILE, head_size)], axis=1
     )
-    gathered = lax.all_gather(both, "cy", axis=0, tiled=False)
+    copies = jnp.broadcast_to(both[None], (n_y,) + both.shape)
+    gathered = lax.all_to_all(copies, "cy", 0, 0, tiled=False)
     gathered = lax.all_gather(gathered, "cz", axis=0, tiled=False)
     tiles = gathered.reshape(n_z * n_y * per_dev, 2, TILE, head_size)
     attended = device_attention(queries, keys, values, selection[0], tiles, here, n_y, n_z)

time: 167 us -> 165 us (0.988)
  waiting for transfers between devices: 110 us -> 108 us
    all_gather x1 -> x0, blocking collectives: 12.5 us -> none  [per_device(): gathered = lax.all_gather(both, 'cy', axis=0, tiled=False)]
    all_to_all x0 -> x1, blocking collectives: none -> 11.9 us  [per_device(): gathered = lax.all_to_all(copies, 'cy', 0, 0, tiled=False)]
where the time goes in v6:
time: 165 us; the launch traced here: 164 us
  waiting for transfers between devices  108 us (65%)
  blocking collectives  26.1 us (16%)
  between operations  13.5 us (8%)
  Pallas kernels  11.6 us (7%)
  other arithmetic  2.91 us (2%)
  local copies, waits for them, and re-layouts  2 us (1%)
    all_gather x1, waiting for transfers between devices, per_device(): gathered = lax.all_gather(gathered, 'cz', axis=0, tiled=False)  108 us
    all_to_all x1, blocking collectives, per_device(): lax.all_to_all(attended, 'kvh', split_axis=0, concat_axis=1, tiled=True)  14.3 us
    all_to_all x1, blocking collectives, per_device(): gathered = lax.all_to_all(copies, 'cy', 0, 0, tiled=False)  11.9 us
    pallas_call x1, Pallas kernels, block_attention(): pl.pallas_call(functools.partial(attention_kernel, per_dev=per_dev, scale...  11.6 us
  transfers between devices with their start and end apart: 1, of which 1 were waited for; matrix products, arithmetic and copies ran while one was open for 2% of the time, Pallas kernels for 0%

profile of v6, /device:TPU:1, one launch (start us, length us, event | category | flops | bytes accessed | tf_op | source)
XLA Modules:
  0.0 164.3 jit_solution(8769861795262837232)
XLA Ops:
  6.5 0.0 all-gather.3.cloned.1.call-start
  6.5 0.9 pad_maximum_fusion
  7.4 0.1 broadcast_in_dim.5
  7.5 11.9 %all_to_all.24 = bf16[4,4,2,64,128]{4,3,2,1,0:T(8,128)(2,1)} all-to-all(bf16[4,4,2,64,128]{4,3,2,1,0:T(8,128)(2,1)S(1)} %broadcast_in_dim.5), channel_id=1, replica_groups=mesh['cy'=4,'cz'=16,'kvh'=8] {'cy'}, dimensions={0} | all-to-all | bytes 1048576 | tf_op jit(solution)/shard_map/all_to_all | solution.py:153
  19.4 0.0 all-gather.3.cloned.1.call-update
  19.5 0.7 compare_bitcast_fusion
  20.2 0.1 ne.66
  20.3 0.7 maximum_shift-right-logical_fusion
  20.9 0.1 div.35
  21.0 0.1 rem.70
  21.1 0.1 broadcast_in_dim.4
  21.2 0.1 concatenate.15
  21.3 0.1 fusion.1
  21.4 0.6 copy.17.colmask_ref
  22.0 0.5 fusion.2.rows_ref
  22.6 108.2 %all-gather.3.cloned.1.call-done = bf16[64,4,2,64,128]{4,3,2,1,0:T(8,128)(2,1)} async-done(((bf16[4,4,2,64,128]{4,3,2,1,0:T(8,128)(2,1)}), bf16[64,4,2,64,128]{4,3,2,1,0:T(8,128)(2,1)}) %all-gather.3.cloned.1.call-update) | async-done | bytes 8388624 | tf_op jit(solution)/shard_map/all_gather | solution.py:154
  130.8 11.6 %shard_map.46 = bf16[256,1024]{1,0:T(8,128)(2,1)} custom-call(s32[64]{0:T(128)} %fusion.2.rows_ref, s32[1]{0:T(128)} %bitcast.prev_ref, bf16[256,1024]{1,0:T(8,128)(2,1)} %q_ref.1, bf16[256,128]{1,0:T(8,128)(2,1)} %keys_ref.1, bf16[256,128]{1,0:T(8,128)(2,1)} %values_ref.1, s32[4,1,1408]{2,1,0:T(1,128)} %copy.17.colmask_ref, bf16[256,2,64,128]{3,2,1,0:T(8,128)(2,1)} %bitcast.16), custom_call_target="tpu_custom_call" | custom-call | flops 1476395008 | bytes 3145728 | tf_op jit(solution)/shard_map/pallas_call | solution.py:90
  142.4 14.3 %all_to_all.25 = bf16[8,32,1024]{2,1,0:T(8,128)(2,1)S(1)} all-to-all(bf16[8,32,1024]{2,1,0:T(8,128)(2,1)} %bitcast.17), channel_id=1, replica_groups=mesh['cy'=4,'cz'=16,'kvh'=8] {'kvh'}, dimensions={0} | all-to-all | bytes 1048576 | tf_op jit(solution)/shard_map/all_to_all | solution.py:157
  156.7 0.8 copy.19
  (3 shorter events, 0.0 us)
Async XLA Ops:
  6.5 124.3 %all-gather.3.cloned.1.call-start = ((), (), s32[]{:S(2)}) async-start(), calls=%async_computation.2 | async-start | bytes 8912896 | tf_op jit(solution)/shard_map/all_gather | solution.py:154
Sparse Core Ops, SparseCore 0:
  19.5 111.2 all-gather.2

commit v7 on v6

--- a/solution.py
+++ b/solution.py
@@ -18,8 +18,8 @@
 
 
 def attention_kernel(
-    rows_ref, prev_ref, q_ref, keys_ref, values_ref, colmask_ref, tiles_hbm, out_ref,
-    selbuf, prevbuf, wink, winv, sems, prev_sem, *, per_dev, scale,
+    rows_ref, ring_rows_ref, from_ring_ref, prev_ref, q_ref, keys_ref, values_ref, colmask_ref, tiles_hbm, ring_hbm,
+    out_ref, selbuf, prevbuf, wink, winv, sems, prev_sem, *, per_dev, scale,
 ):
     head_size = keys_ref.shape[1]
     tok_rows = keys_ref.shape[0]
@@ -29,13 +29,18 @@
         slot = b % 2
         copies = []
         for i in range(SEL):
-            cp = pltpu.make_async_copy(tiles_hbm.at[rows_ref[b * SEL + i]], selbuf.at[slot, i], sems.at[slot, i])
-            cp.start()
+            k = b * SEL + i
+            cp = pltpu.make_async_copy(tiles_hbm.at[rows_ref[k]], selbuf.at[slot, i], sems.at[slot, i])
+            cr = pltpu.make_async_copy(ring_hbm.at[ring_rows_ref[k]], selbuf.at[slot, i], sems.at[slot, i])
+            pl.when(from_ring_ref[k] == 0)(cp.start)
+            pl.when(from_ring_ref[k] != 0)(cr.start)
             copies.append(cp)
         return copies
 
     prev_copy = pltpu.make_async_copy(tiles_hbm.at[pl.ds(prev_ref[0], per_dev)], prevbuf, prev_sem.at[0])
-    prev_copy.start()
+    prev_ring = pltpu.make_async_copy(ring_hbm.at[pl.ds(prev_ref[1], per_dev)], prevbuf, prev_sem.at[0])
+    pl.when(prev_ref[2] == 0)(prev_copy.start)
+    pl.when(prev_ref[2] != 0)(prev_ring.start)
     pending = fetch(0)
     wink[pl.ds(tok_rows, tok_rows), :] = keys_ref[...]
     winv[pl.ds(tok_rows, tok_rows), :] = values_ref[...]
@@ -81,7 +86,7 @@
             out_ref[pl.ds(b * TILE, TILE), h * head_size : (h + 1) * head_size] = res[h * TILE : (h + 1) * TILE]
 
 
-def block_attention(rows, prev, queries, keys, values, colmask, tiles, per_dev, scale):
+def block_attention(rows, ring_rows, from_ring, prev, queries, keys, values, colmask, tiles, ring, per_dev, scale):
     tok_rows, width = queries.shape
     head_size = keys.shape[1]
     keys_per_block = WIN_COLS + SEL_COLS
@@ -93,10 +98,13 @@
         in_specs=[
             pl.BlockSpec(memory_space=smem),
             pl.BlockSpec(memory_space=smem),
-            pl.BlockSpec(memory_space=vmem),
-            pl.BlockSpec(memory_space=vmem),
-            pl.BlockSpec(memory_space=vmem),
-            pl.BlockSpec(memory_space=vmem),
+            pl.BlockSpec(memory_space=smem),
+            pl.BlockSpec(memory_space=smem),
+            pl.BlockSpec(memory_space=vmem),
+            pl.BlockSpec(memory_space=vmem),
+            pl.BlockSpec(memory_space=vmem),
+            pl.BlockSpec(memory_space=vmem),
+            pl.BlockSpec(memory_space=pl.ANY),
             pl.BlockSpec(memory_space=pl.ANY),
         ],
         out_specs=pl.BlockSpec(memory_space=vmem),
@@ -113,21 +121,27 @@
             transcendentals=tok_rows * (width // head_size) * keys_per_block,
             bytes_accessed=2 * tok_rows * width * 2 + 2 * per_dev * SEL_COLS * head_size * 2,
         ),
-    )(rows, prev, queries, keys, values, colmask, tiles)
-
-
-def device_attention(queries, keys, values, lists, tiles, here, n_y, n_z):
+    )(rows, ring_rows, from_ring, prev, queries, keys, values, colmask, tiles, ring)
+
+
+def device_attention(queries, keys, values, lists, tiles, ring, here, n_y, n_z):
     tok_rows, head_size = keys.shape
     per_dev = tok_rows // TILE
     scale = 1.0 / head_size**0.5
-
-    def tile_index(tile_id):
+    my_z = here % n_z
+
+    def locate(tile_id):
         owner = tile_id // per_dev
-        return ((owner % n_z) * n_y + owner // n_z) * per_dev + tile_id % per_dev
+        y, z = owner // n_z, owner % n_z
+        in_ring = y == n_y - 1
+        row = ((z * (n_y - 1) + jnp.minimum(y, n_y - 2)) * per_dev + tile_id % per_dev).astype(jnp.int32)
+        ring_row = (((my_z - z) % n_z) * per_dev + tile_id % per_dev).astype(jnp.int32)
+        return row, ring_row, in_ring.astype(jnp.int32)
 
     listed = lists >= 0
-    rows = tile_index(jnp.maximum(lists, 0)).reshape(-1).astype(jnp.int32)
-    prev = tile_index(jnp.maximum(here - 1, 0) * per_dev).reshape(1).astype(jnp.int32)
+    rows, ring_rows, from_ring = (a.reshape(-1) for a in locate(jnp.maximum(lists, 0)))
+    prev_row, prev_ring_row, prev_in_ring = locate(jnp.maximum(here - 1, 0) * per_dev)
+    prev = jnp.stack([prev_row, prev_ring_row, prev_in_ring]).astype(jnp.int32)
 
     block_index = jnp.arange(per_dev, dtype=jnp.int32)
     win_col = jnp.arange(WIN_COLS, dtype=jnp.int32)
@@ -136,7 +150,9 @@
     sel_flags = jnp.repeat(listed, TILE, axis=1)
     colmask = jnp.concatenate([win_flags, sel_flags], axis=1).astype(jnp.int32)
     colmask = colmask.reshape(per_dev, 1, WIN_COLS + SEL_COLS)
-    return block_attention(rows, prev, queries, keys, values, colmask, tiles, per_dev, scale)
+    return block_attention(
+        rows, ring_rows, from_ring, prev, queries, keys, values, colmask, tiles, ring, per_dev, scale
+    )
 
 
 def per_device(queries, keys, values, selection):
@@ -151,9 +167,22 @@
     )
     copies = jnp.broadcast_to(both[None], (n_y,) + both.shape)
     gathered = lax.all_to_all(copies, "cy", 0, 0, tiled=False)
-    gathered = lax.all_gather(gathered, "cz", axis=0, tiled=False)
-    tiles = gathered.reshape(n_z * n_y * per_dev, 2, TILE, head_size)
-    attended = device_attention(queries, keys, values, selection[0], tiles, here, n_y, n_z)
+    col_last = gathered[n_y - 1]
+    gathered = lax.all_gather(gathered[: n_y - 1], "cz", axis=0, tiled=False)
+    tiles = gathered.reshape(n_z * (n_y - 1) * per_dev, 2, TILE, head_size)
+    ahead = [(i, (i + 1) % n_z) for i in range(n_z)]
+    behind = [(i, (i - 1) % n_z) for i in range(n_z)]
+    own = col_last
+    by_distance = [own] + [None] * (n_z - 1)
+    fwd = bwd = own
+    for step in range(1, n_z // 2 + 1):
+        fwd = lax.ppermute(fwd, "cz", ahead)
+        by_distance[step] = fwd
+        if step < n_z - step:
+            bwd = lax.ppermute(bwd, "cz", behind)
+            by_distance[n_z - step] = bwd
+    ring = jnp.stack(by_distance).reshape(n_z * per_dev, 2, TILE, head_size)
+    attended = device_attention(queries, keys, values, selection[0], tiles, ring, here, n_y, n_z)
     return lax.all_to_all(attended, "kvh", split_axis=0, concat_axis=1, tiled=True)
 
 

time: 165 us -> 163 us (0.988)
  waiting for transfers between devices: 108 us -> 50.5 us
  starting transfers between devices: 0.01 us -> 53.8 us
    all_gather x1, waiting for transfers between devices: 108 us -> 19.5 us  [per_device(): gathered = lax.all_gather(gathered[:n_y - 1], 'cz', axis=0, tiled=False)]
    ppermute x0 -> x15, starting transfers between devices: none -> 53.8 us  [the longest x7 35.3 us: per_device(): bwd = lax.ppermute(bwd, 'cz', behind)]
    ppermute x0 -> x15, waiting for transfers between devices: none -> 31 us  [the longest x8 27.5 us: per_device(): fwd = lax.ppermute(fwd, 'cz', ahead)]
  transfers between devices with their start and end apart: 1 -> 16, of which waited for: 1 -> 10; matrix products, arithmetic and copies ran while one was open for 2% -> 2% of each run, Pallas kernels for 0% -> 0%
where the time goes in v7:
time: 163 us; the launch traced here: 162 us
  starting transfers between devices  53.8 us (33%)
  waiting for transfers between devices  50.5 us (31%)
  blocking collectives  26.6 us (16%)
  between operations  13.8 us (8%)
  Pallas kernels  11.6 us (7%)
  local copies, waits for them, and re-layouts  3.13 us (2%)
  other arithmetic  2.87 us (2%)
    ppermute x7, starting transfers between devices, per_device(): bwd = lax.ppermute(bwd, 'cz', behind)  35.3 us
    ppermute x8, waiting for transfers between devices, per_device(): fwd = lax.ppermute(fwd, 'cz', ahead)  27.5 us
    all_gather x1, waiting for transfers between devices, per_device(): gathered = lax.all_gather(gathered[:n_y - 1], 'cz', axis=0, tiled=False)  19.5 us
    ppermute x8, starting transfers between devices, per_device(): fwd = lax.ppermute(fwd, 'cz', ahead)  18.5 us
    all_to_all x1, blocking collectives, per_device(): lax.all_to_all(attended, 'kvh', split_axis=0, concat_axis=1, tiled=True)  14.8 us
    all_to_all x1, blocking collectives, per_device(): gathered = lax.all_to_all(copies, 'cy', 0, 0, tiled=False)  11.7 us
    pallas_call x1, Pallas kernels, block_attention(): pl.pallas_call(functools.partial(attention_kernel, per_dev=per_dev, scale...  11.6 us
    ppermute x7, waiting for transfers between devices, per_device(): bwd = lax.ppermute(bwd, 'cz', behind)  3.49 us
  transfers between devices with their start and end apart: 16, of which 10 were waited for; matrix products, arithmetic and copies ran while one was open for 2% of the time, Pallas kernels for 0%

profile of v7, /device:TPU:1, one launch (start us, length us, event | category | flops | bytes accessed | tf_op | source)
XLA Modules:
  0.0 162.2 jit_solution(8514840511193546627)
XLA Ops:
  6.5 0.9 pad_maximum_fusion
  7.4 0.1 broadcast_in_dim.5
  7.6 11.7 %all_to_all.24 = bf16[4,4,2,64,128]{4,3,2,1,0:T(8,128)(2,1)S(1)} all-to-all(bf16[4,4,2,64,128]{4,3,2,1,0:T(8,128)(2,1)S(1)} %broadcast_in_dim.5), channel_id=1, replica_groups=mesh['cy'=4,'cz'=16,'kvh'=8] {'cy'}, dimensions={0} | all-to-all | bytes 1048576 | tf_op jit(solution)/shard_map/all_to_all | solution.py:169
  19.3 0.8 slice.8
  20.1 0.0 all-gather.3.cloned.1.call-update
  20.1 0.1 rem.116
  20.2 0.1 div.39
  20.3 0.1 ne.96
  20.4 0.1 broadcast_in_dim.4
  20.5 0.1 concatenate.15
  20.6 0.1 fusion.1
  20.7 0.6 compare_convert_fusion
  21.4 5.2 %collective-permute-start = (bf16[4,2,64,128]{3,2,1,0:T(8,128)(2,1)S(1)}, bf16[4,2,64,128]{3,2,1,0:T(8,128)(2,1)S(1)}, u32[]{:S(2)}, u32[]{:S(2)}) collective-permute-start(bf16[4,2,64,128]{3,2,1,0:T(8,128)(2,1)S(1)} %get-tuple-element.8), channel_id=1, source_target_pairs={{0,8},{8,16},{16,24},{24,32},{32,40},{40,48},{48,56},{56,64},{64,7... | collective-permute-start | bytes 393224 | tf_op jit(solution)/shard_map/ppermute | solution.py:179
  26.5 9.5 %collective-permute-start.8 = (bf16[4,2,64,128]{3,2,1,0:T(8,128)(2,1)S(1)}, bf16[4,2,64,128]{3,2,1,0:T(8,128)(2,1)S(1)}, u32[]{:S(2)}, u32[]{:S(2)}) collective-permute-start(bf16[4,2,64,128]{3,2,1,0:T(8,128)(2,1)S(1)} %get-tuple-element.8), channel_id=1, source_target_pairs={{0,120},{8,0},{16,8},{24,16},{32,24},{40,32},{48,40},{56,48},{64,5... | collective-permute-start | bytes 393224 | tf_op jit(solution)/shard_map/ppermute | solution.py:182
  36.0 0.6 fusion.3
  36.6 0.6 copy.17.colmask_ref
  37.3 0.7 pad_add_fusion.prev_ref
  37.9 0.0 collective-permute-done
  37.9 1.9 %collective-permute-start.1 = (bf16[4,2,64,128]{3,2,1,0:T(8,128)(2,1)S(1)}, bf16[4,2,64,128]{3,2,1,0:T(8,128)(2,1)S(1)}, u32[]{:S(2)}, u32[]{:S(2)}) collective-permute-start(bf16[4,2,64,128]{3,2,1,0:T(8,128)(2,1)S(1)} %collective-permute-done), channel_id=1, source_target_pairs={{0,8},{8,16},{16,24},{24,32},{32,40},{40,48},{48,56},{56,64},{64,7... | collective-permute-start | bytes 393224 | tf_op jit(solution)/shard_map/ppermute | solution.py:179
  39.9 0.0 collective-permute-done.8
  39.9 4.6 %collective-permute-start.9 = (bf16[4,2,64,128]{3,2,1,0:T(8,128)(2,1)S(1)}, bf16[4,2,64,128]{3,2,1,0:T(8,128)(2,1)S(1)}, u32[]{:S(2)}, u32[]{:S(2)}) collective-permute-start(bf16[4,2,64,128]{3,2,1,0:T(8,128)(2,1)S(1)} %collective-permute-done.8), channel_id=1, source_target_pairs={{0,120},{8,0},{16,8},{24,16},{32,24},{40,32},{48,40},{56,48},{64,5... | collective-permute-start | bytes 393224 | tf_op jit(solution)/shard_map/ppermute | solution.py:182
  44.5 0.4 collective-permute-done.1
  44.9 1.9 %collective-permute-start.2 = (bf16[4,2,64,128]{3,2,1,0:T(8,128)(2,1)S(1)}, bf16[4,2,64,128]{3,2,1,0:T(8,128)(2,1)S(1)}, u32[]{:S(2)}, u32[]{:S(2)}) collective-permute-start(bf16[4,2,64,128]{3,2,1,0:T(8,128)(2,1)S(1)} %collective-permute-done.1), channel_id=1, source_target_pairs={{0,8},{8,16},{16,24},{24,32},{32,40},{40,48},{48,56},{56,64},{64,7... | collective-permute-start | bytes 393224 | tf_op jit(solution)/shard_map/ppermute | solution.py:179
  46.8 2.3 %collective-permute-done.9 = bf16[4,2,64,128]{3,2,1,0:T(8,128)(2,1)S(1)} collective-permute-done((bf16[4,2,64,128]{3,2,1,0:T(8,128)(2,1)S(1)}, bf16[4,2,64,128]{3,2,1,0:T(8,128)(2,1)S(1)}, u32[]{:S(2)}, u32[]{:S(2)}) %collective-permute-start.9) | collective-permute-done | bytes 131104 | tf_op jit(solution)/shard_map/ppermute | solution.py:182
  49.1 3.6 %collective-permute-start.10 = (bf16[4,2,64,128]{3,2,1,0:T(8,128)(2,1)S(1)}, bf16[4,2,64,128]{3,2,1,0:T(8,128)(2,1)S(1)}, u32[]{:S(2)}, u32[]{:S(2)}) collective-permute-start(bf16[4,2,64,128]{3,2,1,0:T(8,128)(2,1)S(1)} %collective-permute-done.9), channel_id=1, source_target_pairs={{0,120},{8,0},{16,8},{24,16},{32,24},{40,32},{48,40},{56,48},{64,5... | collective-permute-start | bytes 393224 | tf_op jit(solution)/shard_map/ppermute | solution.py:182
  52.7 2.3 %collective-permute-done.2 = bf16[4,2,64,128]{3,2,1,0:T(8,128)(2,1)S(1)} collective-permute-done((bf16[4,2,64,128]{3,2,1,0:T(8,128)(2,1)S(1)}, bf16[4,2,64,128]{3,2,1,0:T(8,128)(2,1)S(1)}, u32[]{:S(2)}, u32[]{:S(2)}) %collective-permute-start.2) | collective-permute-done | bytes 131104 | tf_op jit(solution)/shard_map/ppermute | solution.py:179
  54.9 1.9 %collective-permute-start.3 = (bf16[4,2,64,128]{3,2,1,0:T(8,128)(2,1)S(1)}, bf16[4,2,64,128]{3,2,1,0:T(8,128)(2,1)S(1)}, u32[]{:S(2)}, u32[]{:S(2)}) collective-permute-start(bf16[4,2,64,128]{3,2,1,0:T(8,128)(2,1)S(1)} %collective-permute-done.2), channel_id=1, source_target_pairs={{0,8},{8,16},{16,24},{24,32},{32,40},{40,48},{48,56},{56,64},{64,7... | collective-permute-start | bytes 393224 | tf_op jit(solution)/shard_map/ppermute | solution.py:179
  56.9 1.2 collective-permute-done.10
  58.1 3.9 %collective-permute-start.11 = (bf16[4,2,64,128]{3,2,1,0:T(8,128)(2,1)S(1)}, bf16[4,2,64,128]{3,2,1,0:T(8,128)(2,1)S(1)}, u32[]{:S(2)}, u32[]{:S(2)}) collective-permute-start(bf16[4,2,64,128]{3,2,1,0:T(8,128)(2,1)S(1)} %collective-permute-done.10), channel_id=1, source_target_pairs={{0,120},{8,0},{16,8},{24,16},{32,24},{40,32},{48,40},{56,48},{64,5... | collective-permute-start | bytes 393224 | tf_op jit(solution)/shard_map/ppermute | solution.py:182
  62.0 3.2 %collective-permute-done.3 = bf16[4,2,64,128]{3,2,1,0:T(8,128)(2,1)S(1)} collective-permute-done((bf16[4,2,64,128]{3,2,1,0:T(8,128)(2,1)S(1)}, bf16[4,2,64,128]{3,2,1,0:T(8,128)(2,1)S(1)}, u32[]{:S(2)}, u32[]{:S(2)}) %collective-permute-start.3) | collective-permute-done | bytes 131104 | tf_op jit(solution)/shard_map/ppermute | solution.py:179
  65.1 1.9 %collective-permute-start.4 = (bf16[4,2,64,128]{3,2,1,0:T(8,128)(2,1)S(1)}, bf16[4,2,64,128]{3,2,1,0:T(8,128)(2,1)S(1)}, u32[]{:S(2)}, u32[]{:S(2)}) collective-permute-start(bf16[4,2,64,128]{3,2,1,0:T(8,128)(2,1)S(1)} %collective-permute-done.3), channel_id=1, source_target_pairs={{0,8},{8,16},{16,24},{24,32},{32,40},{40,48},{48,56},{56,64},{64,7... | collective-permute-start | bytes 393224 | tf_op jit(solution)/shard_map/ppermute | solution.py:179
  67.0 0.0 collective-permute-done.11
  67.0 4.6 %collective-permute-start.12 = (bf16[4,2,64,128]{3,2,1,0:T(8,128)(2,1)S(1)}, bf16[4,2,64,128]{3,2,1,0:T(8,128)(2,1)S(1)}, u32[]{:S(2)}, u32[]{:S(2)}) collective-permute-start(bf16[4,2,64,128]{3,2,1,0:T(8,128)(2,1)S(1)} %collective-permute-done.11), channel_id=1, source_target_pairs={{0,120},{8,0},{16,8},{24,16},{32,24},{40,32},{48,40},{56,48},{64,5... | collective-permute-start | bytes 393224 | tf_op jit(solution)/shard_map/ppermute | solution.py:182
  71.7 3.8 %collective-permute-done.4 = bf16[4,2,64,128]{3,2,1,0:T(8,128)(2,1)S(1)} collective-permute-done((bf16[4,2,64,128]{3,2,1,0:T(8,128)(2,1)S(1)}, bf16[4,2,64,128]{3,2,1,0:T(8,128)(2,1)S(1)}, u32[]{:S(2)}, u32[]{:S(2)}) %collective-permute-start.4) | collective-permute-done | bytes 131104 | tf_op jit(solution)/shard_map/ppermute | solution.py:179
  75.6 1.9 %collective-permute-start.5 = (bf16[4,2,64,128]{3,2,1,0:T(8,128)(2,1)S(1)}, bf16[4,2,64,128]{3,2,1,0:T(8,128)(2,1)S(1)}, u32[]{:S(2)}, u32[]{:S(2)}) collective-permute-start(bf16[4,2,64,128]{3,2,1,0:T(8,128)(2,1)S(1)} %collective-permute-done.4), channel_id=1, source_target_pairs={{0,8},{8,16},{16,24},{24,32},{32,40},{40,48},{48,56},{56,64},{64,7... | collective-permute-start | bytes 393224 | tf_op jit(solution)/shard_map/ppermute | solution.py:179
  77.5 0.0 collective-permute-done.12
  77.5 4.6 %collective-permute-start.13 = (bf16[4,2,64,128]{3,2,1,0:T(8,128)(2,1)S(1)}, bf16[4,2,64,128]{3,2,1,0:T(8,128)(2,1)S(1)}, u32[]{:S(2)}, u32[]{:S(2)}) collective-permute-start(bf16[4,2,64,128]{3,2,1,0:T(8,128)(2,1)S(1)} %collective-permute-done.12), channel_id=1, source_target_pairs={{0,120},{8,0},{16,8},{24,16},{32,24},{40,32},{48,40},{56,48},{64,5... | collective-permute-start | bytes 393224 | tf_op jit(solution)/shard_map/ppermute | solution.py:182
  82.1 4.2 %collective-permute-done.5 = bf16[4,2,64,128]{3,2,1,0:T(8,128)(2,1)S(1)} collective-permute-done((bf16[4,2,64,128]{3,2,1,0:T(8,128)(2,1)S(1)}, bf16[4,2,64,128]{3,2,1,0:T(8,128)(2,1)S(1)}, u32[]{:S(2)}, u32[]{:S(2)}) %collective-permute-start.5) | collective-permute-done | bytes 131104 | tf_op jit(solution)/shard_map/ppermute | solution.py:179
  86.2 1.9 %collective-permute-start.6 = (bf16[4,2,64,128]{3,2,1,0:T(8,128)(2,1)S(1)}, bf16[4,2,64,128]{3,2,1,0:T(8,128)(2,1)S(1)}, u32[]{:S(2)}, u32[]{:S(2)}) collective-permute-start(bf16[4,2,64,128]{3,2,1,0:T(8,128)(2,1)S(1)} %collective-permute-done.5), channel_id=1, source_target_pairs={{0,8},{8,16},{16,24},{24,32},{32,40},{40,48},{48,56},{56,64},{64,7... | collective-permute-start | bytes 393224 | tf_op jit(solution)/shard_map/ppermute | solution.py:179
  88.2 0.0 collective-permute-done.13
  88.2 4.6 %collective-permute-start.14 = (bf16[4,2,64,128]{3,2,1,0:T(8,128)(2,1)S(1)}, bf16[4,2,64,128]{3,2,1,0:T(8,128)(2,1)S(1)}, u32[]{:S(2)}, u32[]{:S(2)}) collective-permute-start(bf16[4,2,64,128]{3,2,1,0:T(8,128)(2,1)S(1)} %collective-permute-done.13), channel_id=1, source_target_pairs={{0,120},{8,0},{16,8},{24,16},{32,24},{40,32},{48,40},{56,48},{64,5... | collective-permute-start | bytes 393224 | tf_op jit(solution)/shard_map/ppermute | solution.py:182
  92.8 4.4 %collective-permute-done.6 = bf16[4,2,64,128]{3,2,1,0:T(8,128)(2,1)S(1)} collective-permute-done((bf16[4,2,64,128]{3,2,1,0:T(8,128)(2,1)S(1)}, bf16[4,2,64,128]{3,2,1,0:T(8,128)(2,1)S(1)}, u32[]{:S(2)}, u32[]{:S(2)}) %collective-permute-start.6) | collective-permute-done | bytes 131104 | tf_op jit(solution)/shard_map/ppermute | solution.py:179
  97.2 1.9 %collective-permute-start.7 = (bf16[4,2,64,128]{3,2,1,0:T(8,128)(2,1)S(1)}, bf16[4,2,64,128]{3,2,1,0:T(8,128)(2,1)S(1)}, u32[]{:S(2)}, u32[]{:S(2)}) collective-permute-start(bf16[4,2,64,128]{3,2,1,0:T(8,128)(2,1)S(1)} %collective-permute-done.6), channel_id=1, source_target_pairs={{0,8},{8,16},{16,24},{24,32},{32,40},{40,48},{48,56},{56,64},{64,7... | collective-permute-start | bytes 393224 | tf_op jit(solution)/shard_map/ppermute | solution.py:179
  99.1 9.2 %collective-permute-done.7 = bf16[4,2,64,128]{3,2,1,0:T(8,128)(2,1)S(1)} collective-permute-done((bf16[4,2,64,128]{3,2,1,0:T(8,128)(2,1)S(1)}, bf16[4,2,64,128]{3,2,1,0:T(8,128)(2,1)S(1)}, u32[]{:S(2)}, u32[]{:S(2)}) %collective-permute-start.7) | collective-permute-done | bytes 131104 | tf_op jit(solution)/shard_map/ppermute | solution.py:179
  108.6 19.5 %all-gather.3.cloned.1.call-done = bf16[48,4,2,64,128]{4,3,2,1,0:T(8,128)(2,1)} async-done(((bf16[3,4,2,64,128]{4,3,2,1,0:T(8,128)(2,1)}), bf16[48,4,2,64,128]{4,3,2,1,0:T(8,128)(2,1)}) %all-gather.3.cloned.1.call-update) | async-done | bytes 6291472 | tf_op jit(solution)/shard_map/all_gather | solution.py:171
  128.2 11.6 %shard_map.46 = bf16[256,1024]{1,0:T(8,128)(2,1)} custom-call(s32[64]{0:T(128)} %get-tuple-element.15.rows_ref, s32[64]{0:T(128)} %get-tuple-element.14.ring_rows_ref, s32[64]{0:T(128)} %get-tuple-element.5.from_ring_ref, s32[3]{0:T(128)} %pad_add_fusion.prev_ref, bf16[256,1024]{1,0:T(8,128)(2,1)} %q_ref.1, bf16[256,128]{1,0:T(8,128)(2,1)} %keys_ref.1, ...), custom_call_target="tpu_custom_call" | custom-call | flops 1476395008 | bytes 3145728 | tf_op jit(solution)/shard_map/pallas_call | solution.py:95
  139.7 14.8 %all_to_all.25 = bf16[8,32,1024]{2,1,0:T(8,128)(2,1)S(1)} all-to-all(bf16[8,32,1024]{2,1,0:T(8,128)(2,1)} %bitcast.54), channel_id=1, replica_groups=mesh['cy'=4,'cz'=16,'kvh'=8] {'kvh'}, dimensions={0} | all-to-all | bytes 1048576 | tf_op jit(solution)/shard_map/all_to_all | solution.py:186
  154.6 0.8 copy.19
  (27 shorter events, 0.4 us)
Async XLA Ops:
  6.5 13.6 %copy-start.1 = (s32[1,4,16]{2,1,0:T(4,128)S(1)}, s32[1,4,16]{2,1,0:T(4,128)}, u32[]{:S(2)}) copy-start(s32[1,4,16]{2,1,0:T(4,128)} %param.7) | copy-start | bytes 772
  6.5 121.6 %all-gather.3.cloned.1.call-start = ((), (), s32[]{:S(2)}) async-start(), calls=%async_computation.2 | async-start | bytes 6684672 | tf_op jit(solution)/shard_map/all_gather | solution.py:171
  21.4 16.6 %collective-permute-start = (bf16[4,2,64,128]{3,2,1,0:T(8,128)(2,1)S(1)}, bf16[4,2,64,128]{3,2,1,0:T(8,128)(2,1)S(1)}, u32[]{:S(2)}, u32[]{:S(2)}) collective-permute-start(bf16[4,2,64,128]{3,2,1,0:T(8,128)(2,1)S(1)} %get-tuple-element.8), channel_id=1, source_target_pairs={{0,8},{8,16},{16,24},{24,32},{32,40},{40,48},{48,56},{56,64},{64,7... | collective-permute-start | bytes 393224 | tf_op jit(solution)/shard_map/ppermute | solution.py:179
  26.5 13.3 %collective-permute-start.8 = (bf16[4,2,64,128]{3,2,1,0:T(8,128)(2,1)S(1)}, bf16[4,2,64,128]{3,2,1,0:T(8,128)(2,1)S(1)}, u32[]{:S(2)}, u32[]{:S(2)}) collective-permute-start(bf16[4,2,64,128]{3,2,1,0:T(8,128)(2,1)S(1)} %get-tuple-element.8), channel_id=1, source_target_pairs={{0,120},{8,0},{16,8},{24,16},{32,24},{40,32},{48,40},{56,48},{64,5... | collective-permute-start | bytes 393224 | tf_op jit(solution)/shard_map/ppermute | solution.py:182
  37.9 6.9 %collective-permute-start.1 = (bf16[4,2,64,128]{3,2,1,0:T(8,128)(2,1)S(1)}, bf16[4,2,64,128]{3,2,1,0:T(8,128)(2,1)S(1)}, u32[]{:S(2)}, u32[]{:S(2)}) collective-permute-start(bf16[4,2,64,128]{3,2,1,0:T(8,128)(2,1)S(1)} %collective-permute-done), channel_id=1, source_target_pairs={{0,8},{8,16},{16,24},{24,32},{32,40},{40,48},{48,56},{56,64},{64,7... | collective-permute-start | bytes 393224 | tf_op jit(solution)/shard_map/ppermute | solution.py:179
  39.9 9.2 %collective-permute-start.9 = (bf16[4,2,64,128]{3,2,1,0:T(8,128)(2,1)S(1)}, bf16[4,2,64,128]{3,2,1,0:T(8,128)(2,1)S(1)}, u32[]{:S(2)}, u32[]{:S(2)}) collective-permute-start(bf16[4,2,64,128]{3,2,1,0:T(8,128)(2,1)S(1)} %collective-permute-done.8), channel_id=1, source_target_pairs={{0,120},{8,0},{16,8},{24,16},{32,24},{40,32},{48,40},{56,48},{64,5... | collective-permute-start | bytes 393224 | tf_op jit(solution)/shard_map/ppermute | solution.py:182
  44.9 10.1 %collective-permute-start.2 = (bf16[4,2,64,128]{3,2,1,0:T(8,128)(2,1)S(1)}, bf16[4,2,64,128]{3,2,1,0:T(8,128)(2,1)S(1)}, u32[]{:S(2)}, u32[]{:S(2)}) collective-permute-start(bf16[4,2,64,128]{3,2,1,0:T(8,128)(2,1)S(1)} %collective-permute-done.1), channel_id=1, source_target_pairs={{0,8},{8,16},{16,24},{24,32},{32,40},{40,48},{48,56},{56,64},{64,7... | collective-permute-start | bytes 393224 | tf_op jit(solution)/shard_map/ppermute | solution.py:179
  49.1 9.0 %collective-permute-start.10 = (bf16[4,2,64,128]{3,2,1,0:T(8,128)(2,1)S(1)}, bf16[4,2,64,128]{3,2,1,0:T(8,128)(2,1)S(1)}, u32[]{:S(2)}, u32[]{:S(2)}) collective-permute-start(bf16[4,2,64,128]{3,2,1,0:T(8,128)(2,1)S(1)} %collective-permute-done.9), channel_id=1, source_target_pairs={{0,120},{8,0},{16,8},{24,16},{32,24},{40,32},{48,40},{56,48},{64,5... | collective-permute-start | bytes 393224 | tf_op jit(solution)/shard_map/ppermute | solution.py:182
  54.9 10.2 %collective-permute-start.3 = (bf16[4,2,64,128]{3,2,1,0:T(8,128)(2,1)S(1)}, bf16[4,2,64,128]{3,2,1,0:T(8,128)(2,1)S(1)}, u32[]{:S(2)}, u32[]{:S(2)}) collective-permute-start(bf16[4,2,64,128]{3,2,1,0:T(8,128)(2,1)S(1)} %collective-permute-done.2), channel_id=1, source_target_pairs={{0,8},{8,16},{16,24},{24,32},{32,40},{40,48},{48,56},{56,64},{64,7... | collective-permute-start | bytes 393224 | tf_op jit(solution)/shard_map/ppermute | solution.py:179
  58.1 9.0 %collective-permute-start.11 = (bf16[4,2,64,128]{3,2,1,0:T(8,128)(2,1)S(1)}, bf16[4,2,64,128]{3,2,1,0:T(8,128)(2,1)S(1)}, u32[]{:S(2)}, u32[]{:S(2)}) collective-permute-start(bf16[4,2,64,128]{3,2,1,0:T(8,128)(2,1)S(1)} %collective-permute-done.10), channel_id=1, source_target_pairs={{0,120},{8,0},{16,8},{24,16},{32,24},{40,32},{48,40},{56,48},{64,5... | collective-permute-start | bytes 393224 | tf_op jit(solution)/shard_map/ppermute | solution.py:182
  65.1 10.4 %collective-permute-start.4 = (bf16[4,2,64,128]{3,2,1,0:T(8,128)(2,1)S(1)}, bf16[4,2,64,128]{3,2,1,0:T(8,128)(2,1)S(1)}, u32[]{:S(2)}, u32[]{:S(2)}) collective-permute-start(bf16[4,2,64,128]{3,2,1,0:T(8,128)(2,1)S(1)} %collective-permute-done.3), channel_id=1, source_target_pairs={{0,8},{8,16},{16,24},{24,32},{32,40},{40,48},{48,56},{56,64},{64,7... | collective-permute-start | bytes 393224 | tf_op jit(solution)/shard_map/ppermute | solution.py:179
  67.0 10.4 %collective-permute-start.12 = (bf16[4,2,64,128]{3,2,1,0:T(8,128)(2,1)S(1)}, bf16[4,2,64,128]{3,2,1,0:T(8,128)(2,1)S(1)}, u32[]{:S(2)}, u32[]{:S(2)}) collective-permute-start(bf16[4,2,64,128]{3,2,1,0:T(8,128)(2,1)S(1)} %collective-permute-done.11), channel_id=1, source_target_pairs={{0,120},{8,0},{16,8},{24,16},{32,24},{40,32},{48,40},{56,48},{64,5... | collective-permute-start | bytes 393224 | tf_op jit(solution)/shard_map/ppermute | solution.py:182
  75.6 10.7 %collective-permute-start.5 = (bf16[4,2,64,128]{3,2,1,0:T(8,128)(2,1)S(1)}, bf16[4,2,64,128]{3,2,1,0:T(8,128)(2,1)S(1)}, u32[]{:S(2)}, u32[]{:S(2)}) collective-permute-start(bf16[4,2,64,128]{3,2,1,0:T(8,128)(2,1)S(1)} %collective-permute-done.4), channel_id=1, source_target_pairs={{0,8},{8,16},{16,24},{24,32},{32,40},{40,48},{48,56},{56,64},{64,7... | collective-permute-start | bytes 393224 | tf_op jit(solution)/shard_map/ppermute | solution.py:179
  77.5 10.7 %collective-permute-start.13 = (bf16[4,2,64,128]{3,2,1,0:T(8,128)(2,1)S(1)}, bf16[4,2,64,128]{3,2,1,0:T(8,128)(2,1)S(1)}, u32[]{:S(2)}, u32[]{:S(2)}) collective-permute-start(bf16[4,2,64,128]{3,2,1,0:T(8,128)(2,1)S(1)} %collective-permute-done.12), channel_id=1, source_target_pairs={{0,120},{8,0},{16,8},{24,16},{32,24},{40,32},{48,40},{56,48},{64,5... | collective-permute-start | bytes 393224 | tf_op jit(solution)/shard_map/ppermute | solution.py:182
  86.2 10.9 %collective-permute-start.6 = (bf16[4,2,64,128]{3,2,1,0:T(8,128)(2,1)S(1)}, bf16[4,2,64,128]{3,2,1,0:T(8,128)(2,1)S(1)}, u32[]{:S(2)}, u32[]{:S(2)}) collective-permute-start(bf16[4,2,64,128]{3,2,1,0:T(8,128)(2,1)S(1)} %collective-permute-done.5), channel_id=1, source_target_pairs={{0,8},{8,16},{16,24},{24,32},{32,40},{40,48},{48,56},{56,64},{64,7... | collective-permute-start | bytes 393224 | tf_op jit(solution)/shard_map/ppermute | solution.py:179
  88.2 20.2 %collective-permute-start.14 = (bf16[4,2,64,128]{3,2,1,0:T(8,128)(2,1)S(1)}, bf16[4,2,64,128]{3,2,1,0:T(8,128)(2,1)S(1)}, u32[]{:S(2)}, u32[]{:S(2)}) collective-permute-start(bf16[4,2,64,128]{3,2,1,0:T(8,128)(2,1)S(1)} %collective-permute-done.13), channel_id=1, source_target_pairs={{0,120},{8,0},{16,8},{24,16},{32,24},{40,32},{48,40},{56,48},{64,5... | collective-permute-start | bytes 393224 | tf_op jit(solution)/shard_map/ppermute | solution.py:182
  97.2 11.2 %collective-permute-start.7 = (bf16[4,2,64,128]{3,2,1,0:T(8,128)(2,1)S(1)}, bf16[4,2,64,128]{3,2,1,0:T(8,128)(2,1)S(1)}, u32[]{:S(2)}, u32[]{:S(2)}) collective-permute-start(bf16[4,2,64,128]{3,2,1,0:T(8,128)(2,1)S(1)} %collective-permute-done.6), channel_id=1, source_target_pairs={{0,8},{8,16},{16,24},{24,32},{32,40},{40,48},{48,56},{56,64},{64,7... | collective-permute-start | bytes 393224 | tf_op jit(solution)/shard_map/ppermute | solution.py:179
  108.6 19.6 %copy-start = (bf16[16,4,2,64,128]{4,3,2,1,0:T(8,128)(2,1)}, bf16[16,4,2,64,128]{4,3,2,1,0:T(8,128)(2,1)S(1)}, u32[]{:S(2)}) copy-start(bf16[16,4,2,64,128]{4,3,2,1,0:T(8,128)(2,1)S(1)} %bitcast_dynamic-update-slice_fusion) | copy-start | bytes 6291460
Sparse Core Ops, SparseCore 0:
  20.2 107.8 all-gather.2

commit v8 on v7

--- a/solution.py
+++ b/solution.py
@@ -12,6 +12,7 @@
 SEL = 16
 WINDOW = 256
 WIN_COLS = WINDOW + 2 * TILE
+RING_ROWS = 2
 SEL_COLS = SEL * TILE
 
 masked_score = -1e30
@@ -133,9 +134,10 @@
     def locate(tile_id):
         owner = tile_id // per_dev
         y, z = owner // n_z, owner % n_z
-        in_ring = y == n_y - 1
-        row = ((z * (n_y - 1) + jnp.minimum(y, n_y - 2)) * per_dev + tile_id % per_dev).astype(jnp.int32)
-        ring_row = (((my_z - z) % n_z) * per_dev + tile_id % per_dev).astype(jnp.int32)
+        in_ring = y >= n_y - RING_ROWS
+        row = ((z * (n_y - RING_ROWS) + jnp.minimum(y, n_y - RING_ROWS - 1)) * per_dev + tile_id % per_dev)
+        ring_row = (((my_z - z) % n_z) * RING_ROWS + jnp.maximum(y - (n_y - RING_ROWS), 0)) * per_dev
+        row, ring_row = row.astype(jnp.int32), (ring_row + tile_id % per_dev).astype(jnp.int32)
         return row, ring_row, in_ring.astype(jnp.int32)
 
     listed = lists >= 0
@@ -167,9 +169,9 @@
     )
     copies = jnp.broadcast_to(both[None], (n_y,) + both.shape)
     gathered = lax.all_to_all(copies, "cy", 0, 0, tiled=False)
-    col_last = gathered[n_y - 1]
-    gathered = lax.all_gather(gathered[: n_y - 1], "cz", axis=0, tiled=False)
-    tiles = gathered.reshape(n_z * (n_y - 1) * per_dev, 2, TILE, head_size)
+    col_last = gathered[n_y - RING_ROWS :]
+    gathered_rest = lax.all_gather(gathered[: n_y - RING_ROWS], "cz", axis=0, tiled=False)
+    tiles = gathered_rest.reshape(n_z * (n_y - RING_ROWS) * per_dev, 2, TILE, head_size)
     ahead = [(i, (i + 1) % n_z) for i in range(n_z)]
     behind = [(i, (i - 1) % n_z) for i in range(n_z)]
     own = col_last
@@ -181,7 +183,7 @@
         if step < n_z - step:
             bwd = lax.ppermute(bwd, "cz", behind)
             by_distance[n_z - step] = bwd
-    ring = jnp.stack(by_distance).reshape(n_z * per_dev, 2, TILE, head_size)
+    ring = jnp.stack(by_distance).reshape(n_z * RING_ROWS * per_dev, 2, TILE, head_size)
     attended = device_attention(queries, keys, values, selection[0], tiles, ring, here, n_y, n_z)
     return lax.all_to_all(attended, "kvh", split_axis=0, concat_axis=1, tiled=True)
 

time: 163 us -> 178 us (1.092)
  local copies, waits for them, and re-layouts: 3.13 us -> 14.5 us
  blocking collectives: 26.6 us -> 34.7 us
  waiting for transfers between devices: 50.5 us -> 47.5 us
  starting transfers between devices: 53.8 us -> 51.1 us
    all_gather x1, waiting for transfers between devices: 19.5 us -> 0.01 us  [per_device(): lax.all_gather(gathered[:n_y - RING_ROWS], 'cz', axis=0, tiled=False)]
    unnamed x18 -> x15, local copies, waits for them, and re-layouts: 0.29 us -> 11 us
    ppermute x8, waiting for transfers between devices: 27.5 us -> 35.9 us  [per_device(): fwd = lax.ppermute(fwd, 'cz', ahead)]
    all_to_all x1, blocking collectives: 14.8 us -> 23 us  [per_device(): lax.all_to_all(attended, 'kvh', split_axis=0, concat_axis=1, tiled=True)]
    ppermute x7, waiting for transfers between devices: 3.49 us -> 11.6 us  [per_device(): bwd = lax.ppermute(bwd, 'cz', behind)]
    ppermute x7, starting transfers between devices: 35.3 us -> 31.3 us  [per_device(): bwd = lax.ppermute(bwd, 'cz', behind)]
  transfers between devices with their start and end apart: 16 -> 16, of which waited for: 10 -> 14; matrix products, arithmetic and copies ran while one was open for 2% -> 9% of each run, Pallas kernels for 0% -> 0%
where the time goes in v8:
time: 178 us; the launch traced here: 177 us
  starting transfers between devices  51.1 us (29%)
  waiting for transfers between devices  47.5 us (27%)
  blocking collectives  34.7 us (19%)
  local copies, waits for them, and re-layouts  14.5 us (8%)
  between operations  13.6 us (8%)
  Pallas kernels  11.6 us (7%)
  other arithmetic  4.15 us (2%)
    ppermute x8, waiting for transfers between devices, per_device(): fwd = lax.ppermute(fwd, 'cz', ahead)  35.9 us
    ppermute x7, starting transfers between devices, per_device(): bwd = lax.ppermute(bwd, 'cz', behind)  31.3 us
    all_to_all x1, blocking collectives, per_device(): lax.all_to_all(attended, 'kvh', split_axis=0, concat_axis=1, tiled=True)  23 us
    ppermute x8, starting transfers between devices, per_device(): fwd = lax.ppermute(fwd, 'cz', ahead)  19.8 us
    all_to_all x1, blocking collectives, per_device(): gathered = lax.all_to_all(copies, 'cy', 0, 0, tiled=False)  11.7 us
    pallas_call x1, Pallas kernels, block_attention(): pl.pallas_call(functools.partial(attention_kernel, per_dev=per_dev, scale...  11.6 us
    ppermute x7, waiting for transfers between devices, per_device(): bwd = lax.ppermute(bwd, 'cz', behind)  11.6 us
    unnamed x15, local copies, waits for them, and re-layouts  11 us
  transfers between devices with their start and end apart: 16, of which 14 were waited for; matrix products, arithmetic and copies ran while one was open for 9% of the time, Pallas kernels for 0%

profile of v8, /device:TPU:1, one launch (start us, length us, event | category | flops | bytes accessed | tf_op | source)
XLA Modules:
  0.0 177.0 jit_solution(501664297123943226)
XLA Ops:
  6.5 0.9 pad_maximum_fusion
  7.5 11.7 %all_to_all.24 = bf16[4,4,2,64,128]{4,3,2,1,0:T(8,128)(2,1)S(1)} all-to-all(bf16[4,4,2,64,128]{4,3,2,1,0:T(8,128)(2,1)S(1)} %broadcast_in_dim.5), channel_id=1, replica_groups=mesh['cy'=4,'cz'=16,'kvh'=8] {'cy'}, dimensions={0} | all-to-all | bytes 1048576 | tf_op jit(solution)/shard_map/all_to_all | solution.py:171
  19.3 0.8 fusion.5
  20.1 5.2 %collective-permute-start = (bf16[2,4,2,64,128]{4,3,2,1,0:T(8,128)(2,1)S(1)}, bf16[2,4,2,64,128]{4,3,2,1,0:T(8,128)(2,1)S(1)}, u32[]{:S(2)}, u32[]{:S(2)}) collective-permute-start(bf16[2,4,2,64,128]{4,3,2,1,0:T(8,128)(2,1)S(1)} %get-tuple-element.8), channel_id=1, source_target_pairs={{0,8},{8,16},{16,24},{24,32},{32,40},{40,48},{48,56},{56,64},{64,7... | collective-permute-start | bytes 786440 | tf_op jit(solution)/shard_map/ppermute | solution.py:181
  26.0 11.6 %collective-permute-done = bf16[2,4,2,64,128]{4,3,2,1,0:T(8,128)(2,1)S(1)} collective-permute-done((bf16[2,4,2,64,128]{4,3,2,1,0:T(8,128)(2,1)S(1)}, bf16[2,4,2,64,128]{4,3,2,1,0:T(8,128)(2,1)S(1)}, u32[]{:S(2)}, u32[]{:S(2)}) %collective-permute-start) | collective-permute-done | bytes 262176 | tf_op jit(solution)/shard_map/ppermute | solution.py:181
  37.6 1.9 %collective-permute-start.1 = (bf16[2,4,2,64,128]{4,3,2,1,0:T(8,128)(2,1)S(1)}, bf16[2,4,2,64,128]{4,3,2,1,0:T(8,128)(2,1)S(1)}, u32[]{:S(2)}, u32[]{:S(2)}) collective-permute-start(bf16[2,4,2,64,128]{4,3,2,1,0:T(8,128)(2,1)S(1)} %collective-permute-done), channel_id=1, source_target_pairs={{0,8},{8,16},{16,24},{24,32},{32,40},{40,48},{48,56},{56,64},{64,7... | collective-permute-start | bytes 786440 | tf_op jit(solution)/shard_map/ppermute | solution.py:181
  39.8 4.6 %collective-permute-start.8 = (bf16[2,4,2,64,128]{4,3,2,1,0:T(8,128)(2,1)S(1)}, bf16[2,4,2,64,128]{4,3,2,1,0:T(8,128)(2,1)S(1)}, u32[]{:S(2)}, u32[]{:S(2)}) collective-permute-start(bf16[2,4,2,64,128]{4,3,2,1,0:T(8,128)(2,1)S(1)} %get-tuple-element.8), channel_id=1, source_target_pairs={{0,120},{8,0},{16,8},{24,16},{32,24},{40,32},{48,40},{56,48},{64,5... | collective-permute-start | bytes 786440 | tf_op jit(solution)/shard_map/ppermute | solution.py:184
  44.3 1.6 collective-permute-done.1
  45.9 3.1 %collective-permute-start.2 = (bf16[2,4,2,64,128]{4,3,2,1,0:T(8,128)(2,1)S(1)}, bf16[2,4,2,64,128]{4,3,2,1,0:T(8,128)(2,1)S(1)}, u32[]{:S(2)}, u32[]{:S(2)}) collective-permute-start(bf16[2,4,2,64,128]{4,3,2,1,0:T(8,128)(2,1)S(1)} %collective-permute-done.1), channel_id=1, source_target_pairs={{0,8},{8,16},{16,24},{24,32},{32,40},{40,48},{48,56},{56,64},{64,7... | collective-permute-start | bytes 786440 | tf_op jit(solution)/shard_map/ppermute | solution.py:181
  50.0 4.4 %collective-permute-done.8 = bf16[2,4,2,64,128]{4,3,2,1,0:T(8,128)(2,1)S(1)} collective-permute-done((bf16[2,4,2,64,128]{4,3,2,1,0:T(8,128)(2,1)S(1)}, bf16[2,4,2,64,128]{4,3,2,1,0:T(8,128)(2,1)S(1)}, u32[]{:S(2)}, u32[]{:S(2)}) %collective-permute-start.8) | collective-permute-done | bytes 262176 | tf_op jit(solution)/shard_map/ppermute | solution.py:184
  54.4 1.9 %collective-permute-start.9 = (bf16[2,4,2,64,128]{4,3,2,1,0:T(8,128)(2,1)S(1)}, bf16[2,4,2,64,128]{4,3,2,1,0:T(8,128)(2,1)S(1)}, u32[]{:S(2)}, u32[]{:S(2)}) collective-permute-start(bf16[2,4,2,64,128]{4,3,2,1,0:T(8,128)(2,1)S(1)} %collective-permute-done.8), channel_id=1, source_target_pairs={{0,120},{8,0},{16,8},{24,16},{32,24},{40,32},{48,40},{56,48},{64,5... | collective-permute-start | bytes 786440 | tf_op jit(solution)/shard_map/ppermute | solution.py:184
  56.8 4.1 %collective-permute-done.2 = bf16[2,4,2,64,128]{4,3,2,1,0:T(8,128)(2,1)S(1)} collective-permute-done((bf16[2,4,2,64,128]{4,3,2,1,0:T(8,128)(2,1)S(1)}, bf16[2,4,2,64,128]{4,3,2,1,0:T(8,128)(2,1)S(1)}, u32[]{:S(2)}, u32[]{:S(2)}) %collective-permute-start.2) | collective-permute-done | bytes 262176 | tf_op jit(solution)/shard_map/ppermute | solution.py:181
  60.9 1.9 %collective-permute-start.3 = (bf16[2,4,2,64,128]{4,3,2,1,0:T(8,128)(2,1)S(1)}, bf16[2,4,2,64,128]{4,3,2,1,0:T(8,128)(2,1)S(1)}, u32[]{:S(2)}, u32[]{:S(2)}) collective-permute-start(bf16[2,4,2,64,128]{4,3,2,1,0:T(8,128)(2,1)S(1)} %collective-permute-done.2), channel_id=1, source_target_pairs={{0,8},{8,16},{16,24},{24,32},{32,40},{40,48},{48,56},{56,64},{64,7... | collective-permute-start | bytes 786440 | tf_op jit(solution)/shard_map/ppermute | solution.py:181
  63.5 2.5 %collective-permute-done.9 = bf16[2,4,2,64,128]{4,3,2,1,0:T(8,128)(2,1)S(1)} collective-permute-done((bf16[2,4,2,64,128]{4,3,2,1,0:T(8,128)(2,1)S(1)}, bf16[2,4,2,64,128]{4,3,2,1,0:T(8,128)(2,1)S(1)}, u32[]{:S(2)}, u32[]{:S(2)}) %collective-permute-start.9) | collective-permute-done | bytes 262176 | tf_op jit(solution)/shard_map/ppermute | solution.py:184
  66.0 4.1 %collective-permute-start.10 = (bf16[2,4,2,64,128]{4,3,2,1,0:T(8,128)(2,1)S(1)}, bf16[2,4,2,64,128]{4,3,2,1,0:T(8,128)(2,1)S(1)}, u32[]{:S(2)}, u32[]{:S(2)}) collective-permute-start(bf16[2,4,2,64,128]{4,3,2,1,0:T(8,128)(2,1)S(1)} %collective-permute-done.9), channel_id=1, source_target_pairs={{0,120},{8,0},{16,8},{24,16},{32,24},{40,32},{48,40},{56,48},{64,5... | collective-permute-start | bytes 786440 | tf_op jit(solution)/shard_map/ppermute | solution.py:184
  71.4 4.5 %collective-permute-done.3 = bf16[2,4,2,64,128]{4,3,2,1,0:T(8,128)(2,1)S(1)} collective-permute-done((bf16[2,4,2,64,128]{4,3,2,1,0:T(8,128)(2,1)S(1)}, bf16[2,4,2,64,128]{4,3,2,1,0:T(8,128)(2,1)S(1)}, u32[]{:S(2)}, u32[]{:S(2)}) %collective-permute-start.3) | collective-permute-done | bytes 262176 | tf_op jit(solution)/shard_map/ppermute | solution.py:181
  75.9 1.9 %collective-permute-start.4 = (bf16[2,4,2,64,128]{4,3,2,1,0:T(8,128)(2,1)S(1)}, bf16[2,4,2,64,128]{4,3,2,1,0:T(8,128)(2,1)S(1)}, u32[]{:S(2)}, u32[]{:S(2)}) collective-permute-start(bf16[2,4,2,64,128]{4,3,2,1,0:T(8,128)(2,1)S(1)} %collective-permute-done.3), channel_id=1, source_target_pairs={{0,8},{8,16},{16,24},{24,32},{32,40},{40,48},{48,56},{56,64},{64,7... | collective-permute-start | bytes 786440 | tf_op jit(solution)/shard_map/ppermute | solution.py:181
  77.8 0.7 bitcast_dynamic-update-slice_fusion.15
  78.6 0.8 collective-permute-done.10
  79.4 5.4 %collective-permute-start.11 = (bf16[2,4,2,64,128]{4,3,2,1,0:T(8,128)(2,1)S(1)}, bf16[2,4,2,64,128]{4,3,2,1,0:T(8,128)(2,1)S(1)}, u32[]{:S(2)}, u32[]{:S(2)}) collective-permute-start(bf16[2,4,2,64,128]{4,3,2,1,0:T(8,128)(2,1)S(1)} %collective-permute-done.10), channel_id=1, source_target_pairs={{0,120},{8,0},{16,8},{24,16},{32,24},{40,32},{48,40},{56,48},{64,5... | collective-permute-start | bytes 786440 | tf_op jit(solution)/shard_map/ppermute | solution.py:184
  84.8 0.8 bitcast_dynamic-update-slice_fusion.14
  85.6 4.9 %collective-permute-done.4 = bf16[2,4,2,64,128]{4,3,2,1,0:T(8,128)(2,1)S(1)} collective-permute-done((bf16[2,4,2,64,128]{4,3,2,1,0:T(8,128)(2,1)S(1)}, bf16[2,4,2,64,128]{4,3,2,1,0:T(8,128)(2,1)S(1)}, u32[]{:S(2)}, u32[]{:S(2)}) %collective-permute-start.4) | collective-permute-done | bytes 262176 | tf_op jit(solution)/shard_map/ppermute | solution.py:181
  90.5 1.9 %collective-permute-start.5 = (bf16[2,4,2,64,128]{4,3,2,1,0:T(8,128)(2,1)S(1)}, bf16[2,4,2,64,128]{4,3,2,1,0:T(8,128)(2,1)S(1)}, u32[]{:S(2)}, u32[]{:S(2)}) collective-permute-start(bf16[2,4,2,64,128]{4,3,2,1,0:T(8,128)(2,1)S(1)} %collective-permute-done.4), channel_id=1, source_target_pairs={{0,8},{8,16},{16,24},{24,32},{32,40},{40,48},{48,56},{56,64},{64,7... | collective-permute-start | bytes 786440 | tf_op jit(solution)/shard_map/ppermute | solution.py:181
  92.4 0.7 bitcast_dynamic-update-slice_fusion.13
  93.1 1.1 collective-permute-done.11
  94.2 5.4 %collective-permute-start.12 = (bf16[2,4,2,64,128]{4,3,2,1,0:T(8,128)(2,1)S(1)}, bf16[2,4,2,64,128]{4,3,2,1,0:T(8,128)(2,1)S(1)}, u32[]{:S(2)}, u32[]{:S(2)}) collective-permute-start(bf16[2,4,2,64,128]{4,3,2,1,0:T(8,128)(2,1)S(1)} %collective-permute-done.11), channel_id=1, source_target_pairs={{0,120},{8,0},{16,8},{24,16},{32,24},{40,32},{48,40},{56,48},{64,5... | collective-permute-start | bytes 786440 | tf_op jit(solution)/shard_map/ppermute | solution.py:184
  99.6 0.7 bitcast_dynamic-update-slice_fusion.12
  100.4 5.1 %collective-permute-done.5 = bf16[2,4,2,64,128]{4,3,2,1,0:T(8,128)(2,1)S(1)} collective-permute-done((bf16[2,4,2,64,128]{4,3,2,1,0:T(8,128)(2,1)S(1)}, bf16[2,4,2,64,128]{4,3,2,1,0:T(8,128)(2,1)S(1)}, u32[]{:S(2)}, u32[]{:S(2)}) %collective-permute-start.5) | collective-permute-done | bytes 262176 | tf_op jit(solution)/shard_map/ppermute | solution.py:181
  105.5 1.9 %collective-permute-start.6 = (bf16[2,4,2,64,128]{4,3,2,1,0:T(8,128)(2,1)S(1)}, bf16[2,4,2,64,128]{4,3,2,1,0:T(8,128)(2,1)S(1)}, u32[]{:S(2)}, u32[]{:S(2)}) collective-permute-start(bf16[2,4,2,64,128]{4,3,2,1,0:T(8,128)(2,1)S(1)} %collective-permute-done.5), channel_id=1, source_target_pairs={{0,8},{8,16},{16,24},{24,32},{32,40},{40,48},{48,56},{56,64},{64,7... | collective-permute-start | bytes 786440 | tf_op jit(solution)/shard_map/ppermute | solution.py:181
  107.4 0.7 bitcast_dynamic-update-slice_fusion.11
  108.2 0.9 collective-permute-done.12
  109.1 5.4 %collective-permute-start.13 = (bf16[2,4,2,64,128]{4,3,2,1,0:T(8,128)(2,1)S(1)}, bf16[2,4,2,64,128]{4,3,2,1,0:T(8,128)(2,1)S(1)}, u32[]{:S(2)}, u32[]{:S(2)}) collective-permute-start(bf16[2,4,2,64,128]{4,3,2,1,0:T(8,128)(2,1)S(1)} %collective-permute-done.12), channel_id=1, source_target_pairs={{0,120},{8,0},{16,8},{24,16},{32,24},{40,32},{48,40},{56,48},{64,5... | collective-permute-start | bytes 786440 | tf_op jit(solution)/shard_map/ppermute | solution.py:184
  114.5 0.7 bitcast_dynamic-update-slice_fusion.10
  115.2 1.2 collective-permute-done.6
  116.4 2.0 %collective-permute-start.7 = (bf16[2,4,2,64,128]{4,3,2,1,0:T(8,128)(2,1)S(1)}, bf16[2,4,2,64,128]{4,3,2,1,0:T(8,128)(2,1)S(1)}, u32[]{:S(2)}, u32[]{:S(2)}) collective-permute-start(bf16[2,4,2,64,128]{4,3,2,1,0:T(8,128)(2,1)S(1)} %collective-permute-done.6), channel_id=1, source_target_pairs={{0,8},{8,16},{16,24},{24,32},{32,40},{40,48},{48,56},{56,64},{64,7... | collective-permute-start | bytes 786440 | tf_op jit(solution)/shard_map/ppermute | solution.py:181
  119.1 4.5 %collective-permute-start.14 = (bf16[2,4,2,64,128]{4,3,2,1,0:T(8,128)(2,1)S(1)}, bf16[2,4,2,64,128]{4,3,2,1,0:T(8,128)(2,1)S(1)}, u32[]{:S(2)}, u32[]{:S(2)}) collective-permute-start(bf16[2,4,2,64,128]{4,3,2,1,0:T(8,128)(2,1)S(1)} %collective-permute-done.13), channel_id=1, source_target_pairs={{0,120},{8,0},{16,8},{24,16},{32,24},{40,32},{48,40},{56,48},{64,5... | collective-permute-start | bytes 786440 | tf_op jit(solution)/shard_map/ppermute | solution.py:184
  124.3 2.9 %collective-permute-done.7 = bf16[2,4,2,64,128]{4,3,2,1,0:T(8,128)(2,1)S(1)} collective-permute-done((bf16[2,4,2,64,128]{4,3,2,1,0:T(8,128)(2,1)S(1)}, bf16[2,4,2,64,128]{4,3,2,1,0:T(8,128)(2,1)S(1)}, u32[]{:S(2)}, u32[]{:S(2)}) %collective-permute-start.7) | collective-permute-done | bytes 262176 | tf_op jit(solution)/shard_map/ppermute | solution.py:181
  127.2 0.7 bitcast_dynamic-update-slice_fusion.7
  127.9 1.7 collective-permute-done.14
  129.7 0.7 bitcast_dynamic-update-slice_fusion.6
  130.4 0.7 bitcast_dynamic-update-slice_fusion.5
  131.1 0.7 bitcast_dynamic-update-slice_fusion.4
  132.6 0.7 bitcast_dynamic-update-slice_fusion.2
  133.3 0.8 bitcast_dynamic-update-slice_fusion.1
  134.1 0.7 bitcast_dynamic-update-slice_fusion
  134.8 11.6 %shard_map.46 = bf16[256,1024]{1,0:T(8,128)(2,1)} custom-call(s32[64]{0:T(128)} %get-tuple-element.15.rows_ref, s32[64]{0:T(128)} %get-tuple-element.14.ring_rows_ref, s32[64]{0:T(128)} %get-tuple-element.5.from_ring_ref, s32[3]{0:T(128)} %pad_add_fusion.prev_ref, bf16[256,1024]{1,0:T(8,128)(2,1)} %q_ref.1, bf16[256,128]{1,0:T(8,128)(2,1)} %keys_ref.1, ...), custom_call_target="tpu_custom_call" | custom-call | flops 1476395008 | bytes 3145728 | tf_op jit(solution)/shard_map/pallas_call | solution.py:96
  146.4 23.0 %all_to_all.25 = bf16[8,32,1024]{2,1,0:T(8,128)(2,1)S(1)} all-to-all(bf16[8,32,1024]{2,1,0:T(8,128)(2,1)} %bitcast.53), channel_id=1, replica_groups=mesh['cy'=4,'cz'=16,'kvh'=8] {'kvh'}, dimensions={0} | all-to-all | bytes 1048576 | tf_op jit(solution)/shard_map/all_to_all | solution.py:188
  169.4 0.8 copy.19
  (23 shorter events, 6.6 us)
Async XLA Ops:
  6.5 128.3 %all-gather.3.cloned.1.call-start = ((), (), s32[]{:S(2)}) async-start(), calls=%async_computation.2 | async-start | bytes 4456448 | tf_op jit(solution)/shard_map/all_gather | solution.py:173
  20.1 17.5 %collective-permute-start = (bf16[2,4,2,64,128]{4,3,2,1,0:T(8,128)(2,1)S(1)}, bf16[2,4,2,64,128]{4,3,2,1,0:T(8,128)(2,1)S(1)}, u32[]{:S(2)}, u32[]{:S(2)}) collective-permute-start(bf16[2,4,2,64,128]{4,3,2,1,0:T(8,128)(2,1)S(1)} %get-tuple-element.8), channel_id=1, source_target_pairs={{0,8},{8,16},{16,24},{24,32},{32,40},{40,48},{48,56},{56,64},{64,7... | collective-permute-start | bytes 786440 | tf_op jit(solution)/shard_map/ppermute | solution.py:181
  37.6 8.3 %collective-permute-start.1 = (bf16[2,4,2,64,128]{4,3,2,1,0:T(8,128)(2,1)S(1)}, bf16[2,4,2,64,128]{4,3,2,1,0:T(8,128)(2,1)S(1)}, u32[]{:S(2)}, u32[]{:S(2)}) collective-permute-start(bf16[2,4,2,64,128]{4,3,2,1,0:T(8,128)(2,1)S(1)} %collective-permute-done), channel_id=1, source_target_pairs={{0,8},{8,16},{16,24},{24,32},{32,40},{40,48},{48,56},{56,64},{64,7... | collective-permute-start | bytes 786440 | tf_op jit(solution)/shard_map/ppermute | solution.py:181
  39.8 14.7 %collective-permute-start.8 = (bf16[2,4,2,64,128]{4,3,2,1,0:T(8,128)(2,1)S(1)}, bf16[2,4,2,64,128]{4,3,2,1,0:T(8,128)(2,1)S(1)}, u32[]{:S(2)}, u32[]{:S(2)}) collective-permute-start(bf16[2,4,2,64,128]{4,3,2,1,0:T(8,128)(2,1)S(1)} %get-tuple-element.8), channel_id=1, source_target_pairs={{0,120},{8,0},{16,8},{24,16},{32,24},{40,32},{48,40},{56,48},{64,5... | collective-permute-start | bytes 786440 | tf_op jit(solution)/shard_map/ppermute | solution.py:184
  45.9 15.0 %collective-permute-start.2 = (bf16[2,4,2,64,128]{4,3,2,1,0:T(8,128)(2,1)S(1)}, bf16[2,4,2,64,128]{4,3,2,1,0:T(8,128)(2,1)S(1)}, u32[]{:S(2)}, u32[]{:S(2)}) collective-permute-start(bf16[2,4,2,64,128]{4,3,2,1,0:T(8,128)(2,1)S(1)} %collective-permute-done.1), channel_id=1, source_target_pairs={{0,8},{8,16},{16,24},{24,32},{32,40},{40,48},{48,56},{56,64},{64,7... | collective-permute-start | bytes 786440 | tf_op jit(solution)/shard_map/ppermute | solution.py:181
  54.4 11.6 %collective-permute-start.9 = (bf16[2,4,2,64,128]{4,3,2,1,0:T(8,128)(2,1)S(1)}, bf16[2,4,2,64,128]{4,3,2,1,0:T(8,128)(2,1)S(1)}, u32[]{:S(2)}, u32[]{:S(2)}) collective-permute-start(bf16[2,4,2,64,128]{4,3,2,1,0:T(8,128)(2,1)S(1)} %collective-permute-done.8), channel_id=1, source_target_pairs={{0,120},{8,0},{16,8},{24,16},{32,24},{40,32},{48,40},{56,48},{64,5... | collective-permute-start | bytes 786440 | tf_op jit(solution)/shard_map/ppermute | solution.py:184
  60.9 15.0 %collective-permute-start.3 = (bf16[2,4,2,64,128]{4,3,2,1,0:T(8,128)(2,1)S(1)}, bf16[2,4,2,64,128]{4,3,2,1,0:T(8,128)(2,1)S(1)}, u32[]{:S(2)}, u32[]{:S(2)}) collective-permute-start(bf16[2,4,2,64,128]{4,3,2,1,0:T(8,128)(2,1)S(1)} %collective-permute-done.2), channel_id=1, source_target_pairs={{0,8},{8,16},{16,24},{24,32},{32,40},{40,48},{48,56},{56,64},{64,7... | collective-permute-start | bytes 786440 | tf_op jit(solution)/shard_map/ppermute | solution.py:181
  66.0 13.4 %collective-permute-start.10 = (bf16[2,4,2,64,128]{4,3,2,1,0:T(8,128)(2,1)S(1)}, bf16[2,4,2,64,128]{4,3,2,1,0:T(8,128)(2,1)S(1)}, u32[]{:S(2)}, u32[]{:S(2)}) collective-permute-start(bf16[2,4,2,64,128]{4,3,2,1,0:T(8,128)(2,1)S(1)} %collective-permute-done.9), channel_id=1, source_target_pairs={{0,120},{8,0},{16,8},{24,16},{32,24},{40,32},{48,40},{56,48},{64,5... | collective-permute-start | bytes 786440 | tf_op jit(solution)/shard_map/ppermute | solution.py:184
  75.9 14.6 %collective-permute-start.4 = (bf16[2,4,2,64,128]{4,3,2,1,0:T(8,128)(2,1)S(1)}, bf16[2,4,2,64,128]{4,3,2,1,0:T(8,128)(2,1)S(1)}, u32[]{:S(2)}, u32[]{:S(2)}) collective-permute-start(bf16[2,4,2,64,128]{4,3,2,1,0:T(8,128)(2,1)S(1)} %collective-permute-done.3), channel_id=1, source_target_pairs={{0,8},{8,16},{16,24},{24,32},{32,40},{40,48},{48,56},{56,64},{64,7... | collective-permute-start | bytes 786440 | tf_op jit(solution)/shard_map/ppermute | solution.py:181
  79.4 14.8 %collective-permute-start.11 = (bf16[2,4,2,64,128]{4,3,2,1,0:T(8,128)(2,1)S(1)}, bf16[2,4,2,64,128]{4,3,2,1,0:T(8,128)(2,1)S(1)}, u32[]{:S(2)}, u32[]{:S(2)}) collective-permute-start(bf16[2,4,2,64,128]{4,3,2,1,0:T(8,128)(2,1)S(1)} %collective-permute-done.10), channel_id=1, source_target_pairs={{0,120},{8,0},{16,8},{24,16},{32,24},{40,32},{48,40},{56,48},{64,5... | collective-permute-start | bytes 786440 | tf_op jit(solution)/shard_map/ppermute | solution.py:184
  90.5 15.0 %collective-permute-start.5 = (bf16[2,4,2,64,128]{4,3,2,1,0:T(8,128)(2,1)S(1)}, bf16[2,4,2,64,128]{4,3,2,1,0:T(8,128)(2,1)S(1)}, u32[]{:S(2)}, u32[]{:S(2)}) collective-permute-start(bf16[2,4,2,64,128]{4,3,2,1,0:T(8,128)(2,1)S(1)} %collective-permute-done.4), channel_id=1, source_target_pairs={{0,8},{8,16},{16,24},{24,32},{32,40},{40,48},{48,56},{56,64},{64,7... | collective-permute-start | bytes 786440 | tf_op jit(solution)/shard_map/ppermute | solution.py:181
  94.2 14.9 %collective-permute-start.12 = (bf16[2,4,2,64,128]{4,3,2,1,0:T(8,128)(2,1)S(1)}, bf16[2,4,2,64,128]{4,3,2,1,0:T(8,128)(2,1)S(1)}, u32[]{:S(2)}, u32[]{:S(2)}) collective-permute-start(bf16[2,4,2,64,128]{4,3,2,1,0:T(8,128)(2,1)S(1)} %collective-permute-done.11), channel_id=1, source_target_pairs={{0,120},{8,0},{16,8},{24,16},{32,24},{40,32},{48,40},{56,48},{64,5... | collective-permute-start | bytes 786440 | tf_op jit(solution)/shard_map/ppermute | solution.py:184
  105.5 10.9 %collective-permute-start.6 = (bf16[2,4,2,64,128]{4,3,2,1,0:T(8,128)(2,1)S(1)}, bf16[2,4,2,64,128]{4,3,2,1,0:T(8,128)(2,1)S(1)}, u32[]{:S(2)}, u32[]{:S(2)}) collective-permute-start(bf16[2,4,2,64,128]{4,3,2,1,0:T(8,128)(2,1)S(1)} %collective-permute-done.5), channel_id=1, source_target_pairs={{0,8},{8,16},{16,24},{24,32},{32,40},{40,48},{48,56},{56,64},{64,7... | collective-permute-start | bytes 786440 | tf_op jit(solution)/shard_map/ppermute | solution.py:181
  109.1 10.0 %collective-permute-start.13 = (bf16[2,4,2,64,128]{4,3,2,1,0:T(8,128)(2,1)S(1)}, bf16[2,4,2,64,128]{4,3,2,1,0:T(8,128)(2,1)S(1)}, u32[]{:S(2)}, u32[]{:S(2)}) collective-permute-start(bf16[2,4,2,64,128]{4,3,2,1,0:T(8,128)(2,1)S(1)} %collective-permute-done.12), channel_id=1, source_target_pairs={{0,120},{8,0},{16,8},{24,16},{32,24},{40,32},{48,40},{56,48},{64,5... | collective-permute-start | bytes 786440 | tf_op jit(solution)/shard_map/ppermute | solution.py:184
  116.4 10.8 %collective-permute-start.7 = (bf16[2,4,2,64,128]{4,3,2,1,0:T(8,128)(2,1)S(1)}, bf16[2,4,2,64,128]{4,3,2,1,0:T(8,128)(2,1)S(1)}, u32[]{:S(2)}, u32[]{:S(2)}) collective-permute-start(bf16[2,4,2,64,128]{4,3,2,1,0:T(8,128)(2,1)S(1)} %collective-permute-done.6), channel_id=1, source_target_pairs={{0,8},{8,16},{16,24},{24,32},{32,40},{40,48},{48,56},{56,64},{64,7... | collective-permute-start | bytes 786440 | tf_op jit(solution)/shard_map/ppermute | solution.py:181
  119.1 10.6 %collective-permute-start.14 = (bf16[2,4,2,64,128]{4,3,2,1,0:T(8,128)(2,1)S(1)}, bf16[2,4,2,64,128]{4,3,2,1,0:T(8,128)(2,1)S(1)}, u32[]{:S(2)}, u32[]{:S(2)}) collective-permute-start(bf16[2,4,2,64,128]{4,3,2,1,0:T(8,128)(2,1)S(1)} %collective-permute-done.13), channel_id=1, source_target_pairs={{0,120},{8,0},{16,8},{24,16},{32,24},{40,32},{48,40},{56,48},{64,5... | collective-permute-start | bytes 786440 | tf_op jit(solution)/shard_map/ppermute | solution.py:184
Sparse Core Ops, SparseCore 0:
  20.2 92.2 all-gather.2

commit v9 on v7

--- a/solution.py
+++ b/solution.py
@@ -129,12 +129,14 @@
     per_dev = tok_rows // TILE
     scale = 1.0 / head_size**0.5
     my_z = here % n_z
+    my_y = here // n_z
 
     def locate(tile_id):
         owner = tile_id // per_dev
         y, z = owner // n_z, owner % n_z
-        in_ring = y == n_y - 1
-        row = ((z * (n_y - 1) + jnp.minimum(y, n_y - 2)) * per_dev + tile_id % per_dev).astype(jnp.int32)
+        in_ring = y == my_y
+        slot = jnp.clip(y - (y > my_y).astype(y.dtype), 0, n_y - 2)
+        row = ((z * (n_y - 1) + slot) * per_dev + tile_id % per_dev).astype(jnp.int32)
         ring_row = (((my_z - z) % n_z) * per_dev + tile_id % per_dev).astype(jnp.int32)
         return row, ring_row, in_ring.astype(jnp.int32)
 
@@ -167,8 +169,11 @@
     )
     copies = jnp.broadcast_to(both[None], (n_y,) + both.shape)
     gathered = lax.all_to_all(copies, "cy", 0, 0, tiled=False)
-    col_last = gathered[n_y - 1]
-    gathered = lax.all_gather(gathered[: n_y - 1], "cz", axis=0, tiled=False)
+    col_last = both
+    my_y = lax.axis_index("cy")
+    others = jnp.arange(n_y - 1, dtype=jnp.int32)
+    others = others + (others >= my_y).astype(jnp.int32)
+    gathered = lax.all_gather(jnp.take(gathered, others, axis=0), "cz", axis=0, tiled=False)
     tiles = gathered.reshape(n_z * (n_y - 1) * per_dev, 2, TILE, head_size)
     ahead = [(i, (i + 1) % n_z) for i in range(n_z)]
     behind = [(i, (i - 1) % n_z) for i in range(n_z)]

time: 163 us -> 164 us (level)
  blocking collectives: 26.6 us -> 14.8 us
  starting transfers between devices: 53.8 us -> 61.3 us
  waiting for transfers between devices: 50.5 us -> 54.9 us
    all_to_all x1 -> x0, blocking collectives: 11.7 us -> none  [per_device(): gathered = lax.all_to_all(copies, 'cy', 0, 0, tiled=False)]
    all_to_all x0 -> x1, waiting for transfers between devices: none -> 6.89 us  [per_device(): gathered = lax.all_to_all(copies, 'cy', 0, 0, tiled=False)]
    all_to_all x0 -> x1, starting transfers between devices: none -> 5.01 us  [per_device(): gathered = lax.all_to_all(copies, 'cy', 0, 0, tiled=False)]
    ppermute x7, starting transfers between devices: 35.3 us -> 38 us  [per_device(): bwd = lax.ppermute(bwd, 'cz', behind)]
    ppermute x8, waiting for transfers between devices: 27.5 us -> 25.3 us  [per_device(): fwd = lax.ppermute(fwd, 'cz', ahead)]
  transfers between devices with their start and end apart: 16 -> 17, of which waited for: 10 -> 11; matrix products, arithmetic and copies ran while one was open for 2% -> 2% of each run, Pallas kernels for 0% -> 0%
where the time goes in v9:
time: 164 us
  starting transfers between devices  61.3 us (37%)
  waiting for transfers between devices  54.9 us (33%)
  blocking collectives  14.8 us (9%)
  between operations  13.9 us (8%)
  Pallas kernels  11.3 us (7%)
  local copies, waits for them, and re-layouts  3.72 us (2%)
  other arithmetic  3.72 us (2%)
    ppermute x7, starting transfers between devices, per_device(): bwd = lax.ppermute(bwd, 'cz', behind)  38 us
    ppermute x8, waiting for transfers between devices, per_device(): fwd = lax.ppermute(fwd, 'cz', ahead)  25.3 us
    all_gather x1, waiting for transfers between devices, per_device(): lax.all_gather(jnp.take(gathered, others, axis=0), 'cz', axis=0, tiled=Fa...  19.3 us
    ppermute x8, starting transfers between devices, per_device(): fwd = lax.ppermute(fwd, 'cz', ahead)  18.3 us
    all_to_all x1, blocking collectives, per_device(): lax.all_to_all(attended, 'kvh', split_axis=0, concat_axis=1, tiled=True)  14.8 us
    pallas_call x1, Pallas kernels, block_attention(): pl.pallas_call(functools.partial(attention_kernel, per_dev=per_dev, scale...  11.3 us
    all_to_all x1, waiting for transfers between devices, per_device(): gathered = lax.all_to_all(copies, 'cy', 0, 0, tiled=False)  6.89 us
    all_to_all x1, starting transfers between devices, per_device(): gathered = lax.all_to_all(copies, 'cy', 0, 0, tiled=False)  5.01 us
  transfers between devices with their start and end apart: 17, of which 11 were waited for; matrix products, arithmetic and copies ran while one was open for 2% of the time, Pallas kernels for 0%

profile of v9, /device:TPU:1, one launch (start us, length us, event | category | flops | bytes accessed | tf_op | source)
XLA Modules:
  0.0 163.5 jit_solution(8015921083337448796)
XLA Ops:
  6.5 0.9 pad_maximum_fusion
  7.5 0.9 broadcast_in_dim.26
  8.4 5.0 %all-to-all-start = ((bf16[4,4,2,64,128]{4,3,2,1,0:T(8,128)(2,1)}), bf16[4,4,2,64,128]{4,3,2,1,0:T(8,128)(2,1)S(1)}, u32[]{:S(2)}, u32[]{:S(2)}) async-start(bf16[4,4,2,64,128]{4,3,2,1,0:T(8,128)(2,1)} %broadcast_in_dim.26), calls=%async_computation | async-start | bytes 1048576 | tf_op jit(solution)/shard_map/all_to_all | solution.py:171
  13.4 6.9 %all-to-all-done = bf16[4,4,2,64,128]{4,3,2,1,0:T(8,128)(2,1)S(1)} async-done(((bf16[4,4,2,64,128]{4,3,2,1,0:T(8,128)(2,1)}), bf16[4,4,2,64,128]{4,3,2,1,0:T(8,128)(2,1)S(1)}, u32[]{:S(2)}, u32[]{:S(2)}) %all-to-all-start) | async-done | bytes 524320 | tf_op jit(solution)/shard_map/all_to_all | solution.py:171
  20.3 0.6 gather_fusion
  21.0 0.8 bitcast_select_fusion
  21.8 0.0 all-gather.2.cloned.1.call-update
  21.8 4.9 %collective-permute-start = (bf16[4,2,64,128]{3,2,1,0:T(8,128)(2,1)S(1)}, bf16[4,2,64,128]{3,2,1,0:T(8,128)(2,1)S(1)}, u32[]{:S(2)}, u32[]{:S(2)}) collective-permute-start(bf16[4,2,64,128]{3,2,1,0:T(8,128)(2,1)S(1)} %pad_maximum_fusion), channel_id=1, source_target_pairs={{0,8},{8,16},{16,24},{24,32},{32,40},{40,48},{48,56},{56,64},{64,7... | collective-permute-start | bytes 393224 | tf_op jit(solution)/shard_map/ppermute | solution.py:184
  26.7 9.5 %collective-permute-start.8 = (bf16[4,2,64,128]{3,2,1,0:T(8,128)(2,1)S(1)}, bf16[4,2,64,128]{3,2,1,0:T(8,128)(2,1)S(1)}, u32[]{:S(2)}, u32[]{:S(2)}) collective-permute-start(bf16[4,2,64,128]{3,2,1,0:T(8,128)(2,1)S(1)} %pad_maximum_fusion), channel_id=1, source_target_pairs={{0,120},{8,0},{16,8},{24,16},{32,24},{40,32},{48,40},{56,48},{64,5... | collective-permute-start | bytes 393224 | tf_op jit(solution)/shard_map/ppermute | solution.py:187
  36.4 0.1 rem.117
  36.4 0.1 div.46
  36.5 0.1 ne.100
  36.6 0.1 broadcast_in_dim.24
  36.7 0.1 concatenate.15
  36.8 0.6 compare_convert_fusion.2
  37.4 0.6 fusion.6
  38.0 0.1 fusion.1
  38.1 0.6 pad_add_fusion.prev_ref
  38.7 0.6 copy.19.colmask_ref
  39.4 1.9 %collective-permute-start.1 = (bf16[4,2,64,128]{3,2,1,0:T(8,128)(2,1)S(1)}, bf16[4,2,64,128]{3,2,1,0:T(8,128)(2,1)S(1)}, u32[]{:S(2)}, u32[]{:S(2)}) collective-permute-start(bf16[4,2,64,128]{3,2,1,0:T(8,128)(2,1)S(1)} %collective-permute-done), channel_id=1, source_target_pairs={{0,8},{8,16},{16,24},{24,32},{32,40},{40,48},{48,56},{56,64},{64,7... | collective-permute-start | bytes 393224 | tf_op jit(solution)/shard_map/ppermute | solution.py:184
  41.3 0.0 collective-permute-done.8
  41.3 4.6 %collective-permute-start.9 = (bf16[4,2,64,128]{3,2,1,0:T(8,128)(2,1)S(1)}, bf16[4,2,64,128]{3,2,1,0:T(8,128)(2,1)S(1)}, u32[]{:S(2)}, u32[]{:S(2)}) collective-permute-start(bf16[4,2,64,128]{3,2,1,0:T(8,128)(2,1)S(1)} %collective-permute-done.8), channel_id=1, source_target_pairs={{0,120},{8,0},{16,8},{24,16},{32,24},{40,32},{48,40},{56,48},{64,5... | collective-permute-start | bytes 393224 | tf_op jit(solution)/shard_map/ppermute | solution.py:187
  45.9 0.4 collective-permute-done.1
  46.3 1.9 %collective-permute-start.2 = (bf16[4,2,64,128]{3,2,1,0:T(8,128)(2,1)S(1)}, bf16[4,2,64,128]{3,2,1,0:T(8,128)(2,1)S(1)}, u32[]{:S(2)}, u32[]{:S(2)}) collective-permute-start(bf16[4,2,64,128]{3,2,1,0:T(8,128)(2,1)S(1)} %collective-permute-done.1), channel_id=1, source_target_pairs={{0,8},{8,16},{16,24},{24,32},{32,40},{40,48},{48,56},{56,64},{64,7... | collective-permute-start | bytes 393224 | tf_op jit(solution)/shard_map/ppermute | solution.py:184
  48.2 2.3 %collective-permute-done.9 = bf16[4,2,64,128]{3,2,1,0:T(8,128)(2,1)S(1)} collective-permute-done((bf16[4,2,64,128]{3,2,1,0:T(8,128)(2,1)S(1)}, bf16[4,2,64,128]{3,2,1,0:T(8,128)(2,1)S(1)}, u32[]{:S(2)}, u32[]{:S(2)}) %collective-permute-start.9) | collective-permute-done | bytes 131104 | tf_op jit(solution)/shard_map/ppermute | solution.py:187
  50.5 4.0 %collective-permute-start.10 = (bf16[4,2,64,128]{3,2,1,0:T(8,128)(2,1)S(1)}, bf16[4,2,64,128]{3,2,1,0:T(8,128)(2,1)S(1)}, u32[]{:S(2)}, u32[]{:S(2)}) collective-permute-start(bf16[4,2,64,128]{3,2,1,0:T(8,128)(2,1)S(1)} %collective-permute-done.9), channel_id=1, source_target_pairs={{0,120},{8,0},{16,8},{24,16},{32,24},{40,32},{48,40},{56,48},{64,5... | collective-permute-start | bytes 393224 | tf_op jit(solution)/shard_map/ppermute | solution.py:187
  54.5 1.8 %collective-permute-done.2 = bf16[4,2,64,128]{3,2,1,0:T(8,128)(2,1)S(1)} collective-permute-done((bf16[4,2,64,128]{3,2,1,0:T(8,128)(2,1)S(1)}, bf16[4,2,64,128]{3,2,1,0:T(8,128)(2,1)S(1)}, u32[]{:S(2)}, u32[]{:S(2)}) %collective-permute-start.2) | collective-permute-done | bytes 131104 | tf_op jit(solution)/shard_map/ppermute | solution.py:184
  56.4 1.9 %collective-permute-start.3 = (bf16[4,2,64,128]{3,2,1,0:T(8,128)(2,1)S(1)}, bf16[4,2,64,128]{3,2,1,0:T(8,128)(2,1)S(1)}, u32[]{:S(2)}, u32[]{:S(2)}) collective-permute-start(bf16[4,2,64,128]{3,2,1,0:T(8,128)(2,1)S(1)} %collective-permute-done.2), channel_id=1, source_target_pairs={{0,8},{8,16},{16,24},{24,32},{32,40},{40,48},{48,56},{56,64},{64,7... | collective-permute-start | bytes 393224 | tf_op jit(solution)/shard_map/ppermute | solution.py:184
  58.3 1.1 collective-permute-done.10
  59.4 4.5 %collective-permute-start.11 = (bf16[4,2,64,128]{3,2,1,0:T(8,128)(2,1)S(1)}, bf16[4,2,64,128]{3,2,1,0:T(8,128)(2,1)S(1)}, u32[]{:S(2)}, u32[]{:S(2)}) collective-permute-start(bf16[4,2,64,128]{3,2,1,0:T(8,128)(2,1)S(1)} %collective-permute-done.10), channel_id=1, source_target_pairs={{0,120},{8,0},{16,8},{24,16},{32,24},{40,32},{48,40},{56,48},{64,5... | collective-permute-start | bytes 393224 | tf_op jit(solution)/shard_map/ppermute | solution.py:187
  63.9 2.8 %collective-permute-done.3 = bf16[4,2,64,128]{3,2,1,0:T(8,128)(2,1)S(1)} collective-permute-done((bf16[4,2,64,128]{3,2,1,0:T(8,128)(2,1)S(1)}, bf16[4,2,64,128]{3,2,1,0:T(8,128)(2,1)S(1)}, u32[]{:S(2)}, u32[]{:S(2)}) %collective-permute-start.3) | collective-permute-done | bytes 131104 | tf_op jit(solution)/shard_map/ppermute | solution.py:184
  66.6 1.9 %collective-permute-start.4 = (bf16[4,2,64,128]{3,2,1,0:T(8,128)(2,1)S(1)}, bf16[4,2,64,128]{3,2,1,0:T(8,128)(2,1)S(1)}, u32[]{:S(2)}, u32[]{:S(2)}) collective-permute-start(bf16[4,2,64,128]{3,2,1,0:T(8,128)(2,1)S(1)} %collective-permute-done.3), channel_id=1, source_target_pairs={{0,8},{8,16},{16,24},{24,32},{32,40},{40,48},{48,56},{56,64},{64,7... | collective-permute-start | bytes 393224 | tf_op jit(solution)/shard_map/ppermute | solution.py:184
  68.6 0.0 collective-permute-done.11
  68.6 5.4 %collective-permute-start.12 = (bf16[4,2,64,128]{3,2,1,0:T(8,128)(2,1)S(1)}, bf16[4,2,64,128]{3,2,1,0:T(8,128)(2,1)S(1)}, u32[]{:S(2)}, u32[]{:S(2)}) collective-permute-start(bf16[4,2,64,128]{3,2,1,0:T(8,128)(2,1)S(1)} %collective-permute-done.11), channel_id=1, source_target_pairs={{0,120},{8,0},{16,8},{24,16},{32,24},{40,32},{48,40},{56,48},{64,5... | collective-permute-start | bytes 393224 | tf_op jit(solution)/shard_map/ppermute | solution.py:187
  74.0 3.1 %collective-permute-done.4 = bf16[4,2,64,128]{3,2,1,0:T(8,128)(2,1)S(1)} collective-permute-done((bf16[4,2,64,128]{3,2,1,0:T(8,128)(2,1)S(1)}, bf16[4,2,64,128]{3,2,1,0:T(8,128)(2,1)S(1)}, u32[]{:S(2)}, u32[]{:S(2)}) %collective-permute-start.4) | collective-permute-done | bytes 131104 | tf_op jit(solution)/shard_map/ppermute | solution.py:184
  77.2 1.9 %collective-permute-start.5 = (bf16[4,2,64,128]{3,2,1,0:T(8,128)(2,1)S(1)}, bf16[4,2,64,128]{3,2,1,0:T(8,128)(2,1)S(1)}, u32[]{:S(2)}, u32[]{:S(2)}) collective-permute-start(bf16[4,2,64,128]{3,2,1,0:T(8,128)(2,1)S(1)} %collective-permute-done.4), channel_id=1, source_target_pairs={{0,8},{8,16},{16,24},{24,32},{32,40},{40,48},{48,56},{56,64},{64,7... | collective-permute-start | bytes 393224 | tf_op jit(solution)/shard_map/ppermute | solution.py:184
  79.1 5.1 %collective-permute-start.13 = (bf16[4,2,64,128]{3,2,1,0:T(8,128)(2,1)S(1)}, bf16[4,2,64,128]{3,2,1,0:T(8,128)(2,1)S(1)}, u32[]{:S(2)}, u32[]{:S(2)}) collective-permute-start(bf16[4,2,64,128]{3,2,1,0:T(8,128)(2,1)S(1)} %collective-permute-done.12), channel_id=1, source_target_pairs={{0,120},{8,0},{16,8},{24,16},{32,24},{40,32},{48,40},{56,48},{64,5... | collective-permute-start | bytes 393224 | tf_op jit(solution)/shard_map/ppermute | solution.py:187
  84.2 3.7 %collective-permute-done.5 = bf16[4,2,64,128]{3,2,1,0:T(8,128)(2,1)S(1)} collective-permute-done((bf16[4,2,64,128]{3,2,1,0:T(8,128)(2,1)S(1)}, bf16[4,2,64,128]{3,2,1,0:T(8,128)(2,1)S(1)}, u32[]{:S(2)}, u32[]{:S(2)}) %collective-permute-start.5) | collective-permute-done | bytes 131104 | tf_op jit(solution)/shard_map/ppermute | solution.py:184
  87.9 1.9 %collective-permute-start.6 = (bf16[4,2,64,128]{3,2,1,0:T(8,128)(2,1)S(1)}, bf16[4,2,64,128]{3,2,1,0:T(8,128)(2,1)S(1)}, u32[]{:S(2)}, u32[]{:S(2)}) collective-permute-start(bf16[4,2,64,128]{3,2,1,0:T(8,128)(2,1)S(1)} %collective-permute-done.5), channel_id=1, source_target_pairs={{0,8},{8,16},{16,24},{24,32},{32,40},{40,48},{48,56},{56,64},{64,7... | collective-permute-start | bytes 393224 | tf_op jit(solution)/shard_map/ppermute | solution.py:184
  89.9 4.9 %collective-permute-start.14 = (bf16[4,2,64,128]{3,2,1,0:T(8,128)(2,1)S(1)}, bf16[4,2,64,128]{3,2,1,0:T(8,128)(2,1)S(1)}, u32[]{:S(2)}, u32[]{:S(2)}) collective-permute-start(bf16[4,2,64,128]{3,2,1,0:T(8,128)(2,1)S(1)} %collective-permute-done.13), channel_id=1, source_target_pairs={{0,120},{8,0},{16,8},{24,16},{32,24},{40,32},{48,40},{56,48},{64,5... | collective-permute-start | bytes 393224 | tf_op jit(solution)/shard_map/ppermute | solution.py:187
  94.8 4.2 %collective-permute-done.6 = bf16[4,2,64,128]{3,2,1,0:T(8,128)(2,1)S(1)} collective-permute-done((bf16[4,2,64,128]{3,2,1,0:T(8,128)(2,1)S(1)}, bf16[4,2,64,128]{3,2,1,0:T(8,128)(2,1)S(1)}, u32[]{:S(2)}, u32[]{:S(2)}) %collective-permute-start.6) | collective-permute-done | bytes 131104 | tf_op jit(solution)/shard_map/ppermute | solution.py:184
  99.0 1.9 %collective-permute-start.7 = (bf16[4,2,64,128]{3,2,1,0:T(8,128)(2,1)S(1)}, bf16[4,2,64,128]{3,2,1,0:T(8,128)(2,1)S(1)}, u32[]{:S(2)}, u32[]{:S(2)}) collective-permute-start(bf16[4,2,64,128]{3,2,1,0:T(8,128)(2,1)S(1)} %collective-permute-done.6), channel_id=1, source_target_pairs={{0,8},{8,16},{16,24},{24,32},{32,40},{40,48},{48,56},{56,64},{64,7... | collective-permute-start | bytes 393224 | tf_op jit(solution)/shard_map/ppermute | solution.py:184
  100.9 9.3 %collective-permute-done.7 = bf16[4,2,64,128]{3,2,1,0:T(8,128)(2,1)S(1)} collective-permute-done((bf16[4,2,64,128]{3,2,1,0:T(8,128)(2,1)S(1)}, bf16[4,2,64,128]{3,2,1,0:T(8,128)(2,1)S(1)}, u32[]{:S(2)}, u32[]{:S(2)}) %collective-permute-start.7) | collective-permute-done | bytes 131104 | tf_op jit(solution)/shard_map/ppermute | solution.py:184
  110.3 0.0 collective-permute-done.14
  110.5 19.3 %all-gather.2.cloned.1.call-done = bf16[16,3,4,2,64,128]{5,4,3,2,1,0:T(8,128)(2,1)} async-done(((bf16[1,3,4,2,64,128]{5,4,3,2,1,0:T(8,128)(2,1)}), bf16[16,3,4,2,64,128]{5,4,3,2,1,0:T(8,128)(2,1)}) %all-gather.2.cloned.1.call-update) | async-done | bytes 6291472 | tf_op jit(solution)/shard_map/all_gather | solution.py:176
  129.8 11.3 %shard_map.46 = bf16[256,1024]{1,0:T(8,128)(2,1)} custom-call(s32[64]{0:T(128)} %get-tuple-element.13.rows_ref, s32[64]{0:T(128)} %get-tuple-element.12.ring_rows_ref, s32[64]{0:T(128)} %get-tuple-element.5.from_ring_ref, s32[3]{0:T(128)} %pad_add_fusion.prev_ref, bf16[256,1024]{1,0:T(8,128)(2,1)} %q_ref.1, bf16[256,128]{1,0:T(8,128)(2,1)} %keys_ref.1, ...), custom_call_target="tpu_custom_call" | custom-call | flops 1476395008 | bytes 3145728 | tf_op jit(solution)/shard_map/pallas_call | solution.py:95
  141.1 14.8 %all_to_all.24 = bf16[8,32,1024]{2,1,0:T(8,128)(2,1)S(1)} all-to-all(bf16[8,32,1024]{2,1,0:T(8,128)(2,1)} %bitcast.58), channel_id=1, replica_groups=mesh['cy'=4,'cz'=16,'kvh'=8] {'kvh'}, dimensions={0} | all-to-all | bytes 1048576 | tf_op jit(solution)/shard_map/all_to_all | solution.py:191
  155.8 0.8 copy.21
  (36 shorter events, 0.4 us)
Async XLA Ops:
  6.5 29.8 %copy-start.3 = (s32[1,4,16]{2,1,0:T(4,128)S(1)}, s32[1,4,16]{2,1,0:T(4,128)}, u32[]{:S(2)}) copy-start(s32[1,4,16]{2,1,0:T(4,128)} %param.7) | copy-start | bytes 772
  6.5 32.8 %copy-start.1 = (bf16[256,128]{1,0:T(8,128)(2,1)S(1)}, bf16[256,128]{1,0:T(8,128)(2,1)}, u32[]{:S(2)}) copy-start(bf16[256,128]{1,0:T(8,128)(2,1)} %keys_ref.1) | copy-start | bytes 196612
  6.5 32.8 %copy-start.2 = (bf16[256,128]{1,0:T(8,128)(2,1)S(1)}, bf16[256,128]{1,0:T(8,128)(2,1)}, u32[]{:S(2)}) copy-start(bf16[256,128]{1,0:T(8,128)(2,1)} %values_ref.1) | copy-start | bytes 196612
  8.4 11.9 %all-to-all-start = ((bf16[4,4,2,64,128]{4,3,2,1,0:T(8,128)(2,1)}), bf16[4,4,2,64,128]{4,3,2,1,0:T(8,128)(2,1)S(1)}, u32[]{:S(2)}, u32[]{:S(2)}) async-start(bf16[4,4,2,64,128]{4,3,2,1,0:T(8,128)(2,1)} %broadcast_in_dim.26), calls=%async_computation | async-start | bytes 1048576 | tf_op jit(solution)/shard_map/all_to_all | solution.py:171
  13.4 116.4 %all-gather.2.cloned.1.call-start = ((), (), s32[]{:S(2)}) async-start(), calls=%async_computation.2 | async-start | bytes 6684672 | tf_op jit(solution)/shard_map/all_gather | solution.py:176
  21.8 17.5 %collective-permute-start = (bf16[4,2,64,128]{3,2,1,0:T(8,128)(2,1)S(1)}, bf16[4,2,64,128]{3,2,1,0:T(8,128)(2,1)S(1)}, u32[]{:S(2)}, u32[]{:S(2)}) collective-permute-start(bf16[4,2,64,128]{3,2,1,0:T(8,128)(2,1)S(1)} %pad_maximum_fusion), channel_id=1, source_target_pairs={{0,8},{8,16},{16,24},{24,32},{32,40},{40,48},{48,56},{56,64},{64,7... | collective-permute-start | bytes 393224 | tf_op jit(solution)/shard_map/ppermute | solution.py:184
  26.7 14.6 %collective-permute-start.8 = (bf16[4,2,64,128]{3,2,1,0:T(8,128)(2,1)S(1)}, bf16[4,2,64,128]{3,2,1,0:T(8,128)(2,1)S(1)}, u32[]{:S(2)}, u32[]{:S(2)}) collective-permute-start(bf16[4,2,64,128]{3,2,1,0:T(8,128)(2,1)S(1)} %pad_maximum_fusion), channel_id=1, source_target_pairs={{0,120},{8,0},{16,8},{24,16},{32,24},{40,32},{48,40},{56,48},{64,5... | collective-permute-start | bytes 393224 | tf_op jit(solution)/shard_map/ppermute | solution.py:187
  39.4 6.9 %collective-permute-start.1 = (bf16[4,2,64,128]{3,2,1,0:T(8,128)(2,1)S(1)}, bf16[4,2,64,128]{3,2,1,0:T(8,128)(2,1)S(1)}, u32[]{:S(2)}, u32[]{:S(2)}) collective-permute-start(bf16[4,2,64,128]{3,2,1,0:T(8,128)(2,1)S(1)} %collective-permute-done), channel_id=1, source_target_pairs={{0,8},{8,16},{16,24},{24,32},{32,40},{40,48},{48,56},{56,64},{64,7... | collective-permute-start | bytes 393224 | tf_op jit(solution)/shard_map/ppermute | solution.py:184
  41.3 9.2 %collective-permute-start.9 = (bf16[4,2,64,128]{3,2,1,0:T(8,128)(2,1)S(1)}, bf16[4,2,64,128]{3,2,1,0:T(8,128)(2,1)S(1)}, u32[]{:S(2)}, u32[]{:S(2)}) collective-permute-start(bf16[4,2,64,128]{3,2,1,0:T(8,128)(2,1)S(1)} %collective-permute-done.8), channel_id=1, source_target_pairs={{0,120},{8,0},{16,8},{24,16},{32,24},{40,32},{48,40},{56,48},{64,5... | collective-permute-start | bytes 393224 | tf_op jit(solution)/shard_map/ppermute | solution.py:187
  46.3 10.1 %collective-permute-start.2 = (bf16[4,2,64,128]{3,2,1,0:T(8,128)(2,1)S(1)}, bf16[4,2,64,128]{3,2,1,0:T(8,128)(2,1)S(1)}, u32[]{:S(2)}, u32[]{:S(2)}) collective-permute-start(bf16[4,2,64,128]{3,2,1,0:T(8,128)(2,1)S(1)} %collective-permute-done.1), channel_id=1, source_target_pairs={{0,8},{8,16},{16,24},{24,32},{32,40},{40,48},{48,56},{56,64},{64,7... | collective-permute-start | bytes 393224 | tf_op jit(solution)/shard_map/ppermute | solution.py:184
  50.5 8.9 %collective-permute-start.10 = (bf16[4,2,64,128]{3,2,1,0:T(8,128)(2,1)S(1)}, bf16[4,2,64,128]{3,2,1,0:T(8,128)(2,1)S(1)}, u32[]{:S(2)}, u32[]{:S(2)}) collective-permute-start(bf16[4,2,64,128]{3,2,1,0:T(8,128)(2,1)S(1)} %collective-permute-done.9), channel_id=1, source_target_pairs={{0,120},{8,0},{16,8},{24,16},{32,24},{40,32},{48,40},{56,48},{64,5... | collective-permute-start | bytes 393224 | tf_op jit(solution)/shard_map/ppermute | solution.py:187
  56.4 10.3 %collective-permute-start.3 = (bf16[4,2,64,128]{3,2,1,0:T(8,128)(2,1)S(1)}, bf16[4,2,64,128]{3,2,1,0:T(8,128)(2,1)S(1)}, u32[]{:S(2)}, u32[]{:S(2)}) collective-permute-start(bf16[4,2,64,128]{3,2,1,0:T(8,128)(2,1)S(1)} %collective-permute-done.2), channel_id=1, source_target_pairs={{0,8},{8,16},{16,24},{24,32},{32,40},{40,48},{48,56},{56,64},{64,7... | collective-permute-start | bytes 393224 | tf_op jit(solution)/shard_map/ppermute | solution.py:184
  59.4 9.2 %collective-permute-start.11 = (bf16[4,2,64,128]{3,2,1,0:T(8,128)(2,1)S(1)}, bf16[4,2,64,128]{3,2,1,0:T(8,128)(2,1)S(1)}, u32[]{:S(2)}, u32[]{:S(2)}) collective-permute-start(bf16[4,2,64,128]{3,2,1,0:T(8,128)(2,1)S(1)} %collective-permute-done.10), channel_id=1, source_target_pairs={{0,120},{8,0},{16,8},{24,16},{32,24},{40,32},{48,40},{56,48},{64,5... | collective-permute-start | bytes 393224 | tf_op jit(solution)/shard_map/ppermute | solution.py:187
  66.6 10.5 %collective-permute-start.4 = (bf16[4,2,64,128]{3,2,1,0:T(8,128)(2,1)S(1)}, bf16[4,2,64,128]{3,2,1,0:T(8,128)(2,1)S(1)}, u32[]{:S(2)}, u32[]{:S(2)}) collective-permute-start(bf16[4,2,64,128]{3,2,1,0:T(8,128)(2,1)S(1)} %collective-permute-done.3), channel_id=1, source_target_pairs={{0,8},{8,16},{16,24},{24,32},{32,40},{40,48},{48,56},{56,64},{64,7... | collective-permute-start | bytes 393224 | tf_op jit(solution)/shard_map/ppermute | solution.py:184
  68.6 10.5 %collective-permute-start.12 = (bf16[4,2,64,128]{3,2,1,0:T(8,128)(2,1)S(1)}, bf16[4,2,64,128]{3,2,1,0:T(8,128)(2,1)S(1)}, u32[]{:S(2)}, u32[]{:S(2)}) collective-permute-start(bf16[4,2,64,128]{3,2,1,0:T(8,128)(2,1)S(1)} %collective-permute-done.11), channel_id=1, source_target_pairs={{0,120},{8,0},{16,8},{24,16},{32,24},{40,32},{48,40},{56,48},{64,5... | collective-permute-start | bytes 393224 | tf_op jit(solution)/shard_map/ppermute | solution.py:187
  77.2 10.8 %collective-permute-start.5 = (bf16[4,2,64,128]{3,2,1,0:T(8,128)(2,1)S(1)}, bf16[4,2,64,128]{3,2,1,0:T(8,128)(2,1)S(1)}, u32[]{:S(2)}, u32[]{:S(2)}) collective-permute-start(bf16[4,2,64,128]{3,2,1,0:T(8,128)(2,1)S(1)} %collective-permute-done.4), channel_id=1, source_target_pairs={{0,8},{8,16},{16,24},{24,32},{32,40},{40,48},{48,56},{56,64},{64,7... | collective-permute-start | bytes 393224 | tf_op jit(solution)/shard_map/ppermute | solution.py:184
  79.1 10.8 %collective-permute-start.13 = (bf16[4,2,64,128]{3,2,1,0:T(8,128)(2,1)S(1)}, bf16[4,2,64,128]{3,2,1,0:T(8,128)(2,1)S(1)}, u32[]{:S(2)}, u32[]{:S(2)}) collective-permute-start(bf16[4,2,64,128]{3,2,1,0:T(8,128)(2,1)S(1)} %collective-permute-done.12), channel_id=1, source_target_pairs={{0,120},{8,0},{16,8},{24,16},{32,24},{40,32},{48,40},{56,48},{64,5... | collective-permute-start | bytes 393224 | tf_op jit(solution)/shard_map/ppermute | solution.py:187
  87.9 11.0 %collective-permute-start.6 = (bf16[4,2,64,128]{3,2,1,0:T(8,128)(2,1)S(1)}, bf16[4,2,64,128]{3,2,1,0:T(8,128)(2,1)S(1)}, u32[]{:S(2)}, u32[]{:S(2)}) collective-permute-start(bf16[4,2,64,128]{3,2,1,0:T(8,128)(2,1)S(1)} %collective-permute-done.5), channel_id=1, source_target_pairs={{0,8},{8,16},{16,24},{24,32},{32,40},{40,48},{48,56},{56,64},{64,7... | collective-permute-start | bytes 393224 | tf_op jit(solution)/shard_map/ppermute | solution.py:184
  89.9 20.4 %collective-permute-start.14 = (bf16[4,2,64,128]{3,2,1,0:T(8,128)(2,1)S(1)}, bf16[4,2,64,128]{3,2,1,0:T(8,128)(2,1)S(1)}, u32[]{:S(2)}, u32[]{:S(2)}) collective-permute-start(bf16[4,2,64,128]{3,2,1,0:T(8,128)(2,1)S(1)} %collective-permute-done.13), channel_id=1, source_target_pairs={{0,120},{8,0},{16,8},{24,16},{32,24},{40,32},{48,40},{56,48},{64,5... | collective-permute-start | bytes 393224 | tf_op jit(solution)/shard_map/ppermute | solution.py:187
  99.0 11.3 %collective-permute-start.7 = (bf16[4,2,64,128]{3,2,1,0:T(8,128)(2,1)S(1)}, bf16[4,2,64,128]{3,2,1,0:T(8,128)(2,1)S(1)}, u32[]{:S(2)}, u32[]{:S(2)}) collective-permute-start(bf16[4,2,64,128]{3,2,1,0:T(8,128)(2,1)S(1)} %collective-permute-done.6), channel_id=1, source_target_pairs={{0,8},{8,16},{16,24},{24,32},{32,40},{40,48},{48,56},{56,64},{64,7... | collective-permute-start | bytes 393224 | tf_op jit(solution)/shard_map/ppermute | solution.py:184
  110.5 19.3 %copy-start = (bf16[16,4,2,64,128]{4,3,2,1,0:T(8,128)(2,1)}, bf16[16,4,2,64,128]{4,3,2,1,0:T(8,128)(2,1)S(1)}, u32[]{:S(2)}) copy-start(bf16[16,4,2,64,128]{4,3,2,1,0:T(8,128)(2,1)S(1)} %bitcast_dynamic-update-slice_fusion) | copy-start | bytes 6291460
Sparse Core Ops, SparseCore 0:
  22.0 107.7 all-gather.1
